TPU v7x, 128 devices: a whole 4x4x4 slice. The times are simulated.
128 devices in a mesh: section: 4 (over x), dp: 32 (over y, z, core).
Axes of the slice: x: 4, y: 4, z: 4, core: 2. Of those that a mesh axis runs over, the one named last changes fastest.
Arguments:
- section_inputs: bfloat16 [4, 4, 64, 8, 8, 512], P('section', None, 'dp'), may hold values from -6 to 6
- grad_out: bfloat16 [4, 64, 8, 8, 512], P(None, 'dp'), may hold values from -6 to 6
- point_weights: bfloat16 [4, 4, 512, 512], P('section'), may hold values from -0.125 to 0.125
- depth_weights: bfloat16 [4, 4, 9, 512], P('section'), may hold values from -2 to 2
Outputs:
- grad_inputs: bfloat16 [4, 4, 64, 8, 8, 512], P('section', None, 'dp')
- grad_point: float32 [4, 4, 512, 512], P('section', None, 'dp')
- grad_depth: float32 [4, 4, 9, 512], P('section', None, None, 'dp')
All inputs are finite; a program needn't handle non-finite values.
Results may differ from a plain program's by a relative error of at most 0.022.
Values may be sent and summed in bfloat16 or wider, within the bound.
No kernel may reach another device: no remote copies, remote signals or barrier semaphores. Data moves between devices by JAX's collectives and lax.ppermute only.
A program may use at most 128 MiB of HBM per device.

v0:
```python
import functools

import jax
import jax.numpy as jnp
from jax import lax
from jax.experimental import pallas as pl
from jax.experimental.pallas import tpu as pltpu
from jax.sharding import PartitionSpec as P

VMEM_LIMIT = 60 * 1024 * 1024


def from_behind(shard, axis, by):
    devices = lax.axis_size(axis)
    pairs = [(i, i + by) for i in range(devices) if 0 <= i + by < devices]
    return lax.ppermute(shard, axis, pairs)


def shift_rows(x, off):
    rows = x.shape[0]
    amount = (-off) % rows
    return x if amount == 0 else pltpu.roll(x, amount, 0)


def tap_mask(shape, di, dj, height, width):
    r = lax.broadcasted_iota(jnp.int32, shape, 0)
    j = lax.rem(r, width)
    i = lax.rem(lax.div(r, width), height)
    return (i + di >= 0) & (i + di < height) & (j + dj >= 0) & (j + dj < width)


def offsets():
    for di in (-1, 0, 1):
        for dj in (-1, 0, 1):
            yield 3 * (di + 1) + (dj + 1), di, dj


def stencil(x, k_ref, layer, height, width, sign):
    total = jnp.zeros(x.shape, jnp.float32)
    for tap, di, dj in offsets():
        di_s, dj_s = sign * di, sign * dj
        moved = shift_rows(x, di_s * width + dj_s)
        moved = jnp.where(tap_mask(x.shape, di_s, dj_s, height, width), moved, 0.0)
        total = total + k_ref[layer, tap : tap + 1, :] * moved
    return total


def fwd_kernel(x_ref, w_ref, k_ref, z_ref, a_ref, xs_ref, *, height, width):
    layers = w_ref.shape[0]
    field = x_ref[...]
    for layer in range(layers):
        xs_ref[layer] = field
        xf = field.astype(jnp.float32)
        zed = stencil(xf, k_ref, layer, height, width, 1)
        z_ref[layer] = zed
        act = (zed * jax.nn.sigmoid(zed)).astype(jnp.bfloat16)
        a_ref[layer] = act
        branch = jnp.dot(act, w_ref[layer], preferred_element_type=jnp.float32)
        field = (xf + branch).astype(jnp.bfloat16)


def step_kernel(p_ref, top_ref, car_ref, z_ref, w_ref, k_ref, h_in, g_ref, h_ref, *, height, width):
    del h_in
    layers = w_ref.shape[0]
    top = top_ref[...].astype(jnp.float32)
    car = car_ref[...].astype(jnp.float32)
    g = jnp.where(p_ref[1] == 1, top, car)
    g = jnp.where(p_ref[2] == 1, g, 0.0).astype(jnp.bfloat16)
    h_ref[layers] = g
    for layer in reversed(range(layers)):
        back = lax.dot_general(
            g, w_ref[layer], (((1,), (1,)), ((), ())), preferred_element_type=jnp.float32
        )
        zed = z_ref[layer]
        sig = jax.nn.sigmoid(zed)
        dzed = back * sig * (1.0 + zed * (1.0 - sig))
        g = (g.astype(jnp.float32) + stencil(dzed, k_ref, layer, height, width, -1)).astype(
            jnp.bfloat16
        )
        h_ref[layer] = g
    g_ref[...] = g


def grad_kernel(
    p_ref, h_ref, a_ref, xs_ref, z_ref, w_ref, k_ref, send_ref, res_ref, *, height, width, scale
):
    layers, chans = w_ref.shape[0], w_ref.shape[2]
    taps = k_ref.shape[1]
    batches = res_ref.shape[0]
    rows = h_ref.shape[2]
    replicas = send_ref.shape[0]
    share = chans // replicas
    pad_taps = send_ref.shape[1] - layers * share
    first = p_ref[0]
    for m in range(batches):
        res_ref[m] = h_ref[0, first + m]
    depth = []
    for layer in range(layers):
        g = h_ref[layer + 1, pl.ds(first, batches)].reshape(batches * rows, chans)
        back = lax.dot_general(
            g, w_ref[layer], (((1,), (1,)), ((), ())), preferred_element_type=jnp.float32
        )
        zed = z_ref[layer]
        sig = jax.nn.sigmoid(zed)
        dzed = back * sig * (1.0 + zed * (1.0 - sig))
        point = lax.dot_general(
            a_ref[layer], g, (((0,), (0,)), ((), ())), preferred_element_type=jnp.float32
        )
        point = point * scale
        for d in range(replicas):
            send_ref[d, layer * share : (layer + 1) * share, :] = point[
                d * share : (d + 1) * share
            ].astype(jnp.bfloat16)
        xf = xs_ref[layer].astype(jnp.float32)
        rows_out = []
        for tap, di, dj in offsets():
            moved = shift_rows(xf, di * width + dj)
            moved = jnp.where(tap_mask(xf.shape, di, dj, height, width), moved, 0.0)
            rows_out.append(jnp.sum(moved * dzed, axis=0, keepdims=True))
        rows_out.append(jnp.zeros((pad_taps - taps, chans), jnp.float32))
        depth.append(jnp.concatenate(rows_out, axis=0) * scale)
    lane = lax.broadcasted_iota(jnp.int32, (pad_taps, chans), 1)
    for d in range(replicas):
        slot = jnp.zeros((pad_taps, chans), jnp.float32)
        for layer in range(layers):
            amount = (layer * share - d * share) % chans
            moved = depth[layer] if amount == 0 else pltpu.roll(depth[layer], amount, 1)
            keep = (lane >= layer * share) & (lane < (layer + 1) * share)
            slot = jnp.where(keep, moved, slot)
        send_ref[d, layers * share :, :] = slot.astype(jnp.bfloat16)


def body(section_inputs, grad_out, point_weights, depth_weights):
    sections = lax.axis_size("section")
    replicas = lax.axis_size("dp")
    my_section = lax.axis_index("section")
    batches = grad_out.shape[0]
    layers = point_weights.shape[1]
    chans = point_weights.shape[3]
    taps = depth_weights.shape[2]
    inputs = section_inputs[0]
    images, height, width = inputs.shape[1], inputs.shape[2], inputs.shape[3]
    rows = images * height * width
    weights = point_weights[0]
    kerns = depth_weights[0].astype(jnp.float32)
    vmem = pl.BlockSpec(memory_space=pltpu.VMEM)
    smem = pl.BlockSpec(memory_space=pltpu.SMEM)
    params = pltpu.CompilerParams(vmem_limit_bytes=VMEM_LIMIT)

    zs, acts, xs = pl.pallas_call(
        functools.partial(fwd_kernel, height=height, width=width),
        out_shape=(
            jax.ShapeDtypeStruct((layers, batches * rows, chans), jnp.float32),
            jax.ShapeDtypeStruct((layers, batches * rows, chans), jnp.bfloat16),
            jax.ShapeDtypeStruct((layers, batches * rows, chans), jnp.bfloat16),
        ),
        in_specs=[vmem, vmem, vmem],
        out_specs=(vmem, vmem, vmem),
        compiler_params=params,
    )(inputs.reshape(batches * rows, chans), weights, kerns)
    z_mb = zs.reshape(layers, batches, rows, chans)
    top_all = grad_out.reshape(batches, rows, chans)

    total_steps = batches + sections - 1
    hbuf = jnp.zeros((layers + 1, total_steps, rows, chans), jnp.bfloat16)
    carried = jnp.zeros((rows, chans), jnp.bfloat16)
    is_last = (my_section == sections - 1).astype(jnp.int32)
    for step in range(total_steps):
        batch_id = step - (sections - 1) + my_section
        valid = ((batch_id >= 0) & (batch_id < batches)).astype(jnp.int32)
        picked = jnp.clip(batch_id, 0, batches - 1)
        scalars = jnp.stack([picked, is_last, valid]).astype(jnp.int32)
        grid_spec = pltpu.PrefetchScalarGridSpec(
            num_scalar_prefetch=1,
            grid=(1,),
            in_specs=[
                pl.BlockSpec((None, rows, chans), lambda i, p: (p[0], 0, 0)),
                pl.BlockSpec((rows, chans), lambda i, p: (0, 0)),
                pl.BlockSpec((layers, None, rows, chans), lambda i, p: (0, p[0], 0, 0)),
                pl.BlockSpec((layers, chans, chans), lambda i, p: (0, 0, 0)),
                pl.BlockSpec((layers, taps, chans), lambda i, p: (0, 0, 0)),
                pl.BlockSpec(memory_space=pl.ANY),
            ],
            out_specs=[
                pl.BlockSpec((rows, chans), lambda i, p: (0, 0)),
                pl.BlockSpec(
                    (layers + 1, None, rows, chans), lambda i, p, s=step: (0, s, 0, 0)
                ),
            ],
        )
        g, hbuf = pl.pallas_call(
            functools.partial(step_kernel, height=height, width=width),
            out_shape=(
                jax.ShapeDtypeStruct((rows, chans), jnp.bfloat16),
                jax.ShapeDtypeStruct(hbuf.shape, jnp.bfloat16),
            ),
            grid_spec=grid_spec,
            input_output_aliases={6: 1},
            compiler_params=params,
        )(scalars, top_all, carried, z_mb, weights, kerns, hbuf)
        if step < total_steps - 1:
            carried = from_behind(g, "section", -1)

    count = batches * images * replicas * height * width
    scale = 1.0 / float(count) ** 0.5
    share = chans // replicas
    pad_taps = -(-taps // 16) * 16
    first = jnp.reshape(sections - 1 - my_section, (1,)).astype(jnp.int32)
    send, res = pl.pallas_call(
        functools.partial(grad_kernel, height=height, width=width, scale=scale),
        out_shape=(
            jax.ShapeDtypeStruct((replicas, layers * share + pad_taps, chans), jnp.bfloat16),
            jax.ShapeDtypeStruct((batches, rows, chans), jnp.bfloat16),
        ),
        in_specs=[smem, vmem, vmem, vmem, vmem, vmem, vmem],
        out_specs=(vmem, vmem),
        compiler_params=params,
    )(first, hbuf, acts, xs, zs, weights, kerns)
    recv = lax.all_to_all(send, "dp", 0, 0, tiled=True)
    summed = jnp.sum(recv.astype(jnp.float32), axis=0)
    point_red = summed[: layers * share].reshape(layers, share, chans)
    depth_red = summed[layers * share : layers * share + taps, : layers * share]
    depth_red = depth_red.reshape(taps, layers, share).transpose(1, 0, 2)
    results = res.reshape(inputs.shape)
    return (results[None], point_red[None], depth_red[None])


def solution(mesh):
    return jax.shard_map(
        body,
        mesh=mesh,
        in_specs=(
            P("section", None, "dp", None, None, None),
            P(None, "dp", None, None, None),
            P("section", None, None, None),
            P("section", None, None, None),
        ),
        out_specs=(
            P("section", None, "dp", None, None, None),
            P("section", None, "dp", None),
            P("section", None, None, "dp"),
        ),
        check_vma=False,
    )
```

profile of v0, /device:TPU:1, one launch (start us, length us, event | category | flops | bytes accessed | tf_op | source)
XLA Modules:
  0.0 163.0 jit_solution(16694454855326613862)
XLA Ops:
  0.6 1.4 bitcast_convert_fusion.k_ref
  2.7 10.9 %shard_map.67 = (f32[4,512,512]{2,1,0:T(8,128)}, bf16[4,512,512]{2,1,0:T(8,128)(2,1)}, bf16[4,512,512]{2,1,0:T(8,128)(2,1)}) custom-call(bf16[512,512]{1,0:T(8,128)(2,1)} %bitcast.51, bf16[4,512,512]{2,1,0:T(8,128)(2,1)} %bitcast.35, f32[4,9,512]{2,1,0:T(8,128)} %bitcast_convert_fusion.k_ref), custom_call_target="tpu_custom_call" | custom-call | tf_op jit(solution)/shard_map/pallas_call | solution.py:150
  13.6 2.6 %broadcast_in_dim.10.h_in = bf16[5,7,128,512]{3,2,1,0:T(8,128)(2,1)} broadcast(bf16[]{:T(256)} %constant.11.clone.1), dimensions={} | broadcast | bytes 4587522 | tf_op jit(solution)/shard_map/broadcast_in_dim | solution.py:165
  16.9 5.6 %shard_map.68 = (bf16[128,512]{1,0:T(8,128)(2,1)}, bf16[5,7,128,512]{3,2,1,0:T(8,128)(2,1)}) custom-call(s32[3]{0:T(128)} %pad_add_fusion.6.p_ref, bf16[4,128,512]{2,1,0:T(8,128)(2,1)} %bitcast.44, bf16[128,512]{1,0:T(8,128)(2,1)} %broadcast_in_dim.9.car_ref, f32[4,4,128,512]{3,2,1,0:T(8,128)} %bitcast.28, ...), custom_call_target="tpu_custom_call", output_to_operand_aliasing={{1}: (6, {})} | custom-call | tf_op jit(solution)/shard_map/pallas_call | solution.py:191
  22.5 1.3 collective-permute-start
  24.5 5.0 %collective-permute-done.car_ref = bf16[128,512]{1,0:T(8,128)(2,1)S(1)} collective-permute-done((bf16[128,512]{1,0:T(8,128)(2,1)}, bf16[128,512]{1,0:T(8,128)(2,1)S(1)}, u32[]{:S(2)}, u32[]{:S(2)}) %collective-permute-start) | collective-permute-done | bytes 131104 | tf_op jit(solution)/shard_map/ppermute | solution.py:16
  30.1 5.6 %shard_map.69 = (bf16[128,512]{1,0:T(8,128)(2,1)}, bf16[5,7,128,512]{3,2,1,0:T(8,128)(2,1)}) custom-call(s32[3]{0:T(128)} %pad_add_fusion.5.p_ref, bf16[4,128,512]{2,1,0:T(8,128)(2,1)} %bitcast.45, bf16[128,512]{1,0:T(8,128)(2,1)} %copy-done.1, f32[4,4,128,512]{3,2,1,0:T(8,128)} %bitcast.29, ...), custom_call_target="tpu_custom_call", output_to_operand_aliasing={{1}: (6, {})} | custom-call | tf_op jit(solution)/shard_map/pallas_call | solution.py:191
  35.7 1.5 collective-permute-start.1
  37.8 3.9 %collective-permute-done.1.car_ref = bf16[128,512]{1,0:T(8,128)(2,1)S(1)} collective-permute-done((bf16[128,512]{1,0:T(8,128)(2,1)}, bf16[128,512]{1,0:T(8,128)(2,1)S(1)}, u32[]{:S(2)}, u32[]{:S(2)}) %collective-permute-start.1) | collective-permute-done | bytes 131104 | tf_op jit(solution)/shard_map/ppermute | solution.py:16
  42.4 5.6 %shard_map.70 = (bf16[128,512]{1,0:T(8,128)(2,1)}, bf16[5,7,128,512]{3,2,1,0:T(8,128)(2,1)}) custom-call(s32[3]{0:T(128)} %pad_add_fusion.4.p_ref, bf16[4,128,512]{2,1,0:T(8,128)(2,1)} %bitcast.46, bf16[128,512]{1,0:T(8,128)(2,1)} %copy-done.2, f32[4,4,128,512]{3,2,1,0:T(8,128)} %bitcast.30, ...), custom_call_target="tpu_custom_call", output_to_operand_aliasing={{1}: (6, {})} | custom-call | tf_op jit(solution)/shard_map/pallas_call | solution.py:191
  48.0 1.3 collective-permute-start.2
  49.9 4.0 %collective-permute-done.2.car_ref = bf16[128,512]{1,0:T(8,128)(2,1)S(1)} collective-permute-done((bf16[128,512]{1,0:T(8,128)(2,1)}, bf16[128,512]{1,0:T(8,128)(2,1)S(1)}, u32[]{:S(2)}, u32[]{:S(2)}) %collective-permute-start.2) | collective-permute-done | bytes 131104 | tf_op jit(solution)/shard_map/ppermute | solution.py:16
  54.6 5.6 %shard_map.71 = (bf16[128,512]{1,0:T(8,128)(2,1)}, bf16[5,7,128,512]{3,2,1,0:T(8,128)(2,1)}) custom-call(s32[3]{0:T(128)} %pad_add_fusion.3.p_ref, bf16[4,128,512]{2,1,0:T(8,128)(2,1)} %bitcast.47, bf16[128,512]{1,0:T(8,128)(2,1)} %copy-done.5, f32[4,4,128,512]{3,2,1,0:T(8,128)} %bitcast.31, ...), custom_call_target="tpu_custom_call", output_to_operand_aliasing={{1}: (6, {})} | custom-call | tf_op jit(solution)/shard_map/pallas_call | solution.py:191
  60.1 1.3 collective-permute-start.3
  62.1 4.0 %collective-permute-done.3.car_ref = bf16[128,512]{1,0:T(8,128)(2,1)S(1)} collective-permute-done((bf16[128,512]{1,0:T(8,128)(2,1)}, bf16[128,512]{1,0:T(8,128)(2,1)S(1)}, u32[]{:S(2)}, u32[]{:S(2)}) %collective-permute-start.3) | collective-permute-done | bytes 131104 | tf_op jit(solution)/shard_map/ppermute | solution.py:16
  66.7 5.6 %shard_map.72 = (bf16[128,512]{1,0:T(8,128)(2,1)}, bf16[5,7,128,512]{3,2,1,0:T(8,128)(2,1)}) custom-call(s32[3]{0:T(128)} %pad_add_fusion.2.p_ref, bf16[4,128,512]{2,1,0:T(8,128)(2,1)} %bitcast.48, bf16[128,512]{1,0:T(8,128)(2,1)} %copy-done.3, f32[4,4,128,512]{3,2,1,0:T(8,128)} %bitcast.32, ...), custom_call_target="tpu_custom_call", output_to_operand_aliasing={{1}: (6, {})} | custom-call | tf_op jit(solution)/shard_map/pallas_call | solution.py:191
  72.3 1.3 collective-permute-start.4
  74.2 4.0 %collective-permute-done.4.car_ref = bf16[128,512]{1,0:T(8,128)(2,1)S(1)} collective-permute-done((bf16[128,512]{1,0:T(8,128)(2,1)}, bf16[128,512]{1,0:T(8,128)(2,1)S(1)}, u32[]{:S(2)}, u32[]{:S(2)}) %collective-permute-start.4) | collective-permute-done | bytes 131104 | tf_op jit(solution)/shard_map/ppermute | solution.py:16
  78.8 5.6 %shard_map.73 = (bf16[128,512]{1,0:T(8,128)(2,1)}, bf16[5,7,128,512]{3,2,1,0:T(8,128)(2,1)}) custom-call(s32[3]{0:T(128)} %pad_add_fusion.1.p_ref, bf16[4,128,512]{2,1,0:T(8,128)(2,1)} %bitcast.49, bf16[128,512]{1,0:T(8,128)(2,1)} %copy-done.4, f32[4,4,128,512]{3,2,1,0:T(8,128)} %bitcast.33, ...), custom_call_target="tpu_custom_call", output_to_operand_aliasing={{1}: (6, {})} | custom-call | tf_op jit(solution)/shard_map/pallas_call | solution.py:191
  84.4 1.5 collective-permute-start.5
  86.6 3.7 %collective-permute-done.5.car_ref = bf16[128,512]{1,0:T(8,128)(2,1)S(1)} collective-permute-done((bf16[128,512]{1,0:T(8,128)(2,1)}, bf16[128,512]{1,0:T(8,128)(2,1)S(1)}, u32[]{:S(2)}, u32[]{:S(2)}) %collective-permute-start.5) | collective-permute-done | bytes 131104 | tf_op jit(solution)/shard_map/ppermute | solution.py:16
  90.9 5.6 %shard_map.74 = (bf16[128,512]{1,0:T(8,128)(2,1)}, bf16[5,7,128,512]{3,2,1,0:T(8,128)(2,1)}) custom-call(s32[3]{0:T(128)} %pad_add_fusion.p_ref, bf16[4,128,512]{2,1,0:T(8,128)(2,1)} %bitcast.50, bf16[128,512]{1,0:T(8,128)(2,1)} %copy-done, f32[4,4,128,512]{3,2,1,0:T(8,128)} %bitcast.34, ...), custom_call_target="tpu_custom_call", output_to_operand_aliasing={{1}: (6, {})} | custom-call | tf_op jit(solution)/shard_map/pallas_call | solution.py:191
  96.5 15.1 %shard_map.75 = (bf16[32,80,512]{2,1,0:T(8,128)(2,1)}, bf16[4,128,512]{2,1,0:T(8,128)(2,1)}) custom-call(s32[1]{0:T(128)} %bitcast.p_ref, bf16[5,7,128,512]{3,2,1,0:T(8,128)(2,1)} %get-tuple-element.34.h_ref, bf16[4,512,512]{2,1,0:T(8,128)(2,1)} %get-tuple-element.35.a_ref, bf16[4,512,512]{2,1,0:T(8,128)(2,1)} %get-tuple-element.36.xs_ref, ...), custom_call_target="tpu_custom_call" | custom-call | tf_op jit(solution)/shard_map/pallas_call | solution.py:209
  111.6 49.7 %all_to_all.5 = bf16[32,80,512]{2,1,0:T(8,128)(2,1)S(1)} all-to-all(bf16[32,80,512]{2,1,0:T(8,128)(2,1)} %get-tuple-element.38), channel_id=1, replica_groups=mesh['section'=4,'dp'=32] {'dp'}, dimensions={0} | all-to-all | bytes 5242880 | tf_op jit(solution)/shard_map/all_to_all | solution.py:219
  (24 shorter events, 10.9 us)
Async XLA Ops:
  22.5 6.9 %collective-permute-start = (bf16[128,512]{1,0:T(8,128)(2,1)}, bf16[128,512]{1,0:T(8,128)(2,1)S(1)}, u32[]{:S(2)}, u32[]{:S(2)}) collective-permute-start(bf16[128,512]{1,0:T(8,128)(2,1)} %get-tuple-element.22), channel_id=1, source_target_pairs={{32,0},{64,32},{96,64},{33,1},{65,33},{97,65},{34,2},{66,34},{98,6... | collective-permute-start | bytes 393224 | tf_op jit(solution)/shard_map/ppermute | solution.py:16
  29.4 0.7 copy-start.1
  35.7 6.0 %collective-permute-start.1 = (bf16[128,512]{1,0:T(8,128)(2,1)}, bf16[128,512]{1,0:T(8,128)(2,1)S(1)}, u32[]{:S(2)}, u32[]{:S(2)}) collective-permute-start(bf16[128,512]{1,0:T(8,128)(2,1)} %get-tuple-element.24), channel_id=1, source_target_pairs={{32,0},{64,32},{96,64},{33,1},{65,33},{97,65},{34,2},{66,34},{98,6... | collective-permute-start | bytes 393224 | tf_op jit(solution)/shard_map/ppermute | solution.py:16
  41.7 0.7 copy-start.2
  48.0 5.9 %collective-permute-start.2 = (bf16[128,512]{1,0:T(8,128)(2,1)}, bf16[128,512]{1,0:T(8,128)(2,1)S(1)}, u32[]{:S(2)}, u32[]{:S(2)}) collective-permute-start(bf16[128,512]{1,0:T(8,128)(2,1)} %get-tuple-element.26), channel_id=1, source_target_pairs={{32,0},{64,32},{96,64},{33,1},{65,33},{97,65},{34,2},{66,34},{98,6... | collective-permute-start | bytes 393224 | tf_op jit(solution)/shard_map/ppermute | solution.py:16
  53.9 0.7 copy-start.5
  60.1 5.9 %collective-permute-start.3 = (bf16[128,512]{1,0:T(8,128)(2,1)}, bf16[128,512]{1,0:T(8,128)(2,1)S(1)}, u32[]{:S(2)}, u32[]{:S(2)}) collective-permute-start(bf16[128,512]{1,0:T(8,128)(2,1)} %get-tuple-element.28), channel_id=1, source_target_pairs={{32,0},{64,32},{96,64},{33,1},{65,33},{97,65},{34,2},{66,34},{98,6... | collective-permute-start | bytes 393224 | tf_op jit(solution)/shard_map/ppermute | solution.py:16
  66.0 0.7 copy-start.3
  72.3 5.9 %collective-permute-start.4 = (bf16[128,512]{1,0:T(8,128)(2,1)}, bf16[128,512]{1,0:T(8,128)(2,1)S(1)}, u32[]{:S(2)}, u32[]{:S(2)}) collective-permute-start(bf16[128,512]{1,0:T(8,128)(2,1)} %get-tuple-element.30), channel_id=1, source_target_pairs={{32,0},{64,32},{96,64},{33,1},{65,33},{97,65},{34,2},{66,34},{98,6... | collective-permute-start | bytes 393224 | tf_op jit(solution)/shard_map/ppermute | solution.py:16
  78.2 0.7 copy-start.4
  84.4 5.9 %collective-permute-start.5 = (bf16[128,512]{1,0:T(8,128)(2,1)}, bf16[128,512]{1,0:T(8,128)(2,1)S(1)}, u32[]{:S(2)}, u32[]{:S(2)}) collective-permute-start(bf16[128,512]{1,0:T(8,128)(2,1)} %get-tuple-element.32), channel_id=1, source_target_pairs={{32,0},{64,32},{96,64},{33,1},{65,33},{97,65},{34,2},{66,34},{98,6... | collective-permute-start | bytes 393224 | tf_op jit(solution)/shard_map/ppermute | solution.py:16
  90.3 0.7 copy-start
where the time goes:
time: 164 us; the launch traced here: 163 us
  Pallas kernels  65 us (40%)
  blocking collectives  49.7 us (30%)
  waiting for transfers between devices  24.5 us (15%)
  local copies, waits for them, and re-layouts  8.59 us (5%)
  starting transfers between devices  8.08 us (5%)
  other arithmetic  6.38 us (4%)
    all_to_all x1, blocking collectives, body(): recv = lax.all_to_all(send, 'dp', 0, 0, tiled=True)  49.7 us
    pallas_call x7, Pallas kernels, body(): pl.pallas_call(functools.partial(step_kernel, height=height, width=width)...  39 us
    ppermute x6, waiting for transfers between devices, from_behind(): return lax.ppermute(shard, axis, pairs)  24.5 us
    pallas_call x1, Pallas kernels, body(): pl.pallas_call(functools.partial(grad_kernel, height=height, width=width,...  15.1 us
    pallas_call x1, Pallas kernels, body(): pl.pallas_call(functools.partial(fwd_kernel, height=height, width=width),...  10.9 us
    ppermute x6, starting transfers between devices, from_behind(): return lax.ppermute(shard, axis, pairs)  8.08 us
    another operation x7, other arithmetic, body(): scalars = jnp.stack([picked, is_last, valid]).astype(jnp.int32)  4.58 us
    unnamed x12, local copies, waits for them, and re-layouts  3.93 us
  transfers between devices with their start and end apart: 6, of which 6 were waited for; matrix products, arithmetic and copies ran while one was open for 2% of the time, Pallas kernels for 0%

commit v1 on v0

--- a/solution.py
+++ b/solution.py
@@ -45,7 +45,8 @@
     return total
 
 
-def fwd_kernel(x_ref, w_ref, k_ref, z_ref, a_ref, xs_ref, *, height, width):
+def fwd_kernel(p_ref, x_ref, w_ref, k_ref, *refs, height, width):
+    z_ref, a_ref, xs_ref = refs[-3:]
     layers = w_ref.shape[0]
     field = x_ref[...]
     for layer in range(layers):
@@ -57,6 +58,11 @@
         a_ref[layer] = act
         branch = jnp.dot(act, w_ref[layer], preferred_element_type=jnp.float32)
         field = (xf + branch).astype(jnp.bfloat16)
+
+
+def fwd_first_kernel(p_ref, x_ref, w_ref, k_ref, z_ref, a_ref, xs_ref, h_ref, *, height, width):
+    del h_ref
+    fwd_kernel(p_ref, x_ref, w_ref, k_ref, z_ref, a_ref, xs_ref, height=height, width=width)
 
 
 def step_kernel(p_ref, top_ref, car_ref, z_ref, w_ref, k_ref, h_in, g_ref, h_ref, *, height, width):
@@ -147,28 +153,51 @@
     smem = pl.BlockSpec(memory_space=pltpu.SMEM)
     params = pltpu.CompilerParams(vmem_limit_bytes=VMEM_LIMIT)
 
-    zs, acts, xs = pl.pallas_call(
-        functools.partial(fwd_kernel, height=height, width=width),
-        out_shape=(
-            jax.ShapeDtypeStruct((layers, batches * rows, chans), jnp.float32),
-            jax.ShapeDtypeStruct((layers, batches * rows, chans), jnp.bfloat16),
-            jax.ShapeDtypeStruct((layers, batches * rows, chans), jnp.bfloat16),
-        ),
-        in_specs=[vmem, vmem, vmem],
-        out_specs=(vmem, vmem, vmem),
+    fwd_flops = 2 * layers * rows * chans * (chans + 3 * taps)
+    fwd_cost = pl.CostEstimate(
+        flops=fwd_flops,
+        transcendentals=layers * rows * chans,
+        bytes_accessed=2 * layers * chans * chans + 8 * layers * rows * chans,
+    )
+    top_all = grad_out.reshape(batches, rows, chans)
+    x_all = inputs.reshape(batches, rows, chans)
+    total_steps = batches + sections - 1
+    buf_shapes = (
+        jax.ShapeDtypeStruct((layers, batches, rows, chans), jnp.float32),
+        jax.ShapeDtypeStruct((layers, batches, rows, chans), jnp.bfloat16),
+        jax.ShapeDtypeStruct((layers, batches, rows, chans), jnp.bfloat16),
+    )
+    slot_spec = pl.BlockSpec((layers, None, rows, chans), lambda i, p: (0, p[0], 0, 0))
+    fwd_in = [
+        pl.BlockSpec((None, rows, chans), lambda i, p: (p[0], 0, 0)),
+        pl.BlockSpec((layers, chans, chans), lambda i, p: (0, 0, 0)),
+        pl.BlockSpec((layers, taps, chans), lambda i, p: (0, 0, 0)),
+    ]
+
+    def picked_at(step):
+        batch_id = step - (sections - 1) + my_section
+        valid = ((batch_id >= 0) & (batch_id < batches)).astype(jnp.int32)
+        return jnp.clip(batch_id, 0, batches - 1), valid
+
+    picked, _ = picked_at(0)
+    zbuf, abuf, xbuf, hbuf = pl.pallas_call(
+        functools.partial(fwd_first_kernel, height=height, width=width),
+        out_shape=buf_shapes
+        + (jax.ShapeDtypeStruct((layers + 1, total_steps, rows, chans), jnp.bfloat16),),
+        grid_spec=pltpu.PrefetchScalarGridSpec(
+            num_scalar_prefetch=1,
+            grid=(1,),
+            in_specs=fwd_in,
+            out_specs=[slot_spec, slot_spec, slot_spec, pl.BlockSpec(memory_space=pl.ANY)],
+        ),
         compiler_params=params,
-    )(inputs.reshape(batches * rows, chans), weights, kerns)
-    z_mb = zs.reshape(layers, batches, rows, chans)
-    top_all = grad_out.reshape(batches, rows, chans)
-
-    total_steps = batches + sections - 1
-    hbuf = jnp.zeros((layers + 1, total_steps, rows, chans), jnp.bfloat16)
+        cost_estimate=fwd_cost,
+    )(jnp.reshape(picked, (1,)).astype(jnp.int32), x_all, weights, kerns)
+
     carried = jnp.zeros((rows, chans), jnp.bfloat16)
     is_last = (my_section == sections - 1).astype(jnp.int32)
     for step in range(total_steps):
-        batch_id = step - (sections - 1) + my_section
-        valid = ((batch_id >= 0) & (batch_id < batches)).astype(jnp.int32)
-        picked = jnp.clip(batch_id, 0, batches - 1)
+        picked, valid = picked_at(step)
         scalars = jnp.stack([picked, is_last, valid]).astype(jnp.int32)
         grid_spec = pltpu.PrefetchScalarGridSpec(
             num_scalar_prefetch=1,
@@ -197,9 +226,27 @@
             grid_spec=grid_spec,
             input_output_aliases={6: 1},
             compiler_params=params,
-        )(scalars, top_all, carried, z_mb, weights, kerns, hbuf)
+            cost_estimate=fwd_cost,
+        )(scalars, top_all, carried, zbuf, weights, kerns, hbuf)
         if step < total_steps - 1:
             carried = from_behind(g, "section", -1)
+            nxt, _ = picked_at(step + 1)
+            zbuf, abuf, xbuf = pl.pallas_call(
+                functools.partial(fwd_kernel, height=height, width=width),
+                out_shape=buf_shapes,
+                grid_spec=pltpu.PrefetchScalarGridSpec(
+                    num_scalar_prefetch=1,
+                    grid=(1,),
+                    in_specs=fwd_in + [pl.BlockSpec(memory_space=pl.ANY)] * 3,
+                    out_specs=[slot_spec, slot_spec, slot_spec],
+                ),
+                input_output_aliases={4: 0, 5: 1, 6: 2},
+                compiler_params=params,
+                cost_estimate=fwd_cost,
+            )(jnp.reshape(nxt, (1,)).astype(jnp.int32), x_all, weights, kerns, zbuf, abuf, xbuf)
+    zs = zbuf.reshape(layers, batches * rows, chans)
+    acts = abuf.reshape(layers, batches * rows, chans)
+    xs = xbuf.reshape(layers, batches * rows, chans)
 
     count = batches * images * replicas * height * width
     scale = 1.0 / float(count) ** 0.5

time: 164 us -> 156 us (0.951)
  the two profiles are of different devices: /device:TPU:1 before, /device:TPU:6 now
where the time goes in v1:
time: 156 us; the launch traced here: 155 us
  Pallas kernels  85.9 us (55%)
  blocking collectives  42.2 us (27%)
  starting transfers between devices  13.7 us (9%)
  other arithmetic  6.28 us (4%)
  local copies, waits for them, and re-layouts  5.95 us (4%)
    all_to_all x1, blocking collectives, body(): recv = lax.all_to_all(send, 'dp', 0, 0, tiled=True)  42.2 us
    pallas_call x7, Pallas kernels, body(): pl.pallas_call(functools.partial(step_kernel, height=height, width=width)...  39.1 us
    pallas_call x6, Pallas kernels, body(): pl.pallas_call(functools.partial(fwd_kernel, height=height, width=width),...  27.2 us
    pallas_call x1, Pallas kernels, body(): pl.pallas_call(functools.partial(grad_kernel, height=height, width=width,...  15.1 us
    ppermute x6, starting transfers between devices, from_behind(): return lax.ppermute(shard, axis, pairs)  13.7 us
    pallas_call x1, Pallas kernels, body(): pl.pallas_call(functools.partial(fwd_first_kernel, height=height, width=w...  4.55 us
    another operation x7, other arithmetic, body(): scalars = jnp.stack([picked, is_last, valid]).astype(jnp.int32)  4.47 us
    unnamed x12, local copies, waits for them, and re-layouts  3.93 us
  transfers between devices with their start and end apart: 6, of which 0 were waited for; matrix products, arithmetic and copies ran while one was open for 2% of the time, Pallas kernels for 18%

profile of v1, /device:TPU:6, one launch (start us, length us, event | category | flops | bytes accessed | tf_op | source)
XLA Modules:
  0.0 154.8 jit_solution(9595299039391045189)
XLA Ops:
  0.6 1.4 bitcast_convert_fusion.k_ref
  2.7 4.5 %shard_map.67 = (f32[4,4,128,512]{3,2,1,0:T(8,128)}, bf16[4,4,128,512]{3,2,1,0:T(8,128)(2,1)}, bf16[4,4,128,512]{3,2,1,0:T(8,128)(2,1)}, bf16[5,7,128,512]{3,2,1,0:T(8,128)(2,1)}) custom-call(s32[1]{0:T(128)} %bitcast.15.p_ref, bf16[4,128,512]{2,1,0:T(8,128)(2,1)} %bitcast.55, bf16[4,512,512]{2,1,0:T(8,128)(2,1)} %bitcast.31, ...), custom_call_target="tpu_custom_call" | custom-call | flops 282591232 | bytes 4194304 | tf_op jit(solution)/shard_map/pallas_call | solution.py:183
  8.0 5.6 %shard_map.68 = (bf16[128,512]{1,0:T(8,128)(2,1)}, bf16[5,7,128,512]{3,2,1,0:T(8,128)(2,1)}) custom-call(s32[3]{0:T(128)} %pad_add_fusion.6.p_ref, bf16[4,128,512]{2,1,0:T(8,128)(2,1)} %bitcast.48, bf16[128,512]{1,0:T(8,128)(2,1)} %broadcast_in_dim.6.car_ref, f32[4,4,128,512]{3,2,1,0:T(8,128)} %get-tuple-element.40.z_ref.refs_0_, ...), custom_call_target="tpu_custom_call", output_to_operand_aliasing={{1}: (6, {})} | custom-call | flops 282591232 | bytes 4194304 | tf_op jit(solution)/shard_map/pallas_call | solution.py:220
  13.5 2.7 %collective-permute-start = (bf16[128,512]{1,0:T(8,128)(2,1)}, bf16[128,512]{1,0:T(8,128)(2,1)S(1)}, u32[]{:S(2)}, u32[]{:S(2)}) collective-permute-start(bf16[128,512]{1,0:T(8,128)(2,1)} %get-tuple-element.42), channel_id=1, source_target_pairs={{32,0},{64,32},{96,64},{33,1},{65,33},{97,65},{34,2},{66,34},{98,6... | collective-permute-start | bytes 393224 | tf_op jit(solution)/shard_map/ppermute | solution.py:16
  16.3 4.5 %shard_map.69 = (f32[4,4,128,512]{3,2,1,0:T(8,128)}, bf16[4,4,128,512]{3,2,1,0:T(8,128)(2,1)}, bf16[4,4,128,512]{3,2,1,0:T(8,128)(2,1)}) custom-call(s32[1]{0:T(128)} %bitcast.13.p_ref, bf16[4,128,512]{2,1,0:T(8,128)(2,1)} %bitcast.56, bf16[4,512,512]{2,1,0:T(8,128)(2,1)} %bitcast.33, ...), custom_call_target="tpu_custom_call", output_to_operand_aliasing={{0}: (4, {}), {1}: (5, {}), {2}: (6, {})} | custom-call | flops 282591232 | bytes 4194304 | tf_op jit(solution)/shard_map/pallas_call | solution.py:234
  22.1 5.6 %shard_map.70 = (bf16[128,512]{1,0:T(8,128)(2,1)}, bf16[5,7,128,512]{3,2,1,0:T(8,128)(2,1)}) custom-call(s32[3]{0:T(128)} %pad_add_fusion.5.p_ref, bf16[4,128,512]{2,1,0:T(8,128)(2,1)} %bitcast.49, bf16[128,512]{1,0:T(8,128)(2,1)} %copy-done, f32[4,4,128,512]{3,2,1,0:T(8,128)} %get-tuple-element.45.z_ref.refs_0_, ...), custom_call_target="tpu_custom_call", output_to_operand_aliasing={{1}: (6, {})} | custom-call | flops 282591232 | bytes 4194304 | tf_op jit(solution)/shard_map/pallas_call | solution.py:220
  27.7 2.4 %collective-permute-start.1 = (bf16[128,512]{1,0:T(8,128)(2,1)}, bf16[128,512]{1,0:T(8,128)(2,1)S(1)}, u32[]{:S(2)}, u32[]{:S(2)}) collective-permute-start(bf16[128,512]{1,0:T(8,128)(2,1)} %get-tuple-element.47), channel_id=1, source_target_pairs={{32,0},{64,32},{96,64},{33,1},{65,33},{97,65},{34,2},{66,34},{98,6... | collective-permute-start | bytes 393224 | tf_op jit(solution)/shard_map/ppermute | solution.py:16
  30.8 4.5 %shard_map.71 = (f32[4,4,128,512]{3,2,1,0:T(8,128)}, bf16[4,4,128,512]{3,2,1,0:T(8,128)(2,1)}, bf16[4,4,128,512]{3,2,1,0:T(8,128)(2,1)}) custom-call(s32[1]{0:T(128)} %bitcast.11.p_ref, bf16[4,128,512]{2,1,0:T(8,128)(2,1)} %bitcast.57, bf16[4,512,512]{2,1,0:T(8,128)(2,1)} %bitcast.35, ...), custom_call_target="tpu_custom_call", output_to_operand_aliasing={{0}: (4, {}), {1}: (5, {}), {2}: (6, {})} | custom-call | flops 282591232 | bytes 4194304 | tf_op jit(solution)/shard_map/pallas_call | solution.py:234
  36.0 5.6 %shard_map.72 = (bf16[128,512]{1,0:T(8,128)(2,1)}, bf16[5,7,128,512]{3,2,1,0:T(8,128)(2,1)}) custom-call(s32[3]{0:T(128)} %pad_add_fusion.4.p_ref, bf16[4,128,512]{2,1,0:T(8,128)(2,1)} %bitcast.50, bf16[128,512]{1,0:T(8,128)(2,1)} %copy-done.2, f32[4,4,128,512]{3,2,1,0:T(8,128)} %get-tuple-element.50.z_ref.refs_0_, ...), custom_call_target="tpu_custom_call", output_to_operand_aliasing={{1}: (6, {})} | custom-call | flops 282591232 | bytes 4194304 | tf_op jit(solution)/shard_map/pallas_call | solution.py:220
  41.6 2.5 %collective-permute-start.2 = (bf16[128,512]{1,0:T(8,128)(2,1)}, bf16[128,512]{1,0:T(8,128)(2,1)S(1)}, u32[]{:S(2)}, u32[]{:S(2)}) collective-permute-start(bf16[128,512]{1,0:T(8,128)(2,1)} %get-tuple-element.52), channel_id=1, source_target_pairs={{32,0},{64,32},{96,64},{33,1},{65,33},{97,65},{34,2},{66,34},{98,6... | collective-permute-start | bytes 393224 | tf_op jit(solution)/shard_map/ppermute | solution.py:16
  44.7 4.5 %shard_map.73 = (f32[4,4,128,512]{3,2,1,0:T(8,128)}, bf16[4,4,128,512]{3,2,1,0:T(8,128)(2,1)}, bf16[4,4,128,512]{3,2,1,0:T(8,128)(2,1)}) custom-call(s32[1]{0:T(128)} %bitcast.9.p_ref, bf16[4,128,512]{2,1,0:T(8,128)(2,1)} %bitcast.58, bf16[4,512,512]{2,1,0:T(8,128)(2,1)} %bitcast.37, ...), custom_call_target="tpu_custom_call", output_to_operand_aliasing={{0}: (4, {}), {1}: (5, {}), {2}: (6, {})} | custom-call | flops 282591232 | bytes 4194304 | tf_op jit(solution)/shard_map/pallas_call | solution.py:234
  49.9 5.6 %shard_map.74 = (bf16[128,512]{1,0:T(8,128)(2,1)}, bf16[5,7,128,512]{3,2,1,0:T(8,128)(2,1)}) custom-call(s32[3]{0:T(128)} %pad_add_fusion.3.p_ref, bf16[4,128,512]{2,1,0:T(8,128)(2,1)} %bitcast.51, bf16[128,512]{1,0:T(8,128)(2,1)} %copy-done.3, f32[4,4,128,512]{3,2,1,0:T(8,128)} %get-tuple-element.55.z_ref.refs_0_, ...), custom_call_target="tpu_custom_call", output_to_operand_aliasing={{1}: (6, {})} | custom-call | flops 282591232 | bytes 4194304 | tf_op jit(solution)/shard_map/pallas_call | solution.py:220
  55.5 2.0 %collective-permute-start.3 = (bf16[128,512]{1,0:T(8,128)(2,1)}, bf16[128,512]{1,0:T(8,128)(2,1)S(1)}, u32[]{:S(2)}, u32[]{:S(2)}) collective-permute-start(bf16[128,512]{1,0:T(8,128)(2,1)} %get-tuple-element.57), channel_id=1, source_target_pairs={{32,0},{64,32},{96,64},{33,1},{65,33},{97,65},{34,2},{66,34},{98,6... | collective-permute-start | bytes 393224 | tf_op jit(solution)/shard_map/ppermute | solution.py:16
  58.1 4.5 %shard_map.75 = (f32[4,4,128,512]{3,2,1,0:T(8,128)}, bf16[4,4,128,512]{3,2,1,0:T(8,128)(2,1)}, bf16[4,4,128,512]{3,2,1,0:T(8,128)(2,1)}) custom-call(s32[1]{0:T(128)} %bitcast.7.p_ref, bf16[4,128,512]{2,1,0:T(8,128)(2,1)} %bitcast.59, bf16[4,512,512]{2,1,0:T(8,128)(2,1)} %bitcast.39, ...), custom_call_target="tpu_custom_call", output_to_operand_aliasing={{0}: (4, {}), {1}: (5, {}), {2}: (6, {})} | custom-call | flops 282591232 | bytes 4194304 | tf_op jit(solution)/shard_map/pallas_call | solution.py:234
  63.3 5.6 %shard_map.76 = (bf16[128,512]{1,0:T(8,128)(2,1)}, bf16[5,7,128,512]{3,2,1,0:T(8,128)(2,1)}) custom-call(s32[3]{0:T(128)} %pad_add_fusion.2.p_ref, bf16[4,128,512]{2,1,0:T(8,128)(2,1)} %bitcast.52, bf16[128,512]{1,0:T(8,128)(2,1)} %copy-done.4, f32[4,4,128,512]{3,2,1,0:T(8,128)} %get-tuple-element.60.z_ref.refs_0_, ...), custom_call_target="tpu_custom_call", output_to_operand_aliasing={{1}: (6, {})} | custom-call | flops 282591232 | bytes 4194304 | tf_op jit(solution)/shard_map/pallas_call | solution.py:220
  68.9 1.9 %collective-permute-start.4 = (bf16[128,512]{1,0:T(8,128)(2,1)}, bf16[128,512]{1,0:T(8,128)(2,1)S(1)}, u32[]{:S(2)}, u32[]{:S(2)}) collective-permute-start(bf16[128,512]{1,0:T(8,128)(2,1)} %get-tuple-element.62), channel_id=1, source_target_pairs={{32,0},{64,32},{96,64},{33,1},{65,33},{97,65},{34,2},{66,34},{98,6... | collective-permute-start | bytes 393224 | tf_op jit(solution)/shard_map/ppermute | solution.py:16
  71.5 4.5 %shard_map.77 = (f32[4,4,128,512]{3,2,1,0:T(8,128)}, bf16[4,4,128,512]{3,2,1,0:T(8,128)(2,1)}, bf16[4,4,128,512]{3,2,1,0:T(8,128)(2,1)}) custom-call(s32[1]{0:T(128)} %bitcast.5.p_ref, bf16[4,128,512]{2,1,0:T(8,128)(2,1)} %bitcast.60, bf16[4,512,512]{2,1,0:T(8,128)(2,1)} %bitcast.41, ...), custom_call_target="tpu_custom_call", output_to_operand_aliasing={{0}: (4, {}), {1}: (5, {}), {2}: (6, {})} | custom-call | flops 282591232 | bytes 4194304 | tf_op jit(solution)/shard_map/pallas_call | solution.py:234
  76.7 5.6 %shard_map.78 = (bf16[128,512]{1,0:T(8,128)(2,1)}, bf16[5,7,128,512]{3,2,1,0:T(8,128)(2,1)}) custom-call(s32[3]{0:T(128)} %pad_add_fusion.1.p_ref, bf16[4,128,512]{2,1,0:T(8,128)(2,1)} %bitcast.53, bf16[128,512]{1,0:T(8,128)(2,1)} %copy-done.5, f32[4,4,128,512]{3,2,1,0:T(8,128)} %get-tuple-element.65.z_ref.refs_0_, ...), custom_call_target="tpu_custom_call", output_to_operand_aliasing={{1}: (6, {})} | custom-call | flops 282591232 | bytes 4194304 | tf_op jit(solution)/shard_map/pallas_call | solution.py:220
  82.3 2.1 %collective-permute-start.5 = (bf16[128,512]{1,0:T(8,128)(2,1)}, bf16[128,512]{1,0:T(8,128)(2,1)S(1)}, u32[]{:S(2)}, u32[]{:S(2)}) collective-permute-start(bf16[128,512]{1,0:T(8,128)(2,1)} %get-tuple-element.67), channel_id=1, source_target_pairs={{32,0},{64,32},{96,64},{33,1},{65,33},{97,65},{34,2},{66,34},{98,6... | collective-permute-start | bytes 393224 | tf_op jit(solution)/shard_map/ppermute | solution.py:16
  85.0 4.5 %shard_map.79 = (f32[4,4,128,512]{3,2,1,0:T(8,128)}, bf16[4,4,128,512]{3,2,1,0:T(8,128)(2,1)}, bf16[4,4,128,512]{3,2,1,0:T(8,128)(2,1)}) custom-call(s32[1]{0:T(128)} %bitcast.1.p_ref, bf16[4,128,512]{2,1,0:T(8,128)(2,1)} %bitcast.61, bf16[4,512,512]{2,1,0:T(8,128)(2,1)} %bitcast.43, ...), custom_call_target="tpu_custom_call", output_to_operand_aliasing={{0}: (4, {}), {1}: (5, {}), {2}: (6, {})} | custom-call | flops 282591232 | bytes 4194304 | tf_op jit(solution)/shard_map/pallas_call | solution.py:234
  90.2 5.6 %shard_map.80 = (bf16[128,512]{1,0:T(8,128)(2,1)}, bf16[5,7,128,512]{3,2,1,0:T(8,128)(2,1)}) custom-call(s32[3]{0:T(128)} %pad_add_fusion.p_ref, bf16[4,128,512]{2,1,0:T(8,128)(2,1)} %bitcast.54, bf16[128,512]{1,0:T(8,128)(2,1)} %copy-done.1, f32[4,4,128,512]{3,2,1,0:T(8,128)} %get-tuple-element.70.z_ref, ...), custom_call_target="tpu_custom_call", output_to_operand_aliasing={{1}: (6, {})} | custom-call | flops 282591232 | bytes 4194304 | tf_op jit(solution)/shard_map/pallas_call | solution.py:220
  95.8 15.1 %shard_map.81 = (bf16[32,80,512]{2,1,0:T(8,128)(2,1)}, bf16[4,128,512]{2,1,0:T(8,128)(2,1)}) custom-call(s32[1]{0:T(128)} %bitcast.p_ref, bf16[5,7,128,512]{3,2,1,0:T(8,128)(2,1)} %get-tuple-element.72.h_ref, bf16[4,512,512]{2,1,0:T(8,128)(2,1)} %bitcast.46, bf16[4,512,512]{2,1,0:T(8,128)(2,1)} %bitcast.47, f32[4,512,512]{2,1,0:T(8,128)} %bitcast.30, ...), custom_call_target="tpu_custom_call" | custom-call | tf_op jit(solution)/shard_map/pallas_call | solution.py:256
  110.9 42.2 %all_to_all.5 = bf16[32,80,512]{2,1,0:T(8,128)(2,1)S(1)} all-to-all(bf16[32,80,512]{2,1,0:T(8,128)(2,1)} %get-tuple-element.76), channel_id=1, replica_groups=mesh['section'=4,'dp'=32] {'dp'}, dimensions={0} | all-to-all | bytes 5242880 | tf_op jit(solution)/shard_map/all_to_all | solution.py:266
  154.1 0.7 reshape.38
  (29 shorter events, 10.1 us)
Async XLA Ops:
  13.5 7.9 %collective-permute-start = (bf16[128,512]{1,0:T(8,128)(2,1)}, bf16[128,512]{1,0:T(8,128)(2,1)S(1)}, u32[]{:S(2)}, u32[]{:S(2)}) collective-permute-start(bf16[128,512]{1,0:T(8,128)(2,1)} %get-tuple-element.42), channel_id=1, source_target_pairs={{32,0},{64,32},{96,64},{33,1},{65,33},{97,65},{34,2},{66,34},{98,6... | collective-permute-start | bytes 393224 | tf_op jit(solution)/shard_map/ppermute | solution.py:16
  21.5 0.7 copy-start
  27.7 7.6 %collective-permute-start.1 = (bf16[128,512]{1,0:T(8,128)(2,1)}, bf16[128,512]{1,0:T(8,128)(2,1)S(1)}, u32[]{:S(2)}, u32[]{:S(2)}) collective-permute-start(bf16[128,512]{1,0:T(8,128)(2,1)} %get-tuple-element.47), channel_id=1, source_target_pairs={{32,0},{64,32},{96,64},{33,1},{65,33},{97,65},{34,2},{66,34},{98,6... | collective-permute-start | bytes 393224 | tf_op jit(solution)/shard_map/ppermute | solution.py:16
  35.3 0.7 copy-start.2
  41.6 7.6 %collective-permute-start.2 = (bf16[128,512]{1,0:T(8,128)(2,1)}, bf16[128,512]{1,0:T(8,128)(2,1)S(1)}, u32[]{:S(2)}, u32[]{:S(2)}) collective-permute-start(bf16[128,512]{1,0:T(8,128)(2,1)} %get-tuple-element.52), channel_id=1, source_target_pairs={{32,0},{64,32},{96,64},{33,1},{65,33},{97,65},{34,2},{66,34},{98,6... | collective-permute-start | bytes 393224 | tf_op jit(solution)/shard_map/ppermute | solution.py:16
  49.2 0.7 copy-start.3
  55.5 7.2 %collective-permute-start.3 = (bf16[128,512]{1,0:T(8,128)(2,1)}, bf16[128,512]{1,0:T(8,128)(2,1)S(1)}, u32[]{:S(2)}, u32[]{:S(2)}) collective-permute-start(bf16[128,512]{1,0:T(8,128)(2,1)} %get-tuple-element.57), channel_id=1, source_target_pairs={{32,0},{64,32},{96,64},{33,1},{65,33},{97,65},{34,2},{66,34},{98,6... | collective-permute-start | bytes 393224 | tf_op jit(solution)/shard_map/ppermute | solution.py:16
  62.7 0.7 copy-start.4
  68.9 7.2 %collective-permute-start.4 = (bf16[128,512]{1,0:T(8,128)(2,1)}, bf16[128,512]{1,0:T(8,128)(2,1)S(1)}, u32[]{:S(2)}, u32[]{:S(2)}) collective-permute-start(bf16[128,512]{1,0:T(8,128)(2,1)} %get-tuple-element.62), channel_id=1, source_target_pairs={{32,0},{64,32},{96,64},{33,1},{65,33},{97,65},{34,2},{66,34},{98,6... | collective-permute-start | bytes 393224 | tf_op jit(solution)/shard_map/ppermute | solution.py:16
  76.1 0.7 copy-start.5
  82.3 7.3 %collective-permute-start.5 = (bf16[128,512]{1,0:T(8,128)(2,1)}, bf16[128,512]{1,0:T(8,128)(2,1)S(1)}, u32[]{:S(2)}, u32[]{:S(2)}) collective-permute-start(bf16[128,512]{1,0:T(8,128)(2,1)} %get-tuple-element.67), channel_id=1, source_target_pairs={{32,0},{64,32},{96,64},{33,1},{65,33},{97,65},{34,2},{66,34},{98,6... | collective-permute-start | bytes 393224 | tf_op jit(solution)/shard_map/ppermute | solution.py:16
  89.6 0.7 copy-start.1

commit v2 on v1

--- a/solution.py
+++ b/solution.py
@@ -22,11 +22,20 @@
     return x if amount == 0 else pltpu.roll(x, amount, 0)
 
 
-def tap_mask(shape, di, dj, height, width):
+def edge_masks(shape, height, width):
     r = lax.broadcasted_iota(jnp.int32, shape, 0)
-    j = lax.rem(r, width)
-    i = lax.rem(lax.div(r, width), height)
-    return (i + di >= 0) & (i + di < height) & (j + dj >= 0) & (j + dj < width)
+    if width & (width - 1) == 0 and height & (height - 1) == 0:
+        j = r & (width - 1)
+        i = lax.shift_right_logical(r, width.bit_length() - 1) & (height - 1)
+    else:
+        j = lax.rem(r, width)
+        i = lax.rem(lax.div(r, width), height)
+    return {
+        ("i", -1): i >= 1,
+        ("i", 1): i < height - 1,
+        ("j", -1): j >= 1,
+        ("j", 1): j < width - 1,
+    }
 
 
 def offsets():
@@ -35,12 +44,20 @@
             yield 3 * (di + 1) + (dj + 1), di, dj
 
 
-def stencil(x, k_ref, layer, height, width, sign):
+def shifted_taps(x, masks, width, sign):
+    cols = {}
+    for dj in (-1, 0, 1):
+        s = sign * dj
+        cols[dj] = x if s == 0 else jnp.where(masks[("j", s)], shift_rows(x, s), 0.0)
+    for tap, di, dj in offsets():
+        s = sign * di
+        c = cols[dj]
+        yield tap, (c if s == 0 else jnp.where(masks[("i", s)], shift_rows(c, s * width), 0.0))
+
+
+def stencil(x, k_ref, layer, masks, width, sign):
     total = jnp.zeros(x.shape, jnp.float32)
-    for tap, di, dj in offsets():
-        di_s, dj_s = sign * di, sign * dj
-        moved = shift_rows(x, di_s * width + dj_s)
-        moved = jnp.where(tap_mask(x.shape, di_s, dj_s, height, width), moved, 0.0)
+    for tap, moved in shifted_taps(x, masks, width, sign):
         total = total + k_ref[layer, tap : tap + 1, :] * moved
     return total
 
@@ -49,10 +66,11 @@
     z_ref, a_ref, xs_ref = refs[-3:]
     layers = w_ref.shape[0]
     field = x_ref[...]
+    masks = edge_masks(field.shape, height, width)
     for layer in range(layers):
         xs_ref[layer] = field
         xf = field.astype(jnp.float32)
-        zed = stencil(xf, k_ref, layer, height, width, 1)
+        zed = stencil(xf, k_ref, layer, masks, width, 1)
         z_ref[layer] = zed
         act = (zed * jax.nn.sigmoid(zed)).astype(jnp.bfloat16)
         a_ref[layer] = act
@@ -73,6 +91,7 @@
     g = jnp.where(p_ref[1] == 1, top, car)
     g = jnp.where(p_ref[2] == 1, g, 0.0).astype(jnp.bfloat16)
     h_ref[layers] = g
+    masks = edge_masks(g.shape, height, width)
     for layer in reversed(range(layers)):
         back = lax.dot_general(
             g, w_ref[layer], (((1,), (1,)), ((), ())), preferred_element_type=jnp.float32
@@ -80,7 +99,7 @@
         zed = z_ref[layer]
         sig = jax.nn.sigmoid(zed)
         dzed = back * sig * (1.0 + zed * (1.0 - sig))
-        g = (g.astype(jnp.float32) + stencil(dzed, k_ref, layer, height, width, -1)).astype(
+        g = (g.astype(jnp.float32) + stencil(dzed, k_ref, layer, masks, width, -1)).astype(
             jnp.bfloat16
         )
         h_ref[layer] = g
@@ -101,6 +120,7 @@
     for m in range(batches):
         res_ref[m] = h_ref[0, first + m]
     depth = []
+    masks = edge_masks((batches * rows, chans), height, width)
     for layer in range(layers):
         g = h_ref[layer + 1, pl.ds(first, batches)].reshape(batches * rows, chans)
         back = lax.dot_general(
@@ -119,9 +139,7 @@
             ].astype(jnp.bfloat16)
         xf = xs_ref[layer].astype(jnp.float32)
         rows_out = []
-        for tap, di, dj in offsets():
-            moved = shift_rows(xf, di * width + dj)
-            moved = jnp.where(tap_mask(xf.shape, di, dj, height, width), moved, 0.0)
+        for tap, moved in shifted_taps(xf, masks, width, 1):
             rows_out.append(jnp.sum(moved * dzed, axis=0, keepdims=True))
         rows_out.append(jnp.zeros((pad_taps - taps, chans), jnp.float32))
         depth.append(jnp.concatenate(rows_out, axis=0) * scale)

time: 156 us -> 152 us (0.974)
  Pallas kernels: 85.9 us -> 80.4 us
    pallas_call x6, Pallas kernels: 27.2 us -> 25.2 us  [body(): pl.pallas_call(functools.partial(fwd_kernel, height=height, width=width),...]
    pallas_call x1, Pallas kernels: 15.1 us -> 13.1 us  [body(): pl.pallas_call(functools.partial(grad_kernel, height=height, width=width,...]
  transfers between devices with their start and end apart: 6 -> 6, of which waited for: 0 -> 0; matrix products, arithmetic and copies ran while one was open for 2% -> 3% of each run, Pallas kernels for 18% -> 17%
where the time goes in v2:
time: 152 us; the launch traced here: 150 us
  Pallas kernels  80.4 us (53%)
  blocking collectives  42.2 us (28%)
  starting transfers between devices  14.4 us (9%)
  other arithmetic  6.28 us (4%)
  local copies, waits for them, and re-layouts  5.95 us (4%)
    all_to_all x1, blocking collectives, body(): recv = lax.all_to_all(send, 'dp', 0, 0, tiled=True)  42.2 us
    pallas_call x7, Pallas kernels, body(): pl.pallas_call(functools.partial(step_kernel, height=height, width=width)...  37.8 us
    pallas_call x6, Pallas kernels, body(): pl.pallas_call(functools.partial(fwd_kernel, height=height, width=width),...  25.2 us
    ppermute x6, starting transfers between devices, from_behind(): return lax.ppermute(shard, axis, pairs)  14.4 us
    pallas_call x1, Pallas kernels, body(): pl.pallas_call(functools.partial(grad_kernel, height=height, width=width,...  13.1 us
    another operation x7, other arithmetic, body(): scalars = jnp.stack([picked, is_last, valid]).astype(jnp.int32)  4.47 us
    pallas_call x1, Pallas kernels, body(): pl.pallas_call(functools.partial(fwd_first_kernel, height=height, width=w...  4.22 us
    unnamed x12, local copies, waits for them, and re-layouts  3.93 us
  transfers between devices with their start and end apart: 6, of which 0 were waited for; matrix products, arithmetic and copies ran while one was open for 3% of the time, Pallas kernels for 17%

profile of v2, /device:TPU:6, one launch (start us, length us, event | category | flops | bytes accessed | tf_op | source)
XLA Modules:
  0.0 150.0 jit_solution(1752065942002853533)
XLA Ops:
  0.6 1.4 bitcast_convert_fusion.k_ref
  2.7 4.2 %shard_map.67 = (f32[4,4,128,512]{3,2,1,0:T(8,128)}, bf16[4,4,128,512]{3,2,1,0:T(8,128)(2,1)}, bf16[4,4,128,512]{3,2,1,0:T(8,128)(2,1)}, bf16[5,7,128,512]{3,2,1,0:T(8,128)(2,1)}) custom-call(s32[1]{0:T(128)} %bitcast.15.p_ref, bf16[4,128,512]{2,1,0:T(8,128)(2,1)} %bitcast.55, bf16[4,512,512]{2,1,0:T(8,128)(2,1)} %bitcast.31, ...), custom_call_target="tpu_custom_call" | custom-call | flops 282591232 | bytes 4194304 | tf_op jit(solution)/shard_map/pallas_call | solution.py:201
  7.6 5.4 %shard_map.68 = (bf16[128,512]{1,0:T(8,128)(2,1)}, bf16[5,7,128,512]{3,2,1,0:T(8,128)(2,1)}) custom-call(s32[3]{0:T(128)} %pad_add_fusion.6.p_ref, bf16[4,128,512]{2,1,0:T(8,128)(2,1)} %bitcast.48, bf16[128,512]{1,0:T(8,128)(2,1)} %broadcast_in_dim.6.car_ref, f32[4,4,128,512]{3,2,1,0:T(8,128)} %get-tuple-element.40.z_ref.refs_0_, ...), custom_call_target="tpu_custom_call", output_to_operand_aliasing={{1}: (6, {})} | custom-call | flops 282591232 | bytes 4194304 | tf_op jit(solution)/shard_map/pallas_call | solution.py:238
  13.0 2.7 %collective-permute-start = (bf16[128,512]{1,0:T(8,128)(2,1)}, bf16[128,512]{1,0:T(8,128)(2,1)S(1)}, u32[]{:S(2)}, u32[]{:S(2)}) collective-permute-start(bf16[128,512]{1,0:T(8,128)(2,1)} %get-tuple-element.42), channel_id=1, source_target_pairs={{32,0},{64,32},{96,64},{33,1},{65,33},{97,65},{34,2},{66,34},{98,6... | collective-permute-start | bytes 393224 | tf_op jit(solution)/shard_map/ppermute | solution.py:16
  15.8 4.2 %shard_map.69 = (f32[4,4,128,512]{3,2,1,0:T(8,128)}, bf16[4,4,128,512]{3,2,1,0:T(8,128)(2,1)}, bf16[4,4,128,512]{3,2,1,0:T(8,128)(2,1)}) custom-call(s32[1]{0:T(128)} %bitcast.13.p_ref, bf16[4,128,512]{2,1,0:T(8,128)(2,1)} %bitcast.56, bf16[4,512,512]{2,1,0:T(8,128)(2,1)} %bitcast.33, ...), custom_call_target="tpu_custom_call", output_to_operand_aliasing={{0}: (4, {}), {1}: (5, {}), {2}: (6, {})} | custom-call | flops 282591232 | bytes 4194304 | tf_op jit(solution)/shard_map/pallas_call | solution.py:252
  21.3 5.4 %shard_map.70 = (bf16[128,512]{1,0:T(8,128)(2,1)}, bf16[5,7,128,512]{3,2,1,0:T(8,128)(2,1)}) custom-call(s32[3]{0:T(128)} %pad_add_fusion.5.p_ref, bf16[4,128,512]{2,1,0:T(8,128)(2,1)} %bitcast.49, bf16[128,512]{1,0:T(8,128)(2,1)} %copy-done, f32[4,4,128,512]{3,2,1,0:T(8,128)} %get-tuple-element.45.z_ref.refs_0_, ...), custom_call_target="tpu_custom_call", output_to_operand_aliasing={{1}: (6, {})} | custom-call | flops 282591232 | bytes 4194304 | tf_op jit(solution)/shard_map/pallas_call | solution.py:238
  26.7 2.5 %collective-permute-start.1 = (bf16[128,512]{1,0:T(8,128)(2,1)}, bf16[128,512]{1,0:T(8,128)(2,1)S(1)}, u32[]{:S(2)}, u32[]{:S(2)}) collective-permute-start(bf16[128,512]{1,0:T(8,128)(2,1)} %get-tuple-element.47), channel_id=1, source_target_pairs={{32,0},{64,32},{96,64},{33,1},{65,33},{97,65},{34,2},{66,34},{98,6... | collective-permute-start | bytes 393224 | tf_op jit(solution)/shard_map/ppermute | solution.py:16
  29.8 4.2 %shard_map.71 = (f32[4,4,128,512]{3,2,1,0:T(8,128)}, bf16[4,4,128,512]{3,2,1,0:T(8,128)(2,1)}, bf16[4,4,128,512]{3,2,1,0:T(8,128)(2,1)}) custom-call(s32[1]{0:T(128)} %bitcast.11.p_ref, bf16[4,128,512]{2,1,0:T(8,128)(2,1)} %bitcast.57, bf16[4,512,512]{2,1,0:T(8,128)(2,1)} %bitcast.35, ...), custom_call_target="tpu_custom_call", output_to_operand_aliasing={{0}: (4, {}), {1}: (5, {}), {2}: (6, {})} | custom-call | flops 282591232 | bytes 4194304 | tf_op jit(solution)/shard_map/pallas_call | solution.py:252
  34.7 5.4 %shard_map.72 = (bf16[128,512]{1,0:T(8,128)(2,1)}, bf16[5,7,128,512]{3,2,1,0:T(8,128)(2,1)}) custom-call(s32[3]{0:T(128)} %pad_add_fusion.4.p_ref, bf16[4,128,512]{2,1,0:T(8,128)(2,1)} %bitcast.50, bf16[128,512]{1,0:T(8,128)(2,1)} %copy-done.2, f32[4,4,128,512]{3,2,1,0:T(8,128)} %get-tuple-element.50.z_ref.refs_0_, ...), custom_call_target="tpu_custom_call", output_to_operand_aliasing={{1}: (6, {})} | custom-call | flops 282591232 | bytes 4194304 | tf_op jit(solution)/shard_map/pallas_call | solution.py:238
  40.1 2.4 %collective-permute-start.2 = (bf16[128,512]{1,0:T(8,128)(2,1)}, bf16[128,512]{1,0:T(8,128)(2,1)S(1)}, u32[]{:S(2)}, u32[]{:S(2)}) collective-permute-start(bf16[128,512]{1,0:T(8,128)(2,1)} %get-tuple-element.52), channel_id=1, source_target_pairs={{32,0},{64,32},{96,64},{33,1},{65,33},{97,65},{34,2},{66,34},{98,6... | collective-permute-start | bytes 393224 | tf_op jit(solution)/shard_map/ppermute | solution.py:16
  43.1 4.2 %shard_map.73 = (f32[4,4,128,512]{3,2,1,0:T(8,128)}, bf16[4,4,128,512]{3,2,1,0:T(8,128)(2,1)}, bf16[4,4,128,512]{3,2,1,0:T(8,128)(2,1)}) custom-call(s32[1]{0:T(128)} %bitcast.9.p_ref, bf16[4,128,512]{2,1,0:T(8,128)(2,1)} %bitcast.58, bf16[4,512,512]{2,1,0:T(8,128)(2,1)} %bitcast.37, ...), custom_call_target="tpu_custom_call", output_to_operand_aliasing={{0}: (4, {}), {1}: (5, {}), {2}: (6, {})} | custom-call | flops 282591232 | bytes 4194304 | tf_op jit(solution)/shard_map/pallas_call | solution.py:252
  48.0 5.4 %shard_map.74 = (bf16[128,512]{1,0:T(8,128)(2,1)}, bf16[5,7,128,512]{3,2,1,0:T(8,128)(2,1)}) custom-call(s32[3]{0:T(128)} %pad_add_fusion.3.p_ref, bf16[4,128,512]{2,1,0:T(8,128)(2,1)} %bitcast.51, bf16[128,512]{1,0:T(8,128)(2,1)} %copy-done.3, f32[4,4,128,512]{3,2,1,0:T(8,128)} %get-tuple-element.55.z_ref.refs_0_, ...), custom_call_target="tpu_custom_call", output_to_operand_aliasing={{1}: (6, {})} | custom-call | flops 282591232 | bytes 4194304 | tf_op jit(solution)/shard_map/pallas_call | solution.py:238
  53.4 2.4 %collective-permute-start.3 = (bf16[128,512]{1,0:T(8,128)(2,1)}, bf16[128,512]{1,0:T(8,128)(2,1)S(1)}, u32[]{:S(2)}, u32[]{:S(2)}) collective-permute-start(bf16[128,512]{1,0:T(8,128)(2,1)} %get-tuple-element.57), channel_id=1, source_target_pairs={{32,0},{64,32},{96,64},{33,1},{65,33},{97,65},{34,2},{66,34},{98,6... | collective-permute-start | bytes 393224 | tf_op jit(solution)/shard_map/ppermute | solution.py:16
  56.5 4.2 %shard_map.75 = (f32[4,4,128,512]{3,2,1,0:T(8,128)}, bf16[4,4,128,512]{3,2,1,0:T(8,128)(2,1)}, bf16[4,4,128,512]{3,2,1,0:T(8,128)(2,1)}) custom-call(s32[1]{0:T(128)} %bitcast.7.p_ref, bf16[4,128,512]{2,1,0:T(8,128)(2,1)} %bitcast.59, bf16[4,512,512]{2,1,0:T(8,128)(2,1)} %bitcast.39, ...), custom_call_target="tpu_custom_call", output_to_operand_aliasing={{0}: (4, {}), {1}: (5, {}), {2}: (6, {})} | custom-call | flops 282591232 | bytes 4194304 | tf_op jit(solution)/shard_map/pallas_call | solution.py:252
  61.3 5.4 %shard_map.76 = (bf16[128,512]{1,0:T(8,128)(2,1)}, bf16[5,7,128,512]{3,2,1,0:T(8,128)(2,1)}) custom-call(s32[3]{0:T(128)} %pad_add_fusion.2.p_ref, bf16[4,128,512]{2,1,0:T(8,128)(2,1)} %bitcast.52, bf16[128,512]{1,0:T(8,128)(2,1)} %copy-done.4, f32[4,4,128,512]{3,2,1,0:T(8,128)} %get-tuple-element.60.z_ref.refs_0_, ...), custom_call_target="tpu_custom_call", output_to_operand_aliasing={{1}: (6, {})} | custom-call | flops 282591232 | bytes 4194304 | tf_op jit(solution)/shard_map/pallas_call | solution.py:238
  66.7 2.2 %collective-permute-start.4 = (bf16[128,512]{1,0:T(8,128)(2,1)}, bf16[128,512]{1,0:T(8,128)(2,1)S(1)}, u32[]{:S(2)}, u32[]{:S(2)}) collective-permute-start(bf16[128,512]{1,0:T(8,128)(2,1)} %get-tuple-element.62), channel_id=1, source_target_pairs={{32,0},{64,32},{96,64},{33,1},{65,33},{97,65},{34,2},{66,34},{98,6... | collective-permute-start | bytes 393224 | tf_op jit(solution)/shard_map/ppermute | solution.py:16
  69.6 4.2 %shard_map.77 = (f32[4,4,128,512]{3,2,1,0:T(8,128)}, bf16[4,4,128,512]{3,2,1,0:T(8,128)(2,1)}, bf16[4,4,128,512]{3,2,1,0:T(8,128)(2,1)}) custom-call(s32[1]{0:T(128)} %bitcast.5.p_ref, bf16[4,128,512]{2,1,0:T(8,128)(2,1)} %bitcast.60, bf16[4,512,512]{2,1,0:T(8,128)(2,1)} %bitcast.41, ...), custom_call_target="tpu_custom_call", output_to_operand_aliasing={{0}: (4, {}), {1}: (5, {}), {2}: (6, {})} | custom-call | flops 282591232 | bytes 4194304 | tf_op jit(solution)/shard_map/pallas_call | solution.py:252
  74.5 5.4 %shard_map.78 = (bf16[128,512]{1,0:T(8,128)(2,1)}, bf16[5,7,128,512]{3,2,1,0:T(8,128)(2,1)}) custom-call(s32[3]{0:T(128)} %pad_add_fusion.1.p_ref, bf16[4,128,512]{2,1,0:T(8,128)(2,1)} %bitcast.53, bf16[128,512]{1,0:T(8,128)(2,1)} %copy-done.5, f32[4,4,128,512]{3,2,1,0:T(8,128)} %get-tuple-element.65.z_ref.refs_0_, ...), custom_call_target="tpu_custom_call", output_to_operand_aliasing={{1}: (6, {})} | custom-call | flops 282591232 | bytes 4194304 | tf_op jit(solution)/shard_map/pallas_call | solution.py:238
  79.9 2.2 %collective-permute-start.5 = (bf16[128,512]{1,0:T(8,128)(2,1)}, bf16[128,512]{1,0:T(8,128)(2,1)S(1)}, u32[]{:S(2)}, u32[]{:S(2)}) collective-permute-start(bf16[128,512]{1,0:T(8,128)(2,1)} %get-tuple-element.67), channel_id=1, source_target_pairs={{32,0},{64,32},{96,64},{33,1},{65,33},{97,65},{34,2},{66,34},{98,6... | collective-permute-start | bytes 393224 | tf_op jit(solution)/shard_map/ppermute | solution.py:16
  82.6 4.2 %shard_map.79 = (f32[4,4,128,512]{3,2,1,0:T(8,128)}, bf16[4,4,128,512]{3,2,1,0:T(8,128)(2,1)}, bf16[4,4,128,512]{3,2,1,0:T(8,128)(2,1)}) custom-call(s32[1]{0:T(128)} %bitcast.1.p_ref, bf16[4,128,512]{2,1,0:T(8,128)(2,1)} %bitcast.61, bf16[4,512,512]{2,1,0:T(8,128)(2,1)} %bitcast.43, ...), custom_call_target="tpu_custom_call", output_to_operand_aliasing={{0}: (4, {}), {1}: (5, {}), {2}: (6, {})} | custom-call | flops 282591232 | bytes 4194304 | tf_op jit(solution)/shard_map/pallas_call | solution.py:252
  87.5 5.4 %shard_map.80 = (bf16[128,512]{1,0:T(8,128)(2,1)}, bf16[5,7,128,512]{3,2,1,0:T(8,128)(2,1)}) custom-call(s32[3]{0:T(128)} %pad_add_fusion.p_ref, bf16[4,128,512]{2,1,0:T(8,128)(2,1)} %bitcast.54, bf16[128,512]{1,0:T(8,128)(2,1)} %copy-done.1, f32[4,4,128,512]{3,2,1,0:T(8,128)} %get-tuple-element.70.z_ref, ...), custom_call_target="tpu_custom_call", output_to_operand_aliasing={{1}: (6, {})} | custom-call | flops 282591232 | bytes 4194304 | tf_op jit(solution)/shard_map/pallas_call | solution.py:238
  92.9 13.1 %shard_map.81 = (bf16[32,80,512]{2,1,0:T(8,128)(2,1)}, bf16[4,128,512]{2,1,0:T(8,128)(2,1)}) custom-call(s32[1]{0:T(128)} %bitcast.p_ref, bf16[5,7,128,512]{3,2,1,0:T(8,128)(2,1)} %get-tuple-element.72.h_ref, bf16[4,512,512]{2,1,0:T(8,128)(2,1)} %bitcast.46, bf16[4,512,512]{2,1,0:T(8,128)(2,1)} %bitcast.47, f32[4,512,512]{2,1,0:T(8,128)} %bitcast.30, ...), custom_call_target="tpu_custom_call" | custom-call | tf_op jit(solution)/shard_map/pallas_call | solution.py:274
  106.1 42.2 %all_to_all.5 = bf16[32,80,512]{2,1,0:T(8,128)(2,1)S(1)} all-to-all(bf16[32,80,512]{2,1,0:T(8,128)(2,1)} %get-tuple-element.76), channel_id=1, replica_groups=mesh['section'=4,'dp'=32] {'dp'}, dimensions={0} | all-to-all | bytes 5242880 | tf_op jit(solution)/shard_map/all_to_all | solution.py:284
  149.3 0.7 reshape.38
  (29 shorter events, 10.1 us)
Async XLA Ops:
  13.0 7.6 %collective-permute-start = (bf16[128,512]{1,0:T(8,128)(2,1)}, bf16[128,512]{1,0:T(8,128)(2,1)S(1)}, u32[]{:S(2)}, u32[]{:S(2)}) collective-permute-start(bf16[128,512]{1,0:T(8,128)(2,1)} %get-tuple-element.42), channel_id=1, source_target_pairs={{32,0},{64,32},{96,64},{33,1},{65,33},{97,65},{34,2},{66,34},{98,6... | collective-permute-start | bytes 393224 | tf_op jit(solution)/shard_map/ppermute | solution.py:16
  20.6 0.7 copy-start
  26.7 7.3 %collective-permute-start.1 = (bf16[128,512]{1,0:T(8,128)(2,1)}, bf16[128,512]{1,0:T(8,128)(2,1)S(1)}, u32[]{:S(2)}, u32[]{:S(2)}) collective-permute-start(bf16[128,512]{1,0:T(8,128)(2,1)} %get-tuple-element.47), channel_id=1, source_target_pairs={{32,0},{64,32},{96,64},{33,1},{65,33},{97,65},{34,2},{66,34},{98,6... | collective-permute-start | bytes 393224 | tf_op jit(solution)/shard_map/ppermute | solution.py:16
  34.0 0.7 copy-start.2
  40.1 7.2 %collective-permute-start.2 = (bf16[128,512]{1,0:T(8,128)(2,1)}, bf16[128,512]{1,0:T(8,128)(2,1)S(1)}, u32[]{:S(2)}, u32[]{:S(2)}) collective-permute-start(bf16[128,512]{1,0:T(8,128)(2,1)} %get-tuple-element.52), channel_id=1, source_target_pairs={{32,0},{64,32},{96,64},{33,1},{65,33},{97,65},{34,2},{66,34},{98,6... | collective-permute-start | bytes 393224 | tf_op jit(solution)/shard_map/ppermute | solution.py:16
  47.3 0.7 copy-start.3
  53.4 7.3 %collective-permute-start.3 = (bf16[128,512]{1,0:T(8,128)(2,1)}, bf16[128,512]{1,0:T(8,128)(2,1)S(1)}, u32[]{:S(2)}, u32[]{:S(2)}) collective-permute-start(bf16[128,512]{1,0:T(8,128)(2,1)} %get-tuple-element.57), channel_id=1, source_target_pairs={{32,0},{64,32},{96,64},{33,1},{65,33},{97,65},{34,2},{66,34},{98,6... | collective-permute-start | bytes 393224 | tf_op jit(solution)/shard_map/ppermute | solution.py:16
  60.7 0.7 copy-start.4
  66.7 7.1 %collective-permute-start.4 = (bf16[128,512]{1,0:T(8,128)(2,1)}, bf16[128,512]{1,0:T(8,128)(2,1)S(1)}, u32[]{:S(2)}, u32[]{:S(2)}) collective-permute-start(bf16[128,512]{1,0:T(8,128)(2,1)} %get-tuple-element.62), channel_id=1, source_target_pairs={{32,0},{64,32},{96,64},{33,1},{65,33},{97,65},{34,2},{66,34},{98,6... | collective-permute-start | bytes 393224 | tf_op jit(solution)/shard_map/ppermute | solution.py:16
  73.8 0.7 copy-start.5
  79.9 7.0 %collective-permute-start.5 = (bf16[128,512]{1,0:T(8,128)(2,1)}, bf16[128,512]{1,0:T(8,128)(2,1)S(1)}, u32[]{:S(2)}, u32[]{:S(2)}) collective-permute-start(bf16[128,512]{1,0:T(8,128)(2,1)} %get-tuple-element.67), channel_id=1, source_target_pairs={{32,0},{64,32},{96,64},{33,1},{65,33},{97,65},{34,2},{66,34},{98,6... | collective-permute-start | bytes 393224 | tf_op jit(solution)/shard_map/ppermute | solution.py:16
  86.9 0.7 copy-start.1

commit v3 on v2

--- a/solution.py
+++ b/solution.py
@@ -83,13 +83,15 @@
     fwd_kernel(p_ref, x_ref, w_ref, k_ref, z_ref, a_ref, xs_ref, height=height, width=width)
 
 
-def step_kernel(p_ref, top_ref, car_ref, z_ref, w_ref, k_ref, h_in, g_ref, h_ref, *, height, width):
+def step_kernel(
+    p_ref, top_ref, car_ref, z_ref, w_ref, k_ref, h_in, g_ref, h_ref, *, height, width, step
+):
     del h_in
     layers = w_ref.shape[0]
     top = top_ref[...].astype(jnp.float32)
     car = car_ref[...].astype(jnp.float32)
-    g = jnp.where(p_ref[1] == 1, top, car)
-    g = jnp.where(p_ref[2] == 1, g, 0.0).astype(jnp.bfloat16)
+    g = jnp.where(p_ref[step, 1] == 1, top, car)
+    g = jnp.where(p_ref[step, 2] == 1, g, 0.0).astype(jnp.bfloat16)
     h_ref[layers] = g
     masks = edge_masks(g.shape, height, width)
     for layer in reversed(range(layers)):
@@ -185,19 +187,26 @@
         jax.ShapeDtypeStruct((layers, batches, rows, chans), jnp.bfloat16),
         jax.ShapeDtypeStruct((layers, batches, rows, chans), jnp.bfloat16),
     )
-    slot_spec = pl.BlockSpec((layers, None, rows, chans), lambda i, p: (0, p[0], 0, 0))
-    fwd_in = [
-        pl.BlockSpec((None, rows, chans), lambda i, p: (p[0], 0, 0)),
-        pl.BlockSpec((layers, chans, chans), lambda i, p: (0, 0, 0)),
-        pl.BlockSpec((layers, taps, chans), lambda i, p: (0, 0, 0)),
-    ]
+
+    def slot_spec(step):
+        return pl.BlockSpec((layers, None, rows, chans), lambda i, p, s=step: (0, p[s, 0], 0, 0))
+
+    def fwd_in(step):
+        return [
+            pl.BlockSpec((None, rows, chans), lambda i, p, s=step: (p[s, 0], 0, 0)),
+            pl.BlockSpec((layers, chans, chans), lambda i, p: (0, 0, 0)),
+            pl.BlockSpec((layers, taps, chans), lambda i, p: (0, 0, 0)),
+        ]
 
     def picked_at(step):
         batch_id = step - (sections - 1) + my_section
         valid = ((batch_id >= 0) & (batch_id < batches)).astype(jnp.int32)
         return jnp.clip(batch_id, 0, batches - 1), valid
 
-    picked, _ = picked_at(0)
+    is_last = (my_section == sections - 1).astype(jnp.int32)
+    table = jnp.stack(
+        [jnp.stack([picked_at(s)[0], is_last, picked_at(s)[1]]) for s in range(total_steps)]
+    ).astype(jnp.int32)
     zbuf, abuf, xbuf, hbuf = pl.pallas_call(
         functools.partial(fwd_first_kernel, height=height, width=width),
         out_shape=buf_shapes
@@ -205,25 +214,22 @@
         grid_spec=pltpu.PrefetchScalarGridSpec(
             num_scalar_prefetch=1,
             grid=(1,),
-            in_specs=fwd_in,
-            out_specs=[slot_spec, slot_spec, slot_spec, pl.BlockSpec(memory_space=pl.ANY)],
+            in_specs=fwd_in(0),
+            out_specs=[slot_spec(0)] * 3 + [pl.BlockSpec(memory_space=pl.ANY)],
         ),
         compiler_params=params,
         cost_estimate=fwd_cost,
-    )(jnp.reshape(picked, (1,)).astype(jnp.int32), x_all, weights, kerns)
+    )(table, x_all, weights, kerns)
 
     carried = jnp.zeros((rows, chans), jnp.bfloat16)
-    is_last = (my_section == sections - 1).astype(jnp.int32)
     for step in range(total_steps):
-        picked, valid = picked_at(step)
-        scalars = jnp.stack([picked, is_last, valid]).astype(jnp.int32)
         grid_spec = pltpu.PrefetchScalarGridSpec(
             num_scalar_prefetch=1,
             grid=(1,),
             in_specs=[
-                pl.BlockSpec((None, rows, chans), lambda i, p: (p[0], 0, 0)),
-                pl.BlockSpec((rows, chans), lambda i, p: (0, 0)),
-                pl.BlockSpec((layers, None, rows, chans), lambda i, p: (0, p[0], 0, 0)),
+                pl.BlockSpec((None, rows, chans), lambda i, p, s=step: (p[s, 0], 0, 0)),
+                pl.BlockSpec(memory_space=pltpu.VMEM),
+                slot_spec(step),
                 pl.BlockSpec((layers, chans, chans), lambda i, p: (0, 0, 0)),
                 pl.BlockSpec((layers, taps, chans), lambda i, p: (0, 0, 0)),
                 pl.BlockSpec(memory_space=pl.ANY),
@@ -236,7 +242,7 @@
             ],
         )
         g, hbuf = pl.pallas_call(
-            functools.partial(step_kernel, height=height, width=width),
+            functools.partial(step_kernel, height=height, width=width, step=step),
             out_shape=(
                 jax.ShapeDtypeStruct((rows, chans), jnp.bfloat16),
                 jax.ShapeDtypeStruct(hbuf.shape, jnp.bfloat16),
@@ -245,23 +251,22 @@
             input_output_aliases={6: 1},
             compiler_params=params,
             cost_estimate=fwd_cost,
-        )(scalars, top_all, carried, zbuf, weights, kerns, hbuf)
+        )(table, top_all, carried, zbuf, weights, kerns, hbuf)
         if step < total_steps - 1:
             carried = from_behind(g, "section", -1)
-            nxt, _ = picked_at(step + 1)
             zbuf, abuf, xbuf = pl.pallas_call(
                 functools.partial(fwd_kernel, height=height, width=width),
                 out_shape=buf_shapes,
                 grid_spec=pltpu.PrefetchScalarGridSpec(
                     num_scalar_prefetch=1,
                     grid=(1,),
-                    in_specs=fwd_in + [pl.BlockSpec(memory_space=pl.ANY)] * 3,
-                    out_specs=[slot_spec, slot_spec, slot_spec],
+                    in_specs=fwd_in(step + 1) + [pl.BlockSpec(memory_space=pl.ANY)] * 3,
+                    out_specs=[slot_spec(step + 1)] * 3,
                 ),
                 input_output_aliases={4: 0, 5: 1, 6: 2},
                 compiler_params=params,
                 cost_estimate=fwd_cost,
-            )(jnp.reshape(nxt, (1,)).astype(jnp.int32), x_all, weights, kerns, zbuf, abuf, xbuf)
+            )(table, x_all, weights, kerns, zbuf, abuf, xbuf)
     zs = zbuf.reshape(layers, batches * rows, chans)
     acts = abuf.reshape(layers, batches * rows, chans)
     xs = xbuf.reshape(layers, batches * rows, chans)

time: 152 us -> 153 us (level)
  Pallas kernels: 80.4 us -> 85.5 us
  other arithmetic: 6.28 us -> 2.11 us
    pallas_call x6, Pallas kernels: 25.2 us -> 29.4 us  [body(): pl.pallas_call(functools.partial(fwd_kernel, height=height, width=width),...]
    another operation x7 -> x4, other arithmetic: 4.47 us -> 0.3 us  [body(): jnp.stack([jnp.stack([picked_at(s)[0], is_last, picked_at(s)[1]]) for s i...]
  transfers between devices with their start and end apart: 6 -> 6, of which waited for: 0 -> 0; matrix products, arithmetic and copies ran while one was open for 3% -> 0% of each run, Pallas kernels for 17% -> 19%
where the time goes in v3:
time: 153 us; the launch traced here: 151 us
  Pallas kernels  85.5 us (56%)
  blocking collectives  42.2 us (28%)
  starting transfers between devices  14.3 us (9%)
  local copies, waits for them, and re-layouts  6.57 us (4%)
  other arithmetic  2.11 us (1%)
    all_to_all x1, blocking collectives, body(): recv = lax.all_to_all(send, 'dp', 0, 0, tiled=True)  42.2 us
    pallas_call x7, Pallas kernels, body(): pl.pallas_call(functools.partial(step_kernel, height=height, width=width,...  38.1 us
    pallas_call x6, Pallas kernels, body(): pl.pallas_call(functools.partial(fwd_kernel, height=height, width=width),...  29.4 us
    ppermute x6, starting transfers between devices, from_behind(): return lax.ppermute(shard, axis, pairs)  14.3 us
    pallas_call x1, Pallas kernels, body(): pl.pallas_call(functools.partial(grad_kernel, height=height, width=width,...  13.1 us
    pallas_call x1, Pallas kernels, body(): pl.pallas_call(functools.partial(fwd_first_kernel, height=height, width=w...  4.9 us
    unnamed x12, local copies, waits for them, and re-layouts  3.93 us
  transfers between devices with their start and end apart: 6, of which 0 were waited for; matrix products, arithmetic and copies ran while one was open for 0% of the time, Pallas kernels for 19%

profile of v3, /device:TPU:6, one launch (start us, length us, event | category | flops | bytes accessed | tf_op | source)
XLA Modules:
  0.0 151.4 jit_solution(2264541903447067288)
XLA Ops:
  0.7 1.4 bitcast_convert_fusion.k_ref
  3.0 4.9 %shard_map.67 = (f32[4,4,128,512]{3,2,1,0:T(8,128)}, bf16[4,4,128,512]{3,2,1,0:T(8,128)(2,1)}, bf16[4,4,128,512]{3,2,1,0:T(8,128)(2,1)}, bf16[5,7,128,512]{3,2,1,0:T(8,128)(2,1)}) custom-call(s32[7,3]{1,0:T(8,128)} %stack.157.p_ref, bf16[4,128,512]{2,1,0:T(8,128)(2,1)} %bitcast.62, bf16[4,512,512]{2,1,0:T(8,128)(2,1)} %bitcast.45, ...), custom_call_target="tpu_custom_call" | custom-call | flops 282591232 | bytes 4194304 | tf_op jit(solution)/shard_map/pallas_call | solution.py:210
  8.6 5.4 %shard_map.68 = (bf16[128,512]{1,0:T(8,128)(2,1)}, bf16[5,7,128,512]{3,2,1,0:T(8,128)(2,1)}) custom-call(s32[7,3]{1,0:T(8,128)} %stack.157.p_ref, bf16[4,128,512]{2,1,0:T(8,128)(2,1)} %bitcast.69, bf16[128,512]{1,0:T(8,128)(2,1)} %broadcast_in_dim.6.car_ref, f32[4,4,128,512]{3,2,1,0:T(8,128)} %get-tuple-element.40.z_ref.refs_0_, ...), custom_call_target="tpu_custom_call", output_to_operand_aliasing={{1}: (6, {})} | custom-call | flops 282591232 | bytes 4194304 | tf_op jit(solution)/shard_map/pallas_call | solution.py:244
  14.0 2.7 %collective-permute-start = (bf16[128,512]{1,0:T(8,128)(2,1)}, bf16[128,512]{1,0:T(8,128)(2,1)S(1)}, u32[]{:S(2)}, u32[]{:S(2)}) collective-permute-start(bf16[128,512]{1,0:T(8,128)(2,1)} %get-tuple-element.42), channel_id=1, source_target_pairs={{32,0},{64,32},{96,64},{33,1},{65,33},{97,65},{34,2},{66,34},{98,6... | collective-permute-start | bytes 393224 | tf_op jit(solution)/shard_map/ppermute | solution.py:16
  16.8 4.9 %shard_map.69 = (f32[4,4,128,512]{3,2,1,0:T(8,128)}, bf16[4,4,128,512]{3,2,1,0:T(8,128)(2,1)}, bf16[4,4,128,512]{3,2,1,0:T(8,128)(2,1)}) custom-call(s32[7,3]{1,0:T(8,128)} %stack.157.p_ref, bf16[4,128,512]{2,1,0:T(8,128)(2,1)} %bitcast.63, bf16[4,512,512]{2,1,0:T(8,128)(2,1)} %bitcast.47, ...), custom_call_target="tpu_custom_call", output_to_operand_aliasing={{0}: (4, {}), {1}: (5, {}), {2}: (6, {})} | custom-call | flops 282591232 | bytes 4194304 | tf_op jit(solution)/shard_map/pallas_call | solution.py:257
  22.3 5.4 %shard_map.70 = (bf16[128,512]{1,0:T(8,128)(2,1)}, bf16[5,7,128,512]{3,2,1,0:T(8,128)(2,1)}) custom-call(s32[7,3]{1,0:T(8,128)} %stack.157.p_ref, bf16[4,128,512]{2,1,0:T(8,128)(2,1)} %bitcast.70, bf16[128,512]{1,0:T(8,128)(2,1)} %copy-done.1, f32[4,4,128,512]{3,2,1,0:T(8,128)} %get-tuple-element.45.z_ref.refs_0_, ...), custom_call_target="tpu_custom_call", output_to_operand_aliasing={{1}: (6, {})} | custom-call | flops 282591232 | bytes 4194304 | tf_op jit(solution)/shard_map/pallas_call | solution.py:244
  27.8 2.4 %collective-permute-start.1 = (bf16[128,512]{1,0:T(8,128)(2,1)}, bf16[128,512]{1,0:T(8,128)(2,1)S(1)}, u32[]{:S(2)}, u32[]{:S(2)}) collective-permute-start(bf16[128,512]{1,0:T(8,128)(2,1)} %get-tuple-element.47), channel_id=1, source_target_pairs={{32,0},{64,32},{96,64},{33,1},{65,33},{97,65},{34,2},{66,34},{98,6... | collective-permute-start | bytes 393224 | tf_op jit(solution)/shard_map/ppermute | solution.py:16
  30.2 4.9 %shard_map.71 = (f32[4,4,128,512]{3,2,1,0:T(8,128)}, bf16[4,4,128,512]{3,2,1,0:T(8,128)(2,1)}, bf16[4,4,128,512]{3,2,1,0:T(8,128)(2,1)}) custom-call(s32[7,3]{1,0:T(8,128)} %stack.157.p_ref, bf16[4,128,512]{2,1,0:T(8,128)(2,1)} %bitcast.64, bf16[4,512,512]{2,1,0:T(8,128)(2,1)} %bitcast.49, ...), custom_call_target="tpu_custom_call", output_to_operand_aliasing={{0}: (4, {}), {1}: (5, {}), {2}: (6, {})} | custom-call | flops 282591232 | bytes 4194304 | tf_op jit(solution)/shard_map/pallas_call | solution.py:257
  35.8 5.4 %shard_map.72 = (bf16[128,512]{1,0:T(8,128)(2,1)}, bf16[5,7,128,512]{3,2,1,0:T(8,128)(2,1)}) custom-call(s32[7,3]{1,0:T(8,128)} %stack.157.p_ref, bf16[4,128,512]{2,1,0:T(8,128)(2,1)} %bitcast.71, bf16[128,512]{1,0:T(8,128)(2,1)} %copy-done.2, f32[4,4,128,512]{3,2,1,0:T(8,128)} %get-tuple-element.50.z_ref.refs_0_, ...), custom_call_target="tpu_custom_call", output_to_operand_aliasing={{1}: (6, {})} | custom-call | flops 282591232 | bytes 4194304 | tf_op jit(solution)/shard_map/pallas_call | solution.py:244
  41.2 2.4 %collective-permute-start.2 = (bf16[128,512]{1,0:T(8,128)(2,1)}, bf16[128,512]{1,0:T(8,128)(2,1)S(1)}, u32[]{:S(2)}, u32[]{:S(2)}) collective-permute-start(bf16[128,512]{1,0:T(8,128)(2,1)} %get-tuple-element.52), channel_id=1, source_target_pairs={{32,0},{64,32},{96,64},{33,1},{65,33},{97,65},{34,2},{66,34},{98,6... | collective-permute-start | bytes 393224 | tf_op jit(solution)/shard_map/ppermute | solution.py:16
  43.6 4.9 %shard_map.73 = (f32[4,4,128,512]{3,2,1,0:T(8,128)}, bf16[4,4,128,512]{3,2,1,0:T(8,128)(2,1)}, bf16[4,4,128,512]{3,2,1,0:T(8,128)(2,1)}) custom-call(s32[7,3]{1,0:T(8,128)} %stack.157.p_ref, bf16[4,128,512]{2,1,0:T(8,128)(2,1)} %bitcast.65, bf16[4,512,512]{2,1,0:T(8,128)(2,1)} %bitcast.51, ...), custom_call_target="tpu_custom_call", output_to_operand_aliasing={{0}: (4, {}), {1}: (5, {}), {2}: (6, {})} | custom-call | flops 282591232 | bytes 4194304 | tf_op jit(solution)/shard_map/pallas_call | solution.py:257
  49.2 5.4 %shard_map.74 = (bf16[128,512]{1,0:T(8,128)(2,1)}, bf16[5,7,128,512]{3,2,1,0:T(8,128)(2,1)}) custom-call(s32[7,3]{1,0:T(8,128)} %stack.157.p_ref, bf16[4,128,512]{2,1,0:T(8,128)(2,1)} %bitcast.72, bf16[128,512]{1,0:T(8,128)(2,1)} %copy-done.3, f32[4,4,128,512]{3,2,1,0:T(8,128)} %get-tuple-element.55.z_ref.refs_0_, ...), custom_call_target="tpu_custom_call", output_to_operand_aliasing={{1}: (6, {})} | custom-call | flops 282591232 | bytes 4194304 | tf_op jit(solution)/shard_map/pallas_call | solution.py:244
  54.6 2.4 %collective-permute-start.3 = (bf16[128,512]{1,0:T(8,128)(2,1)}, bf16[128,512]{1,0:T(8,128)(2,1)S(1)}, u32[]{:S(2)}, u32[]{:S(2)}) collective-permute-start(bf16[128,512]{1,0:T(8,128)(2,1)} %get-tuple-element.57), channel_id=1, source_target_pairs={{32,0},{64,32},{96,64},{33,1},{65,33},{97,65},{34,2},{66,34},{98,6... | collective-permute-start | bytes 393224 | tf_op jit(solution)/shard_map/ppermute | solution.py:16
  57.0 4.9 %shard_map.75 = (f32[4,4,128,512]{3,2,1,0:T(8,128)}, bf16[4,4,128,512]{3,2,1,0:T(8,128)(2,1)}, bf16[4,4,128,512]{3,2,1,0:T(8,128)(2,1)}) custom-call(s32[7,3]{1,0:T(8,128)} %stack.157.p_ref, bf16[4,128,512]{2,1,0:T(8,128)(2,1)} %bitcast.66, bf16[4,512,512]{2,1,0:T(8,128)(2,1)} %bitcast.53, ...), custom_call_target="tpu_custom_call", output_to_operand_aliasing={{0}: (4, {}), {1}: (5, {}), {2}: (6, {})} | custom-call | flops 282591232 | bytes 4194304 | tf_op jit(solution)/shard_map/pallas_call | solution.py:257
  62.6 5.5 %shard_map.76 = (bf16[128,512]{1,0:T(8,128)(2,1)}, bf16[5,7,128,512]{3,2,1,0:T(8,128)(2,1)}) custom-call(s32[7,3]{1,0:T(8,128)} %stack.157.p_ref, bf16[4,128,512]{2,1,0:T(8,128)(2,1)} %bitcast.73, bf16[128,512]{1,0:T(8,128)(2,1)} %copy-done.4, f32[4,4,128,512]{3,2,1,0:T(8,128)} %get-tuple-element.60.z_ref.refs_0_, ...), custom_call_target="tpu_custom_call", output_to_operand_aliasing={{1}: (6, {})} | custom-call | flops 282591232 | bytes 4194304 | tf_op jit(solution)/shard_map/pallas_call | solution.py:244
  68.1 2.1 %collective-permute-start.4 = (bf16[128,512]{1,0:T(8,128)(2,1)}, bf16[128,512]{1,0:T(8,128)(2,1)S(1)}, u32[]{:S(2)}, u32[]{:S(2)}) collective-permute-start(bf16[128,512]{1,0:T(8,128)(2,1)} %get-tuple-element.62), channel_id=1, source_target_pairs={{32,0},{64,32},{96,64},{33,1},{65,33},{97,65},{34,2},{66,34},{98,6... | collective-permute-start | bytes 393224 | tf_op jit(solution)/shard_map/ppermute | solution.py:16
  70.2 4.9 %shard_map.77 = (f32[4,4,128,512]{3,2,1,0:T(8,128)}, bf16[4,4,128,512]{3,2,1,0:T(8,128)(2,1)}, bf16[4,4,128,512]{3,2,1,0:T(8,128)(2,1)}) custom-call(s32[7,3]{1,0:T(8,128)} %stack.157.p_ref, bf16[4,128,512]{2,1,0:T(8,128)(2,1)} %bitcast.67, bf16[4,512,512]{2,1,0:T(8,128)(2,1)} %bitcast.55, ...), custom_call_target="tpu_custom_call", output_to_operand_aliasing={{0}: (4, {}), {1}: (5, {}), {2}: (6, {})} | custom-call | flops 282591232 | bytes 4194304 | tf_op jit(solution)/shard_map/pallas_call | solution.py:257
  75.7 5.4 %shard_map.78 = (bf16[128,512]{1,0:T(8,128)(2,1)}, bf16[5,7,128,512]{3,2,1,0:T(8,128)(2,1)}) custom-call(s32[7,3]{1,0:T(8,128)} %stack.157.p_ref, bf16[4,128,512]{2,1,0:T(8,128)(2,1)} %bitcast.74, bf16[128,512]{1,0:T(8,128)(2,1)} %copy-done.5, f32[4,4,128,512]{3,2,1,0:T(8,128)} %get-tuple-element.65.z_ref.refs_0_, ...), custom_call_target="tpu_custom_call", output_to_operand_aliasing={{1}: (6, {})} | custom-call | flops 282591232 | bytes 4194304 | tf_op jit(solution)/shard_map/pallas_call | solution.py:244
  81.2 2.2 %collective-permute-start.5 = (bf16[128,512]{1,0:T(8,128)(2,1)}, bf16[128,512]{1,0:T(8,128)(2,1)S(1)}, u32[]{:S(2)}, u32[]{:S(2)}) collective-permute-start(bf16[128,512]{1,0:T(8,128)(2,1)} %get-tuple-element.67), channel_id=1, source_target_pairs={{32,0},{64,32},{96,64},{33,1},{65,33},{97,65},{34,2},{66,34},{98,6... | collective-permute-start | bytes 393224 | tf_op jit(solution)/shard_map/ppermute | solution.py:16
  83.3 4.9 %shard_map.79 = (f32[4,4,128,512]{3,2,1,0:T(8,128)}, bf16[4,4,128,512]{3,2,1,0:T(8,128)(2,1)}, bf16[4,4,128,512]{3,2,1,0:T(8,128)(2,1)}) custom-call(s32[7,3]{1,0:T(8,128)} %stack.157.p_ref, bf16[4,128,512]{2,1,0:T(8,128)(2,1)} %bitcast.68, bf16[4,512,512]{2,1,0:T(8,128)(2,1)} %bitcast.57, ...), custom_call_target="tpu_custom_call", output_to_operand_aliasing={{0}: (4, {}), {1}: (5, {}), {2}: (6, {})} | custom-call | flops 282591232 | bytes 4194304 | tf_op jit(solution)/shard_map/pallas_call | solution.py:257
  88.9 5.5 %shard_map.80 = (bf16[128,512]{1,0:T(8,128)(2,1)}, bf16[5,7,128,512]{3,2,1,0:T(8,128)(2,1)}) custom-call(s32[7,3]{1,0:T(8,128)} %stack.157.p_ref, bf16[4,128,512]{2,1,0:T(8,128)(2,1)} %bitcast.75, bf16[128,512]{1,0:T(8,128)(2,1)} %copy-done, f32[4,4,128,512]{3,2,1,0:T(8,128)} %get-tuple-element.70.z_ref, ...), custom_call_target="tpu_custom_call", output_to_operand_aliasing={{1}: (6, {})} | custom-call | flops 282591232 | bytes 4194304 | tf_op jit(solution)/shard_map/pallas_call | solution.py:244
  94.3 13.1 %shard_map.81 = (bf16[32,80,512]{2,1,0:T(8,128)(2,1)}, bf16[4,128,512]{2,1,0:T(8,128)(2,1)}) custom-call(s32[1]{0:T(128)} %bitcast.p_ref, bf16[5,7,128,512]{3,2,1,0:T(8,128)(2,1)} %get-tuple-element.72.h_ref, bf16[4,512,512]{2,1,0:T(8,128)(2,1)} %bitcast.60, bf16[4,512,512]{2,1,0:T(8,128)(2,1)} %bitcast.61, f32[4,512,512]{2,1,0:T(8,128)} %bitcast.44, ...), custom_call_target="tpu_custom_call" | custom-call | tf_op jit(solution)/shard_map/pallas_call | solution.py:279
  107.5 42.2 %all_to_all.5 = bf16[32,80,512]{2,1,0:T(8,128)(2,1)S(1)} all-to-all(bf16[32,80,512]{2,1,0:T(8,128)(2,1)} %get-tuple-element.76), channel_id=1, replica_groups=mesh['section'=4,'dp'=32] {'dp'}, dimensions={0} | all-to-all | bytes 5242880 | tf_op jit(solution)/shard_map/all_to_all | solution.py:289
  150.7 0.7 reshape.31
  (27 shorter events, 6.6 us)
Async XLA Ops:
  14.0 7.6 %collective-permute-start = (bf16[128,512]{1,0:T(8,128)(2,1)}, bf16[128,512]{1,0:T(8,128)(2,1)S(1)}, u32[]{:S(2)}, u32[]{:S(2)}) collective-permute-start(bf16[128,512]{1,0:T(8,128)(2,1)} %get-tuple-element.42), channel_id=1, source_target_pairs={{32,0},{64,32},{96,64},{33,1},{65,33},{97,65},{34,2},{66,34},{98,6... | collective-permute-start | bytes 393224 | tf_op jit(solution)/shard_map/ppermute | solution.py:16
  21.7 0.7 copy-start.1
  27.8 7.4 %collective-permute-start.1 = (bf16[128,512]{1,0:T(8,128)(2,1)}, bf16[128,512]{1,0:T(8,128)(2,1)S(1)}, u32[]{:S(2)}, u32[]{:S(2)}) collective-permute-start(bf16[128,512]{1,0:T(8,128)(2,1)} %get-tuple-element.47), channel_id=1, source_target_pairs={{32,0},{64,32},{96,64},{33,1},{65,33},{97,65},{34,2},{66,34},{98,6... | collective-permute-start | bytes 393224 | tf_op jit(solution)/shard_map/ppermute | solution.py:16
  35.1 0.7 copy-start.2
  41.2 7.3 %collective-permute-start.2 = (bf16[128,512]{1,0:T(8,128)(2,1)}, bf16[128,512]{1,0:T(8,128)(2,1)S(1)}, u32[]{:S(2)}, u32[]{:S(2)}) collective-permute-start(bf16[128,512]{1,0:T(8,128)(2,1)} %get-tuple-element.52), channel_id=1, source_target_pairs={{32,0},{64,32},{96,64},{33,1},{65,33},{97,65},{34,2},{66,34},{98,6... | collective-permute-start | bytes 393224 | tf_op jit(solution)/shard_map/ppermute | solution.py:16
  48.5 0.7 copy-start.3
  54.6 7.3 %collective-permute-start.3 = (bf16[128,512]{1,0:T(8,128)(2,1)}, bf16[128,512]{1,0:T(8,128)(2,1)S(1)}, u32[]{:S(2)}, u32[]{:S(2)}) collective-permute-start(bf16[128,512]{1,0:T(8,128)(2,1)} %get-tuple-element.57), channel_id=1, source_target_pairs={{32,0},{64,32},{96,64},{33,1},{65,33},{97,65},{34,2},{66,34},{98,6... | collective-permute-start | bytes 393224 | tf_op jit(solution)/shard_map/ppermute | solution.py:16
  61.9 0.7 copy-start.4
  68.1 7.0 %collective-permute-start.4 = (bf16[128,512]{1,0:T(8,128)(2,1)}, bf16[128,512]{1,0:T(8,128)(2,1)S(1)}, u32[]{:S(2)}, u32[]{:S(2)}) collective-permute-start(bf16[128,512]{1,0:T(8,128)(2,1)} %get-tuple-element.62), channel_id=1, source_target_pairs={{32,0},{64,32},{96,64},{33,1},{65,33},{97,65},{34,2},{66,34},{98,6... | collective-permute-start | bytes 393224 | tf_op jit(solution)/shard_map/ppermute | solution.py:16
  75.1 0.7 copy-start.5
  81.2 7.1 %collective-permute-start.5 = (bf16[128,512]{1,0:T(8,128)(2,1)}, bf16[128,512]{1,0:T(8,128)(2,1)S(1)}, u32[]{:S(2)}, u32[]{:S(2)}) collective-permute-start(bf16[128,512]{1,0:T(8,128)(2,1)} %get-tuple-element.67), channel_id=1, source_target_pairs={{32,0},{64,32},{96,64},{33,1},{65,33},{97,65},{34,2},{66,34},{98,6... | collective-permute-start | bytes 393224 | tf_op jit(solution)/shard_map/ppermute | solution.py:16
  88.2 0.7 copy-start

commit v4 on v2

--- a/solution.py
+++ b/solution.py
@@ -5,7 +5,7 @@
 from jax import lax
 from jax.experimental import pallas as pl
 from jax.experimental.pallas import tpu as pltpu
-from jax.sharding import PartitionSpec as P
+from jax.sharding import Mesh, PartitionSpec as P
 
 VMEM_LIMIT = 60 * 1024 * 1024
 
@@ -156,7 +156,7 @@
 
 def body(section_inputs, grad_out, point_weights, depth_weights):
     sections = lax.axis_size("section")
-    replicas = lax.axis_size("dp")
+    replicas = lax.axis_size("chip") * lax.axis_size("core")
     my_section = lax.axis_index("section")
     batches = grad_out.shape[0]
     layers = point_weights.shape[1]
@@ -281,7 +281,11 @@
         out_specs=(vmem, vmem),
         compiler_params=params,
     )(first, hbuf, acts, xs, zs, weights, kerns)
-    recv = lax.all_to_all(send, "dp", 0, 0, tiled=True)
+    cores = lax.axis_size("core")
+    send = send.reshape((replicas // cores, cores) + send.shape[1:])
+    pair = lax.all_to_all(send, "core", 1, 1, tiled=True)
+    pair = jnp.sum(pair.astype(jnp.float32), axis=1).astype(jnp.bfloat16)
+    recv = lax.all_to_all(pair, "chip", 0, 0, tiled=True)
     summed = jnp.sum(recv.astype(jnp.float32), axis=0)
     point_red = summed[: layers * share].reshape(layers, share, chans)
     depth_red = summed[layers * share : layers * share + taps, : layers * share]
@@ -291,19 +295,22 @@
 
 
 def solution(mesh):
+    sections, replicas = mesh.devices.shape
+    split = Mesh(mesh.devices.reshape(sections, replicas // 2, 2), ("section", "chip", "core"))
+    dp = ("chip", "core")
     return jax.shard_map(
         body,
-        mesh=mesh,
+        mesh=split,
         in_specs=(
-            P("section", None, "dp", None, None, None),
-            P(None, "dp", None, None, None),
+            P("section", None, dp, None, None, None),
+            P(None, dp, None, None, None),
             P("section", None, None, None),
             P("section", None, None, None),
         ),
         out_specs=(
-            P("section", None, "dp", None, None, None),
-            P("section", None, "dp", None),
-            P("section", None, None, "dp"),
+            P("section", None, dp, None, None, None),
+            P("section", None, dp, None),
+            P("section", None, None, dp),
         ),
         check_vma=False,
     )

time: 152 us -> 146 us (0.961)
  blocking collectives: 42.2 us -> 34.1 us
  local copies, waits for them, and re-layouts: 5.95 us -> 7.86 us
    all_to_all x1 -> x2, blocking collectives: 42.2 us -> 34.1 us  [the longest x1 28.2 us: body(): recv = lax.all_to_all(pair, 'chip', 0, 0, tiled=True)]
    reduce_sum x0 -> x1, other arithmetic: none -> 1.93 us  [body(): pair = jnp.sum(pair.astype(jnp.float32), axis=1).astype(jnp.bfloat16)]
    reshape x0 -> x1, local copies, waits for them, and re-layouts: none -> 1.91 us  [body(): send = send.reshape((replicas // cores, cores) + send.shape[1:])]
where the time goes in v4:
time: 146 us; the launch traced here: 145 us
  Pallas kernels  79.9 us (55%)
  blocking collectives  34.1 us (23%)
  starting transfers between devices  14.8 us (10%)
  local copies, waits for them, and re-layouts  7.86 us (5%)
  other arithmetic  7.77 us (5%)
    pallas_call x7, Pallas kernels, body(): pl.pallas_call(functools.partial(step_kernel, height=height, width=width)...  37.7 us
    all_to_all x1, blocking collectives, body(): recv = lax.all_to_all(pair, 'chip', 0, 0, tiled=True)  28.2 us
    pallas_call x6, Pallas kernels, body(): pl.pallas_call(functools.partial(fwd_kernel, height=height, width=width),...  24.9 us
    ppermute x6, starting transfers between devices, from_behind(): return lax.ppermute(shard, axis, pairs)  14.8 us
    pallas_call x1, Pallas kernels, body(): pl.pallas_call(functools.partial(grad_kernel, height=height, width=width,...  13.1 us
    all_to_all x1, blocking collectives, body(): pair = lax.all_to_all(send, 'core', 1, 1, tiled=True)  5.84 us
    another operation x7, other arithmetic, body(): scalars = jnp.stack([picked, is_last, valid]).astype(jnp.int32)  4.23 us
    pallas_call x1, Pallas kernels, body(): pl.pallas_call(functools.partial(fwd_first_kernel, height=height, width=w...  4.18 us
  transfers between devices with their start and end apart: 6, of which 0 were waited for; matrix products, arithmetic and copies ran while one was open for 3% of the time, Pallas kernels for 17%

profile of v4, /device:TPU:6, one launch (start us, length us, event | category | flops | bytes accessed | tf_op | source)
XLA Modules:
  0.0 145.1 jit_solution(6625154279508731594)
XLA Ops:
  2.7 4.2 %shard_map.67 = (f32[4,4,128,512]{3,2,1,0:T(8,128)}, bf16[4,4,128,512]{3,2,1,0:T(8,128)(2,1)}, bf16[4,4,128,512]{3,2,1,0:T(8,128)(2,1)}, bf16[5,7,128,512]{3,2,1,0:T(8,128)(2,1)}) custom-call(s32[1]{0:T(128)} %bitcast.15.p_ref, bf16[4,128,512]{2,1,0:T(8,128)(2,1)} %bitcast.56, bf16[4,512,512]{2,1,0:T(8,128)(2,1)} %bitcast.32, ...), custom_call_target="tpu_custom_call" | custom-call | flops 282591232 | bytes 4194304 | tf_op jit(solution)/shard_map/pallas_call | solution.py:201
  7.5 5.4 %shard_map.68 = (bf16[128,512]{1,0:T(8,128)(2,1)}, bf16[5,7,128,512]{3,2,1,0:T(8,128)(2,1)}) custom-call(s32[3]{0:T(128)} %pad_add_fusion.6.p_ref, bf16[4,128,512]{2,1,0:T(8,128)(2,1)} %bitcast.49, bf16[128,512]{1,0:T(8,128)(2,1)} %broadcast_in_dim.6.car_ref, f32[4,4,128,512]{3,2,1,0:T(8,128)} %get-tuple-element.40.z_ref.refs_0_, ...), custom_call_target="tpu_custom_call", output_to_operand_aliasing={{1}: (6, {})} | custom-call | flops 282591232 | bytes 4194304 | tf_op jit(solution)/shard_map/pallas_call | solution.py:238
  12.9 2.7 %collective-permute-start = (bf16[128,512]{1,0:T(8,128)(2,1)}, bf16[128,512]{1,0:T(8,128)(2,1)S(1)}, u32[]{:S(2)}, u32[]{:S(2)}) collective-permute-start(bf16[128,512]{1,0:T(8,128)(2,1)} %get-tuple-element.42), channel_id=1, source_target_pairs={{32,0},{64,32},{96,64},{33,1},{65,33},{97,65},{34,2},{66,34},{98,6... | collective-permute-start | bytes 393224 | tf_op jit(solution)/shard_map/ppermute | solution.py:16
  15.7 4.1 %shard_map.69 = (f32[4,4,128,512]{3,2,1,0:T(8,128)}, bf16[4,4,128,512]{3,2,1,0:T(8,128)(2,1)}, bf16[4,4,128,512]{3,2,1,0:T(8,128)(2,1)}) custom-call(s32[1]{0:T(128)} %bitcast.13.p_ref, bf16[4,128,512]{2,1,0:T(8,128)(2,1)} %bitcast.57, bf16[4,512,512]{2,1,0:T(8,128)(2,1)} %bitcast.34, ...), custom_call_target="tpu_custom_call", output_to_operand_aliasing={{0}: (4, {}), {1}: (5, {}), {2}: (6, {})} | custom-call | flops 282591232 | bytes 4194304 | tf_op jit(solution)/shard_map/pallas_call | solution.py:252
  21.1 5.4 %shard_map.70 = (bf16[128,512]{1,0:T(8,128)(2,1)}, bf16[5,7,128,512]{3,2,1,0:T(8,128)(2,1)}) custom-call(s32[3]{0:T(128)} %pad_add_fusion.5.p_ref, bf16[4,128,512]{2,1,0:T(8,128)(2,1)} %bitcast.50, bf16[128,512]{1,0:T(8,128)(2,1)} %copy-done, f32[4,4,128,512]{3,2,1,0:T(8,128)} %get-tuple-element.45.z_ref.refs_0_, ...), custom_call_target="tpu_custom_call", output_to_operand_aliasing={{1}: (6, {})} | custom-call | flops 282591232 | bytes 4194304 | tf_op jit(solution)/shard_map/pallas_call | solution.py:238
  26.4 2.6 %collective-permute-start.1 = (bf16[128,512]{1,0:T(8,128)(2,1)}, bf16[128,512]{1,0:T(8,128)(2,1)S(1)}, u32[]{:S(2)}, u32[]{:S(2)}) collective-permute-start(bf16[128,512]{1,0:T(8,128)(2,1)} %get-tuple-element.47), channel_id=1, source_target_pairs={{32,0},{64,32},{96,64},{33,1},{65,33},{97,65},{34,2},{66,34},{98,6... | collective-permute-start | bytes 393224 | tf_op jit(solution)/shard_map/ppermute | solution.py:16
  29.6 4.2 %shard_map.71 = (f32[4,4,128,512]{3,2,1,0:T(8,128)}, bf16[4,4,128,512]{3,2,1,0:T(8,128)(2,1)}, bf16[4,4,128,512]{3,2,1,0:T(8,128)(2,1)}) custom-call(s32[1]{0:T(128)} %bitcast.11.p_ref, bf16[4,128,512]{2,1,0:T(8,128)(2,1)} %bitcast.58, bf16[4,512,512]{2,1,0:T(8,128)(2,1)} %bitcast.36, ...), custom_call_target="tpu_custom_call", output_to_operand_aliasing={{0}: (4, {}), {1}: (5, {}), {2}: (6, {})} | custom-call | flops 282591232 | bytes 4194304 | tf_op jit(solution)/shard_map/pallas_call | solution.py:252
  34.4 5.4 %shard_map.72 = (bf16[128,512]{1,0:T(8,128)(2,1)}, bf16[5,7,128,512]{3,2,1,0:T(8,128)(2,1)}) custom-call(s32[3]{0:T(128)} %pad_add_fusion.4.p_ref, bf16[4,128,512]{2,1,0:T(8,128)(2,1)} %bitcast.51, bf16[128,512]{1,0:T(8,128)(2,1)} %copy-done.2, f32[4,4,128,512]{3,2,1,0:T(8,128)} %get-tuple-element.50.z_ref.refs_0_, ...), custom_call_target="tpu_custom_call", output_to_operand_aliasing={{1}: (6, {})} | custom-call | flops 282591232 | bytes 4194304 | tf_op jit(solution)/shard_map/pallas_call | solution.py:238
  39.8 2.4 %collective-permute-start.2 = (bf16[128,512]{1,0:T(8,128)(2,1)}, bf16[128,512]{1,0:T(8,128)(2,1)S(1)}, u32[]{:S(2)}, u32[]{:S(2)}) collective-permute-start(bf16[128,512]{1,0:T(8,128)(2,1)} %get-tuple-element.52), channel_id=1, source_target_pairs={{32,0},{64,32},{96,64},{33,1},{65,33},{97,65},{34,2},{66,34},{98,6... | collective-permute-start | bytes 393224 | tf_op jit(solution)/shard_map/ppermute | solution.py:16
  42.8 4.2 %shard_map.73 = (f32[4,4,128,512]{3,2,1,0:T(8,128)}, bf16[4,4,128,512]{3,2,1,0:T(8,128)(2,1)}, bf16[4,4,128,512]{3,2,1,0:T(8,128)(2,1)}) custom-call(s32[1]{0:T(128)} %bitcast.9.p_ref, bf16[4,128,512]{2,1,0:T(8,128)(2,1)} %bitcast.59, bf16[4,512,512]{2,1,0:T(8,128)(2,1)} %bitcast.38, ...), custom_call_target="tpu_custom_call", output_to_operand_aliasing={{0}: (4, {}), {1}: (5, {}), {2}: (6, {})} | custom-call | flops 282591232 | bytes 4194304 | tf_op jit(solution)/shard_map/pallas_call | solution.py:252
  47.7 5.4 %shard_map.74 = (bf16[128,512]{1,0:T(8,128)(2,1)}, bf16[5,7,128,512]{3,2,1,0:T(8,128)(2,1)}) custom-call(s32[3]{0:T(128)} %pad_add_fusion.3.p_ref, bf16[4,128,512]{2,1,0:T(8,128)(2,1)} %bitcast.52, bf16[128,512]{1,0:T(8,128)(2,1)} %copy-done.3, f32[4,4,128,512]{3,2,1,0:T(8,128)} %get-tuple-element.55.z_ref.refs_0_, ...), custom_call_target="tpu_custom_call", output_to_operand_aliasing={{1}: (6, {})} | custom-call | flops 282591232 | bytes 4194304 | tf_op jit(solution)/shard_map/pallas_call | solution.py:238
  53.0 2.5 %collective-permute-start.3 = (bf16[128,512]{1,0:T(8,128)(2,1)}, bf16[128,512]{1,0:T(8,128)(2,1)S(1)}, u32[]{:S(2)}, u32[]{:S(2)}) collective-permute-start(bf16[128,512]{1,0:T(8,128)(2,1)} %get-tuple-element.57), channel_id=1, source_target_pairs={{32,0},{64,32},{96,64},{33,1},{65,33},{97,65},{34,2},{66,34},{98,6... | collective-permute-start | bytes 393224 | tf_op jit(solution)/shard_map/ppermute | solution.py:16
  56.1 4.2 %shard_map.75 = (f32[4,4,128,512]{3,2,1,0:T(8,128)}, bf16[4,4,128,512]{3,2,1,0:T(8,128)(2,1)}, bf16[4,4,128,512]{3,2,1,0:T(8,128)(2,1)}) custom-call(s32[1]{0:T(128)} %bitcast.7.p_ref, bf16[4,128,512]{2,1,0:T(8,128)(2,1)} %bitcast.60, bf16[4,512,512]{2,1,0:T(8,128)(2,1)} %bitcast.40, ...), custom_call_target="tpu_custom_call", output_to_operand_aliasing={{0}: (4, {}), {1}: (5, {}), {2}: (6, {})} | custom-call | flops 282591232 | bytes 4194304 | tf_op jit(solution)/shard_map/pallas_call | solution.py:252
  60.9 5.4 %shard_map.76 = (bf16[128,512]{1,0:T(8,128)(2,1)}, bf16[5,7,128,512]{3,2,1,0:T(8,128)(2,1)}) custom-call(s32[3]{0:T(128)} %pad_add_fusion.2.p_ref, bf16[4,128,512]{2,1,0:T(8,128)(2,1)} %bitcast.53, bf16[128,512]{1,0:T(8,128)(2,1)} %copy-done.4, f32[4,4,128,512]{3,2,1,0:T(8,128)} %get-tuple-element.60.z_ref.refs_0_, ...), custom_call_target="tpu_custom_call", output_to_operand_aliasing={{1}: (6, {})} | custom-call | flops 282591232 | bytes 4194304 | tf_op jit(solution)/shard_map/pallas_call | solution.py:238
  66.3 2.3 %collective-permute-start.4 = (bf16[128,512]{1,0:T(8,128)(2,1)}, bf16[128,512]{1,0:T(8,128)(2,1)S(1)}, u32[]{:S(2)}, u32[]{:S(2)}) collective-permute-start(bf16[128,512]{1,0:T(8,128)(2,1)} %get-tuple-element.62), channel_id=1, source_target_pairs={{32,0},{64,32},{96,64},{33,1},{65,33},{97,65},{34,2},{66,34},{98,6... | collective-permute-start | bytes 393224 | tf_op jit(solution)/shard_map/ppermute | solution.py:16
  69.2 4.2 %shard_map.77 = (f32[4,4,128,512]{3,2,1,0:T(8,128)}, bf16[4,4,128,512]{3,2,1,0:T(8,128)(2,1)}, bf16[4,4,128,512]{3,2,1,0:T(8,128)(2,1)}) custom-call(s32[1]{0:T(128)} %bitcast.5.p_ref, bf16[4,128,512]{2,1,0:T(8,128)(2,1)} %bitcast.61, bf16[4,512,512]{2,1,0:T(8,128)(2,1)} %bitcast.42, ...), custom_call_target="tpu_custom_call", output_to_operand_aliasing={{0}: (4, {}), {1}: (5, {}), {2}: (6, {})} | custom-call | flops 282591232 | bytes 4194304 | tf_op jit(solution)/shard_map/pallas_call | solution.py:252
  74.0 5.4 %shard_map.78 = (bf16[128,512]{1,0:T(8,128)(2,1)}, bf16[5,7,128,512]{3,2,1,0:T(8,128)(2,1)}) custom-call(s32[3]{0:T(128)} %pad_add_fusion.1.p_ref, bf16[4,128,512]{2,1,0:T(8,128)(2,1)} %bitcast.54, bf16[128,512]{1,0:T(8,128)(2,1)} %copy-done.5, f32[4,4,128,512]{3,2,1,0:T(8,128)} %get-tuple-element.65.z_ref.refs_0_, ...), custom_call_target="tpu_custom_call", output_to_operand_aliasing={{1}: (6, {})} | custom-call | flops 282591232 | bytes 4194304 | tf_op jit(solution)/shard_map/pallas_call | solution.py:238
  79.4 2.3 %collective-permute-start.5 = (bf16[128,512]{1,0:T(8,128)(2,1)}, bf16[128,512]{1,0:T(8,128)(2,1)S(1)}, u32[]{:S(2)}, u32[]{:S(2)}) collective-permute-start(bf16[128,512]{1,0:T(8,128)(2,1)} %get-tuple-element.67), channel_id=1, source_target_pairs={{32,0},{64,32},{96,64},{33,1},{65,33},{97,65},{34,2},{66,34},{98,6... | collective-permute-start | bytes 393224 | tf_op jit(solution)/shard_map/ppermute | solution.py:16
  82.4 4.2 %shard_map.79 = (f32[4,4,128,512]{3,2,1,0:T(8,128)}, bf16[4,4,128,512]{3,2,1,0:T(8,128)(2,1)}, bf16[4,4,128,512]{3,2,1,0:T(8,128)(2,1)}) custom-call(s32[1]{0:T(128)} %bitcast.1.p_ref, bf16[4,128,512]{2,1,0:T(8,128)(2,1)} %bitcast.62, bf16[4,512,512]{2,1,0:T(8,128)(2,1)} %bitcast.44, ...), custom_call_target="tpu_custom_call", output_to_operand_aliasing={{0}: (4, {}), {1}: (5, {}), {2}: (6, {})} | custom-call | flops 282591232 | bytes 4194304 | tf_op jit(solution)/shard_map/pallas_call | solution.py:252
  87.2 5.4 %shard_map.80 = (bf16[128,512]{1,0:T(8,128)(2,1)}, bf16[5,7,128,512]{3,2,1,0:T(8,128)(2,1)}) custom-call(s32[3]{0:T(128)} %pad_add_fusion.p_ref, bf16[4,128,512]{2,1,0:T(8,128)(2,1)} %bitcast.55, bf16[128,512]{1,0:T(8,128)(2,1)} %copy-done.1, f32[4,4,128,512]{3,2,1,0:T(8,128)} %get-tuple-element.70.z_ref, ...), custom_call_target="tpu_custom_call", output_to_operand_aliasing={{1}: (6, {})} | custom-call | flops 282591232 | bytes 4194304 | tf_op jit(solution)/shard_map/pallas_call | solution.py:238
  92.5 13.1 %shard_map.81 = (bf16[32,80,512]{2,1,0:T(8,128)(2,1)}, bf16[4,128,512]{2,1,0:T(8,128)(2,1)}) custom-call(s32[1]{0:T(128)} %bitcast.p_ref, bf16[5,7,128,512]{3,2,1,0:T(8,128)(2,1)} %get-tuple-element.72.h_ref, bf16[4,512,512]{2,1,0:T(8,128)(2,1)} %bitcast.47, bf16[4,512,512]{2,1,0:T(8,128)(2,1)} %bitcast.48, f32[4,512,512]{2,1,0:T(8,128)} %bitcast.31, ...), custom_call_target="tpu_custom_call" | custom-call | tf_op jit(solution)/shard_map/pallas_call | solution.py:274
  107.6 5.8 %all_to_all.10 = bf16[16,2,80,512]{3,2,0,1:T(8,128)(2,1)S(1)} all-to-all(bf16[16,2,80,512]{3,2,0,1:T(8,128)(2,1)S(1)} %copy.36), channel_id=1, replica_groups=mesh['section'=4,'chip'=16,'core'=2] {'core'}, dimensions={1} | all-to-all | bytes 5242880 | tf_op jit(solution)/shard_map/all_to_all | solution.py:286
  113.4 1.9 %reduce_sum.21 = bf16[16,80,512]{2,1,0:T(8,128)(2,1)} reduce(bf16[16,2,80,512]{3,2,0,1:T(8,128)(2,1)S(1)} %all_to_all.10, bf16[]{:T(256)} %constant.25.clone.1), dimensions={1}, to_apply=%region_0.1 | reduce | flops 655360 | bytes 3932162 | tf_op jit(solution)/shard_map/reduce_sum | solution.py:287
  115.3 28.2 %all_to_all.11 = bf16[16,80,512]{2,1,0:T(8,128)(2,1)S(1)} all-to-all(bf16[16,80,512]{2,1,0:T(8,128)(2,1)} %reduce_sum.21), channel_id=1, replica_groups=mesh['section'=4,'chip'=16,'core'=2] {'chip'}, dimensions={0} | all-to-all | bytes 2621440 | tf_op jit(solution)/shard_map/all_to_all | solution.py:288
  (32 shorter events, 13.7 us)
Async XLA Ops:
  12.9 7.5 %collective-permute-start = (bf16[128,512]{1,0:T(8,128)(2,1)}, bf16[128,512]{1,0:T(8,128)(2,1)S(1)}, u32[]{:S(2)}, u32[]{:S(2)}) collective-permute-start(bf16[128,512]{1,0:T(8,128)(2,1)} %get-tuple-element.42), channel_id=1, source_target_pairs={{32,0},{64,32},{96,64},{33,1},{65,33},{97,65},{34,2},{66,34},{98,6... | collective-permute-start | bytes 393224 | tf_op jit(solution)/shard_map/ppermute | solution.py:16
  20.4 0.7 copy-start
  26.4 7.3 %collective-permute-start.1 = (bf16[128,512]{1,0:T(8,128)(2,1)}, bf16[128,512]{1,0:T(8,128)(2,1)S(1)}, u32[]{:S(2)}, u32[]{:S(2)}) collective-permute-start(bf16[128,512]{1,0:T(8,128)(2,1)} %get-tuple-element.47), channel_id=1, source_target_pairs={{32,0},{64,32},{96,64},{33,1},{65,33},{97,65},{34,2},{66,34},{98,6... | collective-permute-start | bytes 393224 | tf_op jit(solution)/shard_map/ppermute | solution.py:16
  33.8 0.7 copy-start.2
  39.8 7.2 %collective-permute-start.2 = (bf16[128,512]{1,0:T(8,128)(2,1)}, bf16[128,512]{1,0:T(8,128)(2,1)S(1)}, u32[]{:S(2)}, u32[]{:S(2)}) collective-permute-start(bf16[128,512]{1,0:T(8,128)(2,1)} %get-tuple-element.52), channel_id=1, source_target_pairs={{32,0},{64,32},{96,64},{33,1},{65,33},{97,65},{34,2},{66,34},{98,6... | collective-permute-start | bytes 393224 | tf_op jit(solution)/shard_map/ppermute | solution.py:16
  47.0 0.7 copy-start.3
  53.0 7.3 %collective-permute-start.3 = (bf16[128,512]{1,0:T(8,128)(2,1)}, bf16[128,512]{1,0:T(8,128)(2,1)S(1)}, u32[]{:S(2)}, u32[]{:S(2)}) collective-permute-start(bf16[128,512]{1,0:T(8,128)(2,1)} %get-tuple-element.57), channel_id=1, source_target_pairs={{32,0},{64,32},{96,64},{33,1},{65,33},{97,65},{34,2},{66,34},{98,6... | collective-permute-start | bytes 393224 | tf_op jit(solution)/shard_map/ppermute | solution.py:16
  60.3 0.7 copy-start.4
  66.3 7.0 %collective-permute-start.4 = (bf16[128,512]{1,0:T(8,128)(2,1)}, bf16[128,512]{1,0:T(8,128)(2,1)S(1)}, u32[]{:S(2)}, u32[]{:S(2)}) collective-permute-start(bf16[128,512]{1,0:T(8,128)(2,1)} %get-tuple-element.62), channel_id=1, source_target_pairs={{32,0},{64,32},{96,64},{33,1},{65,33},{97,65},{34,2},{66,34},{98,6... | collective-permute-start | bytes 393224 | tf_op jit(solution)/shard_map/ppermute | solution.py:16
  73.4 0.7 copy-start.5
  79.4 7.1 %collective-permute-start.5 = (bf16[128,512]{1,0:T(8,128)(2,1)}, bf16[128,512]{1,0:T(8,128)(2,1)S(1)}, u32[]{:S(2)}, u32[]{:S(2)}) collective-permute-start(bf16[128,512]{1,0:T(8,128)(2,1)} %get-tuple-element.67), channel_id=1, source_target_pairs={{32,0},{64,32},{96,64},{33,1},{65,33},{97,65},{34,2},{66,34},{98,6... | collective-permute-start | bytes 393224 | tf_op jit(solution)/shard_map/ppermute | solution.py:16
  86.5 0.7 copy-start.1

commit v5 on v4

--- a/solution.py
+++ b/solution.py
@@ -1,6 +1,8 @@
 import functools
+import math
 
 import jax
+import numpy as np
 import jax.numpy as jnp
 from jax import lax
 from jax.experimental import pallas as pl
@@ -113,9 +115,10 @@
     taps = k_ref.shape[1]
     batches = res_ref.shape[0]
     rows = h_ref.shape[2]
-    replicas = send_ref.shape[0]
+    lead = send_ref.shape[:-2]
+    replicas = math.prod(lead)
     share = chans // replicas
-    pad_taps = send_ref.shape[1] - layers * share
+    pad_taps = send_ref.shape[-2] - layers * share
     first = p_ref[0]
     for m in range(batches):
         res_ref[m] = h_ref[0, first + m]
@@ -134,7 +137,7 @@
         )
         point = point * scale
         for d in range(replicas):
-            send_ref[d, layer * share : (layer + 1) * share, :] = point[
+            send_ref[np.unravel_index(d, lead) + (slice(layer * share, (layer + 1) * share),)] = point[
                 d * share : (d + 1) * share
             ].astype(jnp.bfloat16)
         xf = xs_ref[layer].astype(jnp.float32)
@@ -151,12 +154,15 @@
             moved = depth[layer] if amount == 0 else pltpu.roll(depth[layer], amount, 1)
             keep = (lane >= layer * share) & (lane < (layer + 1) * share)
             slot = jnp.where(keep, moved, slot)
-        send_ref[d, layers * share :, :] = slot.astype(jnp.bfloat16)
+        send_ref[np.unravel_index(d, lead) + (slice(layers * share, None),)] = slot.astype(
+            jnp.bfloat16
+        )
 
 
 def body(section_inputs, grad_out, point_weights, depth_weights):
     sections = lax.axis_size("section")
-    replicas = lax.axis_size("chip") * lax.axis_size("core")
+    lead = (lax.axis_size("y"), lax.axis_size("z"), lax.axis_size("core"))
+    replicas = math.prod(lead)
     my_section = lax.axis_index("section")
     batches = grad_out.shape[0]
     layers = point_weights.shape[1]
@@ -274,19 +280,20 @@
     send, res = pl.pallas_call(
         functools.partial(grad_kernel, height=height, width=width, scale=scale),
         out_shape=(
-            jax.ShapeDtypeStruct((replicas, layers * share + pad_taps, chans), jnp.bfloat16),
+            jax.ShapeDtypeStruct(lead + (layers * share + pad_taps, chans), jnp.bfloat16),
             jax.ShapeDtypeStruct((batches, rows, chans), jnp.bfloat16),
         ),
         in_specs=[smem, vmem, vmem, vmem, vmem, vmem, vmem],
         out_specs=(vmem, vmem),
         compiler_params=params,
     )(first, hbuf, acts, xs, zs, weights, kerns)
-    cores = lax.axis_size("core")
-    send = send.reshape((replicas // cores, cores) + send.shape[1:])
-    pair = lax.all_to_all(send, "core", 1, 1, tiled=True)
-    pair = jnp.sum(pair.astype(jnp.float32), axis=1).astype(jnp.bfloat16)
-    recv = lax.all_to_all(pair, "chip", 0, 0, tiled=True)
-    summed = jnp.sum(recv.astype(jnp.float32), axis=0)
+    part = send
+    for axis, name in reversed(list(enumerate(("y", "z", "core")))):
+        part = lax.all_to_all(part, name, axis, axis, tiled=True)
+        part = jnp.sum(part.astype(jnp.float32), axis=axis)
+        if axis:
+            part = part.astype(jnp.bfloat16)
+    summed = part
     point_red = summed[: layers * share].reshape(layers, share, chans)
     depth_red = summed[layers * share : layers * share + taps, : layers * share]
     depth_red = depth_red.reshape(taps, layers, share).transpose(1, 0, 2)
@@ -296,8 +303,15 @@
 
 def solution(mesh):
     sections, replicas = mesh.devices.shape
-    split = Mesh(mesh.devices.reshape(sections, replicas // 2, 2), ("section", "chip", "core"))
-    dp = ("chip", "core")
+    try:
+        zsize = len({d.coords[2] for d in mesh.devices[0]})
+    except (AttributeError, IndexError, TypeError):
+        zsize = 1
+    split = Mesh(
+        mesh.devices.reshape(sections, replicas // (2 * zsize), zsize, 2),
+        ("section", "y", "z", "core"),
+    )
+    dp = ("y", "z", "core")
     return jax.shard_map(
         body,
         mesh=split,

time: 146 us -> 154 us (1.055)
  blocking collectives: 34.1 us -> 40.7 us
    all_to_all x2 -> x3, blocking collectives: 34.1 us -> 40.7 us  [body(): part = lax.all_to_all(part, name, axis, axis, tiled=True)]
    pallas_call x0 -> x1, local copies, waits for them, and re-layouts: none -> 1.91 us  [body(): pl.pallas_call(functools.partial(grad_kernel, height=height, width=width,...]
    reshape x1 -> x0, local copies, waits for them, and re-layouts: 1.91 us -> none  [body(): send = send.reshape((replicas // cores, cores) + send.shape[1:])]
  transfers between devices with their start and end apart: 6 -> 6, of which waited for: 0 -> 0; matrix products, arithmetic and copies ran while one was open for 3% -> 2% of each run, Pallas kernels for 17% -> 16%
where the time goes in v5:
time: 154 us; the launch traced here: 153 us
  Pallas kernels  80 us (52%)
  blocking collectives  40.7 us (26%)
  starting transfers between devices  14.7 us (10%)
  local copies, waits for them, and re-layouts  9.26 us (6%)
  other arithmetic  8.07 us (5%)
    all_to_all x3, blocking collectives, body(): part = lax.all_to_all(part, name, axis, axis, tiled=True)  40.7 us
    pallas_call x7, Pallas kernels, body(): pl.pallas_call(functools.partial(step_kernel, height=height, width=width)...  37.7 us
    pallas_call x6, Pallas kernels, body(): pl.pallas_call(functools.partial(fwd_kernel, height=height, width=width),...  24.9 us
    ppermute x6, starting transfers between devices, from_behind(): return lax.ppermute(shard, axis, pairs)  14.7 us
    pallas_call x1, Pallas kernels, body(): pl.pallas_call(functools.partial(grad_kernel, height=height, width=width,...  13.1 us
    another operation x7, other arithmetic, body(): scalars = jnp.stack([picked, is_last, valid]).astype(jnp.int32)  4.34 us
    pallas_call x1, Pallas kernels, body(): pl.pallas_call(functools.partial(fwd_first_kernel, height=height, width=w...  4.2 us
    unnamed x12, local copies, waits for them, and re-layouts  3.93 us
  transfers between devices with their start and end apart: 6, of which 0 were waited for; matrix products, arithmetic and copies ran while one was open for 2% of the time, Pallas kernels for 16%

profile of v5, /device:TPU:6, one launch (start us, length us, event | category | flops | bytes accessed | tf_op | source)
XLA Modules:
  0.0 153.4 jit_solution(4076214058703964552)
XLA Ops:
  2.7 4.2 %shard_map.67 = (f32[4,4,128,512]{3,2,1,0:T(8,128)}, bf16[4,4,128,512]{3,2,1,0:T(8,128)(2,1)}, bf16[4,4,128,512]{3,2,1,0:T(8,128)(2,1)}, bf16[5,7,128,512]{3,2,1,0:T(8,128)(2,1)}) custom-call(s32[1]{0:T(128)} %bitcast.15.p_ref, bf16[4,128,512]{2,1,0:T(8,128)(2,1)} %bitcast.55, bf16[4,512,512]{2,1,0:T(8,128)(2,1)} %bitcast.31, ...), custom_call_target="tpu_custom_call" | custom-call | flops 282591232 | bytes 4194304 | tf_op jit(solution)/shard_map/pallas_call | solution.py:207
  7.6 5.4 %shard_map.68 = (bf16[128,512]{1,0:T(8,128)(2,1)}, bf16[5,7,128,512]{3,2,1,0:T(8,128)(2,1)}) custom-call(s32[3]{0:T(128)} %pad_add_fusion.6.p_ref, bf16[4,128,512]{2,1,0:T(8,128)(2,1)} %bitcast.48, bf16[128,512]{1,0:T(8,128)(2,1)} %broadcast_in_dim.6.car_ref, f32[4,4,128,512]{3,2,1,0:T(8,128)} %get-tuple-element.40.z_ref.refs_0_, ...), custom_call_target="tpu_custom_call", output_to_operand_aliasing={{1}: (6, {})} | custom-call | flops 282591232 | bytes 4194304 | tf_op jit(solution)/shard_map/pallas_call | solution.py:244
  13.0 2.7 %collective-permute-start = (bf16[128,512]{1,0:T(8,128)(2,1)}, bf16[128,512]{1,0:T(8,128)(2,1)S(1)}, u32[]{:S(2)}, u32[]{:S(2)}) collective-permute-start(bf16[128,512]{1,0:T(8,128)(2,1)} %get-tuple-element.42), channel_id=1, source_target_pairs={{32,0},{64,32},{96,64},{33,1},{65,33},{97,65},{34,2},{66,34},{98,6... | collective-permute-start | bytes 393224 | tf_op jit(solution)/shard_map/ppermute | solution.py:18
  15.8 4.2 %shard_map.69 = (f32[4,4,128,512]{3,2,1,0:T(8,128)}, bf16[4,4,128,512]{3,2,1,0:T(8,128)(2,1)}, bf16[4,4,128,512]{3,2,1,0:T(8,128)(2,1)}) custom-call(s32[1]{0:T(128)} %bitcast.13.p_ref, bf16[4,128,512]{2,1,0:T(8,128)(2,1)} %bitcast.56, bf16[4,512,512]{2,1,0:T(8,128)(2,1)} %bitcast.33, ...), custom_call_target="tpu_custom_call", output_to_operand_aliasing={{0}: (4, {}), {1}: (5, {}), {2}: (6, {})} | custom-call | flops 282591232 | bytes 4194304 | tf_op jit(solution)/shard_map/pallas_call | solution.py:258
  21.2 5.4 %shard_map.70 = (bf16[128,512]{1,0:T(8,128)(2,1)}, bf16[5,7,128,512]{3,2,1,0:T(8,128)(2,1)}) custom-call(s32[3]{0:T(128)} %pad_add_fusion.5.p_ref, bf16[4,128,512]{2,1,0:T(8,128)(2,1)} %bitcast.49, bf16[128,512]{1,0:T(8,128)(2,1)} %copy-done, f32[4,4,128,512]{3,2,1,0:T(8,128)} %get-tuple-element.45.z_ref.refs_0_, ...), custom_call_target="tpu_custom_call", output_to_operand_aliasing={{1}: (6, {})} | custom-call | flops 282591232 | bytes 4194304 | tf_op jit(solution)/shard_map/pallas_call | solution.py:244
  26.6 2.5 %collective-permute-start.1 = (bf16[128,512]{1,0:T(8,128)(2,1)}, bf16[128,512]{1,0:T(8,128)(2,1)S(1)}, u32[]{:S(2)}, u32[]{:S(2)}) collective-permute-start(bf16[128,512]{1,0:T(8,128)(2,1)} %get-tuple-element.47), channel_id=1, source_target_pairs={{32,0},{64,32},{96,64},{33,1},{65,33},{97,65},{34,2},{66,34},{98,6... | collective-permute-start | bytes 393224 | tf_op jit(solution)/shard_map/ppermute | solution.py:18
  29.8 4.2 %shard_map.71 = (f32[4,4,128,512]{3,2,1,0:T(8,128)}, bf16[4,4,128,512]{3,2,1,0:T(8,128)(2,1)}, bf16[4,4,128,512]{3,2,1,0:T(8,128)(2,1)}) custom-call(s32[1]{0:T(128)} %bitcast.11.p_ref, bf16[4,128,512]{2,1,0:T(8,128)(2,1)} %bitcast.57, bf16[4,512,512]{2,1,0:T(8,128)(2,1)} %bitcast.35, ...), custom_call_target="tpu_custom_call", output_to_operand_aliasing={{0}: (4, {}), {1}: (5, {}), {2}: (6, {})} | custom-call | flops 282591232 | bytes 4194304 | tf_op jit(solution)/shard_map/pallas_call | solution.py:258
  34.6 5.4 %shard_map.72 = (bf16[128,512]{1,0:T(8,128)(2,1)}, bf16[5,7,128,512]{3,2,1,0:T(8,128)(2,1)}) custom-call(s32[3]{0:T(128)} %pad_add_fusion.4.p_ref, bf16[4,128,512]{2,1,0:T(8,128)(2,1)} %bitcast.50, bf16[128,512]{1,0:T(8,128)(2,1)} %copy-done.2, f32[4,4,128,512]{3,2,1,0:T(8,128)} %get-tuple-element.50.z_ref.refs_0_, ...), custom_call_target="tpu_custom_call", output_to_operand_aliasing={{1}: (6, {})} | custom-call | flops 282591232 | bytes 4194304 | tf_op jit(solution)/shard_map/pallas_call | solution.py:244
  40.0 2.4 %collective-permute-start.2 = (bf16[128,512]{1,0:T(8,128)(2,1)}, bf16[128,512]{1,0:T(8,128)(2,1)S(1)}, u32[]{:S(2)}, u32[]{:S(2)}) collective-permute-start(bf16[128,512]{1,0:T(8,128)(2,1)} %get-tuple-element.52), channel_id=1, source_target_pairs={{32,0},{64,32},{96,64},{33,1},{65,33},{97,65},{34,2},{66,34},{98,6... | collective-permute-start | bytes 393224 | tf_op jit(solution)/shard_map/ppermute | solution.py:18
  43.1 4.1 %shard_map.73 = (f32[4,4,128,512]{3,2,1,0:T(8,128)}, bf16[4,4,128,512]{3,2,1,0:T(8,128)(2,1)}, bf16[4,4,128,512]{3,2,1,0:T(8,128)(2,1)}) custom-call(s32[1]{0:T(128)} %bitcast.9.p_ref, bf16[4,128,512]{2,1,0:T(8,128)(2,1)} %bitcast.58, bf16[4,512,512]{2,1,0:T(8,128)(2,1)} %bitcast.37, ...), custom_call_target="tpu_custom_call", output_to_operand_aliasing={{0}: (4, {}), {1}: (5, {}), {2}: (6, {})} | custom-call | flops 282591232 | bytes 4194304 | tf_op jit(solution)/shard_map/pallas_call | solution.py:258
  47.9 5.4 %shard_map.74 = (bf16[128,512]{1,0:T(8,128)(2,1)}, bf16[5,7,128,512]{3,2,1,0:T(8,128)(2,1)}) custom-call(s32[3]{0:T(128)} %pad_add_fusion.3.p_ref, bf16[4,128,512]{2,1,0:T(8,128)(2,1)} %bitcast.51, bf16[128,512]{1,0:T(8,128)(2,1)} %copy-done.3, f32[4,4,128,512]{3,2,1,0:T(8,128)} %get-tuple-element.55.z_ref.refs_0_, ...), custom_call_target="tpu_custom_call", output_to_operand_aliasing={{1}: (6, {})} | custom-call | flops 282591232 | bytes 4194304 | tf_op jit(solution)/shard_map/pallas_call | solution.py:244
  53.2 2.5 %collective-permute-start.3 = (bf16[128,512]{1,0:T(8,128)(2,1)}, bf16[128,512]{1,0:T(8,128)(2,1)S(1)}, u32[]{:S(2)}, u32[]{:S(2)}) collective-permute-start(bf16[128,512]{1,0:T(8,128)(2,1)} %get-tuple-element.57), channel_id=1, source_target_pairs={{32,0},{64,32},{96,64},{33,1},{65,33},{97,65},{34,2},{66,34},{98,6... | collective-permute-start | bytes 393224 | tf_op jit(solution)/shard_map/ppermute | solution.py:18
  56.4 4.1 %shard_map.75 = (f32[4,4,128,512]{3,2,1,0:T(8,128)}, bf16[4,4,128,512]{3,2,1,0:T(8,128)(2,1)}, bf16[4,4,128,512]{3,2,1,0:T(8,128)(2,1)}) custom-call(s32[1]{0:T(128)} %bitcast.7.p_ref, bf16[4,128,512]{2,1,0:T(8,128)(2,1)} %bitcast.59, bf16[4,512,512]{2,1,0:T(8,128)(2,1)} %bitcast.39, ...), custom_call_target="tpu_custom_call", output_to_operand_aliasing={{0}: (4, {}), {1}: (5, {}), {2}: (6, {})} | custom-call | flops 282591232 | bytes 4194304 | tf_op jit(solution)/shard_map/pallas_call | solution.py:258
  61.2 5.4 %shard_map.76 = (bf16[128,512]{1,0:T(8,128)(2,1)}, bf16[5,7,128,512]{3,2,1,0:T(8,128)(2,1)}) custom-call(s32[3]{0:T(128)} %pad_add_fusion.2.p_ref, bf16[4,128,512]{2,1,0:T(8,128)(2,1)} %bitcast.52, bf16[128,512]{1,0:T(8,128)(2,1)} %copy-done.4, f32[4,4,128,512]{3,2,1,0:T(8,128)} %get-tuple-element.60.z_ref.refs_0_, ...), custom_call_target="tpu_custom_call", output_to_operand_aliasing={{1}: (6, {})} | custom-call | flops 282591232 | bytes 4194304 | tf_op jit(solution)/shard_map/pallas_call | solution.py:244
  66.6 2.2 %collective-permute-start.4 = (bf16[128,512]{1,0:T(8,128)(2,1)}, bf16[128,512]{1,0:T(8,128)(2,1)S(1)}, u32[]{:S(2)}, u32[]{:S(2)}) collective-permute-start(bf16[128,512]{1,0:T(8,128)(2,1)} %get-tuple-element.62), channel_id=1, source_target_pairs={{32,0},{64,32},{96,64},{33,1},{65,33},{97,65},{34,2},{66,34},{98,6... | collective-permute-start | bytes 393224 | tf_op jit(solution)/shard_map/ppermute | solution.py:18
  69.4 4.1 %shard_map.77 = (f32[4,4,128,512]{3,2,1,0:T(8,128)}, bf16[4,4,128,512]{3,2,1,0:T(8,128)(2,1)}, bf16[4,4,128,512]{3,2,1,0:T(8,128)(2,1)}) custom-call(s32[1]{0:T(128)} %bitcast.5.p_ref, bf16[4,128,512]{2,1,0:T(8,128)(2,1)} %bitcast.60, bf16[4,512,512]{2,1,0:T(8,128)(2,1)} %bitcast.41, ...), custom_call_target="tpu_custom_call", output_to_operand_aliasing={{0}: (4, {}), {1}: (5, {}), {2}: (6, {})} | custom-call | flops 282591232 | bytes 4194304 | tf_op jit(solution)/shard_map/pallas_call | solution.py:258
  74.2 5.4 %shard_map.78 = (bf16[128,512]{1,0:T(8,128)(2,1)}, bf16[5,7,128,512]{3,2,1,0:T(8,128)(2,1)}) custom-call(s32[3]{0:T(128)} %pad_add_fusion.1.p_ref, bf16[4,128,512]{2,1,0:T(8,128)(2,1)} %bitcast.53, bf16[128,512]{1,0:T(8,128)(2,1)} %copy-done.5, f32[4,4,128,512]{3,2,1,0:T(8,128)} %get-tuple-element.65.z_ref.refs_0_, ...), custom_call_target="tpu_custom_call", output_to_operand_aliasing={{1}: (6, {})} | custom-call | flops 282591232 | bytes 4194304 | tf_op jit(solution)/shard_map/pallas_call | solution.py:244
  79.6 2.3 %collective-permute-start.5 = (bf16[128,512]{1,0:T(8,128)(2,1)}, bf16[128,512]{1,0:T(8,128)(2,1)S(1)}, u32[]{:S(2)}, u32[]{:S(2)}) collective-permute-start(bf16[128,512]{1,0:T(8,128)(2,1)} %get-tuple-element.67), channel_id=1, source_target_pairs={{32,0},{64,32},{96,64},{33,1},{65,33},{97,65},{34,2},{66,34},{98,6... | collective-permute-start | bytes 393224 | tf_op jit(solution)/shard_map/ppermute | solution.py:18
  82.5 4.1 %shard_map.79 = (f32[4,4,128,512]{3,2,1,0:T(8,128)}, bf16[4,4,128,512]{3,2,1,0:T(8,128)(2,1)}, bf16[4,4,128,512]{3,2,1,0:T(8,128)(2,1)}) custom-call(s32[1]{0:T(128)} %bitcast.1.p_ref, bf16[4,128,512]{2,1,0:T(8,128)(2,1)} %bitcast.61, bf16[4,512,512]{2,1,0:T(8,128)(2,1)} %bitcast.43, ...), custom_call_target="tpu_custom_call", output_to_operand_aliasing={{0}: (4, {}), {1}: (5, {}), {2}: (6, {})} | custom-call | flops 282591232 | bytes 4194304 | tf_op jit(solution)/shard_map/pallas_call | solution.py:258
  87.3 5.4 %shard_map.80 = (bf16[128,512]{1,0:T(8,128)(2,1)}, bf16[5,7,128,512]{3,2,1,0:T(8,128)(2,1)}) custom-call(s32[3]{0:T(128)} %pad_add_fusion.p_ref, bf16[4,128,512]{2,1,0:T(8,128)(2,1)} %bitcast.54, bf16[128,512]{1,0:T(8,128)(2,1)} %copy-done.1, f32[4,4,128,512]{3,2,1,0:T(8,128)} %get-tuple-element.70.z_ref, ...), custom_call_target="tpu_custom_call", output_to_operand_aliasing={{1}: (6, {})} | custom-call | flops 282591232 | bytes 4194304 | tf_op jit(solution)/shard_map/pallas_call | solution.py:244
  92.6 13.1 %shard_map.81 = (bf16[4,4,2,80,512]{4,3,2,1,0:T(8,128)(2,1)}, bf16[4,128,512]{2,1,0:T(8,128)(2,1)}) custom-call(s32[1]{0:T(128)} %bitcast.p_ref, bf16[5,7,128,512]{3,2,1,0:T(8,128)(2,1)} %get-tuple-element.72.h_ref, bf16[4,512,512]{2,1,0:T(8,128)(2,1)} %bitcast.46, bf16[4,512,512]{2,1,0:T(8,128)(2,1)} %bitcast.47, f32[4,512,512]{2,1,0:T(8,128)} %bitcast.30, ...), custom_call_target="tpu_custom_call" | custom-call | tf_op jit(solution)/shard_map/pallas_call | solution.py:280
  107.7 5.8 %all_to_all.15 = bf16[4,4,2,80,512]{4,3,1,0,2:T(8,128)(2,1)S(1)} all-to-all(bf16[4,4,2,80,512]{4,3,1,0,2:T(8,128)(2,1)S(1)} %copy.39), channel_id=1, replica_groups=mesh['section'=4,'y'=4,'z'=4,'core'=2] {'core'}, dimensions={2} | all-to-all | bytes 5242880 | tf_op jit(solution)/shard_map/all_to_all | solution.py:292
  116.9 23.6 %all_to_all.16 = bf16[4,4,80,512]{3,2,0,1:T(8,128)(2,1)S(1)} all-to-all(bf16[4,4,80,512]{3,2,0,1:T(8,128)(2,1)S(1)} %copy.40), channel_id=1, replica_groups=mesh['section'=4,'y'=4,'z'=4,'core'=2] {'z'}, dimensions={1} | all-to-all | bytes 2621440 | tf_op jit(solution)/shard_map/all_to_all | solution.py:292
  140.7 11.3 %all_to_all.17 = bf16[4,80,512]{2,1,0:T(8,128)(2,1)S(1)} all-to-all(bf16[4,80,512]{2,1,0:T(8,128)(2,1)S(1)} %reduce_sum.34), channel_id=1, replica_groups=mesh['section'=4,'y'=4,'z'=4,'core'=2] {'y'}, dimensions={0} | all-to-all | bytes 655360 | tf_op jit(solution)/shard_map/all_to_all | solution.py:292
  (35 shorter events, 17.4 us)
Async XLA Ops:
  13.0 7.6 %collective-permute-start = (bf16[128,512]{1,0:T(8,128)(2,1)}, bf16[128,512]{1,0:T(8,128)(2,1)S(1)}, u32[]{:S(2)}, u32[]{:S(2)}) collective-permute-start(bf16[128,512]{1,0:T(8,128)(2,1)} %get-tuple-element.42), channel_id=1, source_target_pairs={{32,0},{64,32},{96,64},{33,1},{65,33},{97,65},{34,2},{66,34},{98,6... | collective-permute-start | bytes 393224 | tf_op jit(solution)/shard_map/ppermute | solution.py:18
  20.6 0.7 copy-start
  26.6 7.3 %collective-permute-start.1 = (bf16[128,512]{1,0:T(8,128)(2,1)}, bf16[128,512]{1,0:T(8,128)(2,1)S(1)}, u32[]{:S(2)}, u32[]{:S(2)}) collective-permute-start(bf16[128,512]{1,0:T(8,128)(2,1)} %get-tuple-element.47), channel_id=1, source_target_pairs={{32,0},{64,32},{96,64},{33,1},{65,33},{97,65},{34,2},{66,34},{98,6... | collective-permute-start | bytes 393224 | tf_op jit(solution)/shard_map/ppermute | solution.py:18
  34.0 0.7 copy-start.2
  40.0 7.1 %collective-permute-start.2 = (bf16[128,512]{1,0:T(8,128)(2,1)}, bf16[128,512]{1,0:T(8,128)(2,1)S(1)}, u32[]{:S(2)}, u32[]{:S(2)}) collective-permute-start(bf16[128,512]{1,0:T(8,128)(2,1)} %get-tuple-element.52), channel_id=1, source_target_pairs={{32,0},{64,32},{96,64},{33,1},{65,33},{97,65},{34,2},{66,34},{98,6... | collective-permute-start | bytes 393224 | tf_op jit(solution)/shard_map/ppermute | solution.py:18
  47.2 0.7 copy-start.3
  53.2 7.3 %collective-permute-start.3 = (bf16[128,512]{1,0:T(8,128)(2,1)}, bf16[128,512]{1,0:T(8,128)(2,1)S(1)}, u32[]{:S(2)}, u32[]{:S(2)}) collective-permute-start(bf16[128,512]{1,0:T(8,128)(2,1)} %get-tuple-element.57), channel_id=1, source_target_pairs={{32,0},{64,32},{96,64},{33,1},{65,33},{97,65},{34,2},{66,34},{98,6... | collective-permute-start | bytes 393224 | tf_op jit(solution)/shard_map/ppermute | solution.py:18
  60.6 0.7 copy-start.4
  66.6 6.9 %collective-permute-start.4 = (bf16[128,512]{1,0:T(8,128)(2,1)}, bf16[128,512]{1,0:T(8,128)(2,1)S(1)}, u32[]{:S(2)}, u32[]{:S(2)}) collective-permute-start(bf16[128,512]{1,0:T(8,128)(2,1)} %get-tuple-element.62), channel_id=1, source_target_pairs={{32,0},{64,32},{96,64},{33,1},{65,33},{97,65},{34,2},{66,34},{98,6... | collective-permute-start | bytes 393224 | tf_op jit(solution)/shard_map/ppermute | solution.py:18
  73.6 0.7 copy-start.5
  79.6 7.0 %collective-permute-start.5 = (bf16[128,512]{1,0:T(8,128)(2,1)}, bf16[128,512]{1,0:T(8,128)(2,1)S(1)}, u32[]{:S(2)}, u32[]{:S(2)}) collective-permute-start(bf16[128,512]{1,0:T(8,128)(2,1)} %get-tuple-element.67), channel_id=1, source_target_pairs={{32,0},{64,32},{96,64},{33,1},{65,33},{97,65},{34,2},{66,34},{98,6... | collective-permute-start | bytes 393224 | tf_op jit(solution)/shard_map/ppermute | solution.py:18
  86.6 0.7 copy-start.1

commit v6 on v5

--- a/solution.py
+++ b/solution.py
@@ -144,15 +144,23 @@
         rows_out = []
         for tap, moved in shifted_taps(xf, masks, width, 1):
             rows_out.append(jnp.sum(moved * dzed, axis=0, keepdims=True))
-        rows_out.append(jnp.zeros((pad_taps - taps, chans), jnp.float32))
-        depth.append(jnp.concatenate(rows_out, axis=0) * scale)
+        main = jnp.concatenate(rows_out[:pad_taps], axis=0) * scale
+        extra = jnp.broadcast_to(rows_out[pad_taps] * scale, (pad_taps, chans))
+        depth.append((main, extra))
     lane = lax.broadcasted_iota(jnp.int32, (pad_taps, chans), 1)
+    row = lax.broadcasted_iota(jnp.int32, (pad_taps, chans), 0)
     for d in range(replicas):
         slot = jnp.zeros((pad_taps, chans), jnp.float32)
         for layer in range(layers):
+            main, extra = depth[layer]
             amount = (layer * share - d * share) % chans
-            moved = depth[layer] if amount == 0 else pltpu.roll(depth[layer], amount, 1)
+            moved = main if amount == 0 else pltpu.roll(main, amount, 1)
             keep = (lane >= layer * share) & (lane < (layer + 1) * share)
+            slot = jnp.where(keep, moved, slot)
+            start = layers * share + layer * share
+            amount = (start - d * share) % chans
+            moved = extra if amount == 0 else pltpu.roll(extra, amount, 1)
+            keep = (row == 0) & (lane >= start) & (lane < start + share)
             slot = jnp.where(keep, moved, slot)
         send_ref[np.unravel_index(d, lead) + (slice(layers * share, None),)] = slot.astype(
             jnp.bfloat16
@@ -161,7 +169,7 @@
 
 def body(section_inputs, grad_out, point_weights, depth_weights):
     sections = lax.axis_size("section")
-    lead = (lax.axis_size("y"), lax.axis_size("z"), lax.axis_size("core"))
+    lead = (lax.axis_size("chip"), lax.axis_size("core"))
     replicas = math.prod(lead)
     my_section = lax.axis_index("section")
     batches = grad_out.shape[0]
@@ -275,7 +283,7 @@
     count = batches * images * replicas * height * width
     scale = 1.0 / float(count) ** 0.5
     share = chans // replicas
-    pad_taps = -(-taps // 16) * 16
+    pad_taps = taps - 1
     first = jnp.reshape(sections - 1 - my_section, (1,)).astype(jnp.int32)
     send, res = pl.pallas_call(
         functools.partial(grad_kernel, height=height, width=width, scale=scale),
@@ -288,14 +296,17 @@
         compiler_params=params,
     )(first, hbuf, acts, xs, zs, weights, kerns)
     part = send
-    for axis, name in reversed(list(enumerate(("y", "z", "core")))):
+    for axis, name in reversed(list(enumerate(("chip", "core")))):
         part = lax.all_to_all(part, name, axis, axis, tiled=True)
         part = jnp.sum(part.astype(jnp.float32), axis=axis)
         if axis:
             part = part.astype(jnp.bfloat16)
     summed = part
     point_red = summed[: layers * share].reshape(layers, share, chans)
-    depth_red = summed[layers * share : layers * share + taps, : layers * share]
+    dk_rows = summed[layers * share : layers * share + pad_taps]
+    depth_red = jnp.concatenate(
+        [dk_rows[:, : layers * share], dk_rows[:1, layers * share : 2 * layers * share]], axis=0
+    )
     depth_red = depth_red.reshape(taps, layers, share).transpose(1, 0, 2)
     results = res.reshape(inputs.shape)
     return (results[None], point_red[None], depth_red[None])
@@ -303,15 +314,8 @@
 
 def solution(mesh):
     sections, replicas = mesh.devices.shape
-    try:
-        zsize = len({d.coords[2] for d in mesh.devices[0]})
-    except (AttributeError, IndexError, TypeError):
-        zsize = 1
-    split = Mesh(
-        mesh.devices.reshape(sections, replicas // (2 * zsize), zsize, 2),
-        ("section", "y", "z", "core"),
-    )
-    dp = ("y", "z", "core")
+    split = Mesh(mesh.devices.reshape(sections, replicas // 2, 2), ("section", "chip", "core"))
+    dp = ("chip", "core")
     return jax.shard_map(
         body,
         mesh=split,

time: 154 us -> 143 us (0.929)
  blocking collectives: 40.7 us -> 32.3 us
    all_to_all x3 -> x2, blocking collectives: 40.7 us -> 32.3 us  [body(): part = lax.all_to_all(part, name, axis, axis, tiled=True)]
  transfers between devices with their start and end apart: 6 -> 6, of which waited for: 0 -> 0; matrix products, arithmetic and copies ran while one was open for 2% -> 3% of each run, Pallas kernels for 16% -> 17%
where the time goes in v6:
time: 143 us
  Pallas kernels  79.8 us (56%)
  blocking collectives  32.3 us (23%)
  starting transfers between devices  14.8 us (10%)
  local copies, waits for them, and re-layouts  7.85 us (5%)
  other arithmetic  7.06 us (5%)
    pallas_call x7, Pallas kernels, body(): pl.pallas_call(functools.partial(step_kernel, height=height, width=width)...  37.7 us
    all_to_all x2, blocking collectives, body(): part = lax.all_to_all(part, name, axis, axis, tiled=True)  32.3 us
    pallas_call x6, Pallas kernels, body(): pl.pallas_call(functools.partial(fwd_kernel, height=height, width=width),...  24.9 us
    ppermute x6, starting transfers between devices, from_behind(): return lax.ppermute(shard, axis, pairs)  14.8 us
    pallas_call x1, Pallas kernels, body(): pl.pallas_call(functools.partial(grad_kernel, height=height, width=width,...  13 us
    another operation x7, other arithmetic, body(): scalars = jnp.stack([picked, is_last, valid]).astype(jnp.int32)  4.23 us
    pallas_call x1, Pallas kernels, body(): pl.pallas_call(functools.partial(fwd_first_kernel, height=height, width=w...  4.19 us
    unnamed x12, local copies, waits for them, and re-layouts  3.93 us
  transfers between devices with their start and end apart: 6, of which 0 were waited for; matrix products, arithmetic and copies ran while one was open for 3% of the time, Pallas kernels for 17%

profile of v6, /device:TPU:6, one launch (start us, length us, event | category | flops | bytes accessed | tf_op | source)
XLA Modules:
  0.0 142.5 jit_solution(8535335889164118043)
XLA Ops:
  2.7 4.2 %shard_map.67 = (f32[4,4,128,512]{3,2,1,0:T(8,128)}, bf16[4,4,128,512]{3,2,1,0:T(8,128)(2,1)}, bf16[4,4,128,512]{3,2,1,0:T(8,128)(2,1)}, bf16[5,7,128,512]{3,2,1,0:T(8,128)(2,1)}) custom-call(s32[1]{0:T(128)} %bitcast.15.p_ref, bf16[4,128,512]{2,1,0:T(8,128)(2,1)} %bitcast.55, bf16[4,512,512]{2,1,0:T(8,128)(2,1)} %bitcast.31, ...), custom_call_target="tpu_custom_call" | custom-call | flops 282591232 | bytes 4194304 | tf_op jit(solution)/shard_map/pallas_call | solution.py:215
  7.5 5.4 %shard_map.68 = (bf16[128,512]{1,0:T(8,128)(2,1)}, bf16[5,7,128,512]{3,2,1,0:T(8,128)(2,1)}) custom-call(s32[3]{0:T(128)} %pad_add_fusion.6.p_ref, bf16[4,128,512]{2,1,0:T(8,128)(2,1)} %bitcast.48, bf16[128,512]{1,0:T(8,128)(2,1)} %broadcast_in_dim.6.car_ref, f32[4,4,128,512]{3,2,1,0:T(8,128)} %get-tuple-element.40.z_ref.refs_0_, ...), custom_call_target="tpu_custom_call", output_to_operand_aliasing={{1}: (6, {})} | custom-call | flops 282591232 | bytes 4194304 | tf_op jit(solution)/shard_map/pallas_call | solution.py:252
  12.9 2.7 %collective-permute-start = (bf16[128,512]{1,0:T(8,128)(2,1)}, bf16[128,512]{1,0:T(8,128)(2,1)S(1)}, u32[]{:S(2)}, u32[]{:S(2)}) collective-permute-start(bf16[128,512]{1,0:T(8,128)(2,1)} %get-tuple-element.42), channel_id=1, source_target_pairs={{32,0},{64,32},{96,64},{33,1},{65,33},{97,65},{34,2},{66,34},{98,6... | collective-permute-start | bytes 393224 | tf_op jit(solution)/shard_map/ppermute | solution.py:18
  15.7 4.2 %shard_map.69 = (f32[4,4,128,512]{3,2,1,0:T(8,128)}, bf16[4,4,128,512]{3,2,1,0:T(8,128)(2,1)}, bf16[4,4,128,512]{3,2,1,0:T(8,128)(2,1)}) custom-call(s32[1]{0:T(128)} %bitcast.13.p_ref, bf16[4,128,512]{2,1,0:T(8,128)(2,1)} %bitcast.56, bf16[4,512,512]{2,1,0:T(8,128)(2,1)} %bitcast.33, ...), custom_call_target="tpu_custom_call", output_to_operand_aliasing={{0}: (4, {}), {1}: (5, {}), {2}: (6, {})} | custom-call | flops 282591232 | bytes 4194304 | tf_op jit(solution)/shard_map/pallas_call | solution.py:266
  21.1 5.4 %shard_map.70 = (bf16[128,512]{1,0:T(8,128)(2,1)}, bf16[5,7,128,512]{3,2,1,0:T(8,128)(2,1)}) custom-call(s32[3]{0:T(128)} %pad_add_fusion.5.p_ref, bf16[4,128,512]{2,1,0:T(8,128)(2,1)} %bitcast.49, bf16[128,512]{1,0:T(8,128)(2,1)} %copy-done, f32[4,4,128,512]{3,2,1,0:T(8,128)} %get-tuple-element.45.z_ref.refs_0_, ...), custom_call_target="tpu_custom_call", output_to_operand_aliasing={{1}: (6, {})} | custom-call | flops 282591232 | bytes 4194304 | tf_op jit(solution)/shard_map/pallas_call | solution.py:252
  26.5 2.5 %collective-permute-start.1 = (bf16[128,512]{1,0:T(8,128)(2,1)}, bf16[128,512]{1,0:T(8,128)(2,1)S(1)}, u32[]{:S(2)}, u32[]{:S(2)}) collective-permute-start(bf16[128,512]{1,0:T(8,128)(2,1)} %get-tuple-element.47), channel_id=1, source_target_pairs={{32,0},{64,32},{96,64},{33,1},{65,33},{97,65},{34,2},{66,34},{98,6... | collective-permute-start | bytes 393224 | tf_op jit(solution)/shard_map/ppermute | solution.py:18
  29.6 4.2 %shard_map.71 = (f32[4,4,128,512]{3,2,1,0:T(8,128)}, bf16[4,4,128,512]{3,2,1,0:T(8,128)(2,1)}, bf16[4,4,128,512]{3,2,1,0:T(8,128)(2,1)}) custom-call(s32[1]{0:T(128)} %bitcast.11.p_ref, bf16[4,128,512]{2,1,0:T(8,128)(2,1)} %bitcast.57, bf16[4,512,512]{2,1,0:T(8,128)(2,1)} %bitcast.35, ...), custom_call_target="tpu_custom_call", output_to_operand_aliasing={{0}: (4, {}), {1}: (5, {}), {2}: (6, {})} | custom-call | flops 282591232 | bytes 4194304 | tf_op jit(solution)/shard_map/pallas_call | solution.py:266
  34.4 5.4 %shard_map.72 = (bf16[128,512]{1,0:T(8,128)(2,1)}, bf16[5,7,128,512]{3,2,1,0:T(8,128)(2,1)}) custom-call(s32[3]{0:T(128)} %pad_add_fusion.4.p_ref, bf16[4,128,512]{2,1,0:T(8,128)(2,1)} %bitcast.50, bf16[128,512]{1,0:T(8,128)(2,1)} %copy-done.2, f32[4,4,128,512]{3,2,1,0:T(8,128)} %get-tuple-element.50.z_ref.refs_0_, ...), custom_call_target="tpu_custom_call", output_to_operand_aliasing={{1}: (6, {})} | custom-call | flops 282591232 | bytes 4194304 | tf_op jit(solution)/shard_map/pallas_call | solution.py:252
  39.8 2.4 %collective-permute-start.2 = (bf16[128,512]{1,0:T(8,128)(2,1)}, bf16[128,512]{1,0:T(8,128)(2,1)S(1)}, u32[]{:S(2)}, u32[]{:S(2)}) collective-permute-start(bf16[128,512]{1,0:T(8,128)(2,1)} %get-tuple-element.52), channel_id=1, source_target_pairs={{32,0},{64,32},{96,64},{33,1},{65,33},{97,65},{34,2},{66,34},{98,6... | collective-permute-start | bytes 393224 | tf_op jit(solution)/shard_map/ppermute | solution.py:18
  42.9 4.1 %shard_map.73 = (f32[4,4,128,512]{3,2,1,0:T(8,128)}, bf16[4,4,128,512]{3,2,1,0:T(8,128)(2,1)}, bf16[4,4,128,512]{3,2,1,0:T(8,128)(2,1)}) custom-call(s32[1]{0:T(128)} %bitcast.9.p_ref, bf16[4,128,512]{2,1,0:T(8,128)(2,1)} %bitcast.58, bf16[4,512,512]{2,1,0:T(8,128)(2,1)} %bitcast.37, ...), custom_call_target="tpu_custom_call", output_to_operand_aliasing={{0}: (4, {}), {1}: (5, {}), {2}: (6, {})} | custom-call | flops 282591232 | bytes 4194304 | tf_op jit(solution)/shard_map/pallas_call | solution.py:266
  47.7 5.4 %shard_map.74 = (bf16[128,512]{1,0:T(8,128)(2,1)}, bf16[5,7,128,512]{3,2,1,0:T(8,128)(2,1)}) custom-call(s32[3]{0:T(128)} %pad_add_fusion.3.p_ref, bf16[4,128,512]{2,1,0:T(8,128)(2,1)} %bitcast.51, bf16[128,512]{1,0:T(8,128)(2,1)} %copy-done.3, f32[4,4,128,512]{3,2,1,0:T(8,128)} %get-tuple-element.55.z_ref.refs_0_, ...), custom_call_target="tpu_custom_call", output_to_operand_aliasing={{1}: (6, {})} | custom-call | flops 282591232 | bytes 4194304 | tf_op jit(solution)/shard_map/pallas_call | solution.py:252
  53.0 2.5 %collective-permute-start.3 = (bf16[128,512]{1,0:T(8,128)(2,1)}, bf16[128,512]{1,0:T(8,128)(2,1)S(1)}, u32[]{:S(2)}, u32[]{:S(2)}) collective-permute-start(bf16[128,512]{1,0:T(8,128)(2,1)} %get-tuple-element.57), channel_id=1, source_target_pairs={{32,0},{64,32},{96,64},{33,1},{65,33},{97,65},{34,2},{66,34},{98,6... | collective-permute-start | bytes 393224 | tf_op jit(solution)/shard_map/ppermute | solution.py:18
  56.2 4.1 %shard_map.75 = (f32[4,4,128,512]{3,2,1,0:T(8,128)}, bf16[4,4,128,512]{3,2,1,0:T(8,128)(2,1)}, bf16[4,4,128,512]{3,2,1,0:T(8,128)(2,1)}) custom-call(s32[1]{0:T(128)} %bitcast.7.p_ref, bf16[4,128,512]{2,1,0:T(8,128)(2,1)} %bitcast.59, bf16[4,512,512]{2,1,0:T(8,128)(2,1)} %bitcast.39, ...), custom_call_target="tpu_custom_call", output_to_operand_aliasing={{0}: (4, {}), {1}: (5, {}), {2}: (6, {})} | custom-call | flops 282591232 | bytes 4194304 | tf_op jit(solution)/shard_map/pallas_call | solution.py:266
  61.0 5.4 %shard_map.76 = (bf16[128,512]{1,0:T(8,128)(2,1)}, bf16[5,7,128,512]{3,2,1,0:T(8,128)(2,1)}) custom-call(s32[3]{0:T(128)} %pad_add_fusion.2.p_ref, bf16[4,128,512]{2,1,0:T(8,128)(2,1)} %bitcast.52, bf16[128,512]{1,0:T(8,128)(2,1)} %copy-done.4, f32[4,4,128,512]{3,2,1,0:T(8,128)} %get-tuple-element.60.z_ref.refs_0_, ...), custom_call_target="tpu_custom_call", output_to_operand_aliasing={{1}: (6, {})} | custom-call | flops 282591232 | bytes 4194304 | tf_op jit(solution)/shard_map/pallas_call | solution.py:252
  66.4 2.3 %collective-permute-start.4 = (bf16[128,512]{1,0:T(8,128)(2,1)}, bf16[128,512]{1,0:T(8,128)(2,1)S(1)}, u32[]{:S(2)}, u32[]{:S(2)}) collective-permute-start(bf16[128,512]{1,0:T(8,128)(2,1)} %get-tuple-element.62), channel_id=1, source_target_pairs={{32,0},{64,32},{96,64},{33,1},{65,33},{97,65},{34,2},{66,34},{98,6... | collective-permute-start | bytes 393224 | tf_op jit(solution)/shard_map/ppermute | solution.py:18
  69.2 4.1 %shard_map.77 = (f32[4,4,128,512]{3,2,1,0:T(8,128)}, bf16[4,4,128,512]{3,2,1,0:T(8,128)(2,1)}, bf16[4,4,128,512]{3,2,1,0:T(8,128)(2,1)}) custom-call(s32[1]{0:T(128)} %bitcast.5.p_ref, bf16[4,128,512]{2,1,0:T(8,128)(2,1)} %bitcast.60, bf16[4,512,512]{2,1,0:T(8,128)(2,1)} %bitcast.41, ...), custom_call_target="tpu_custom_call", output_to_operand_aliasing={{0}: (4, {}), {1}: (5, {}), {2}: (6, {})} | custom-call | flops 282591232 | bytes 4194304 | tf_op jit(solution)/shard_map/pallas_call | solution.py:266
  74.0 5.4 %shard_map.78 = (bf16[128,512]{1,0:T(8,128)(2,1)}, bf16[5,7,128,512]{3,2,1,0:T(8,128)(2,1)}) custom-call(s32[3]{0:T(128)} %pad_add_fusion.1.p_ref, bf16[4,128,512]{2,1,0:T(8,128)(2,1)} %bitcast.53, bf16[128,512]{1,0:T(8,128)(2,1)} %copy-done.5, f32[4,4,128,512]{3,2,1,0:T(8,128)} %get-tuple-element.65.z_ref.refs_0_, ...), custom_call_target="tpu_custom_call", output_to_operand_aliasing={{1}: (6, {})} | custom-call | flops 282591232 | bytes 4194304 | tf_op jit(solution)/shard_map/pallas_call | solution.py:252
  79.4 2.3 %collective-permute-start.5 = (bf16[128,512]{1,0:T(8,128)(2,1)}, bf16[128,512]{1,0:T(8,128)(2,1)S(1)}, u32[]{:S(2)}, u32[]{:S(2)}) collective-permute-start(bf16[128,512]{1,0:T(8,128)(2,1)} %get-tuple-element.67), channel_id=1, source_target_pairs={{32,0},{64,32},{96,64},{33,1},{65,33},{97,65},{34,2},{66,34},{98,6... | collective-permute-start | bytes 393224 | tf_op jit(solution)/shard_map/ppermute | solution.py:18
  82.4 4.1 %shard_map.79 = (f32[4,4,128,512]{3,2,1,0:T(8,128)}, bf16[4,4,128,512]{3,2,1,0:T(8,128)(2,1)}, bf16[4,4,128,512]{3,2,1,0:T(8,128)(2,1)}) custom-call(s32[1]{0:T(128)} %bitcast.1.p_ref, bf16[4,128,512]{2,1,0:T(8,128)(2,1)} %bitcast.61, bf16[4,512,512]{2,1,0:T(8,128)(2,1)} %bitcast.43, ...), custom_call_target="tpu_custom_call", output_to_operand_aliasing={{0}: (4, {}), {1}: (5, {}), {2}: (6, {})} | custom-call | flops 282591232 | bytes 4194304 | tf_op jit(solution)/shard_map/pallas_call | solution.py:266
  87.2 5.4 %shard_map.80 = (bf16[128,512]{1,0:T(8,128)(2,1)}, bf16[5,7,128,512]{3,2,1,0:T(8,128)(2,1)}) custom-call(s32[3]{0:T(128)} %pad_add_fusion.p_ref, bf16[4,128,512]{2,1,0:T(8,128)(2,1)} %bitcast.54, bf16[128,512]{1,0:T(8,128)(2,1)} %copy-done.1, f32[4,4,128,512]{3,2,1,0:T(8,128)} %get-tuple-element.70.z_ref, ...), custom_call_target="tpu_custom_call", output_to_operand_aliasing={{1}: (6, {})} | custom-call | flops 282591232 | bytes 4194304 | tf_op jit(solution)/shard_map/pallas_call | solution.py:252
  92.5 13.0 %shard_map.81 = (bf16[16,2,72,512]{3,2,1,0:T(8,128)(2,1)}, bf16[4,128,512]{2,1,0:T(8,128)(2,1)}) custom-call(s32[1]{0:T(128)} %bitcast.p_ref, bf16[5,7,128,512]{3,2,1,0:T(8,128)(2,1)} %get-tuple-element.72.h_ref, bf16[4,512,512]{2,1,0:T(8,128)(2,1)} %bitcast.46, bf16[4,512,512]{2,1,0:T(8,128)(2,1)} %bitcast.47, f32[4,512,512]{2,1,0:T(8,128)} %bitcast.30, ...), custom_call_target="tpu_custom_call" | custom-call | tf_op jit(solution)/shard_map/pallas_call | solution.py:288
  105.6 1.8 %copy.36 = bf16[16,2,72,512]{3,2,0,1:T(8,128)(2,1)S(1)} copy(bf16[16,2,72,512]{3,2,1,0:T(8,128)(2,1)} %get-tuple-element.76) | data formatting | bytes 4718592 | tf_op jit(solution)/shard_map/pallas_call | solution.py:288
  107.4 5.6 %all_to_all.10 = bf16[16,2,72,512]{3,2,0,1:T(8,128)(2,1)S(1)} all-to-all(bf16[16,2,72,512]{3,2,0,1:T(8,128)(2,1)S(1)} %copy.36), channel_id=1, replica_groups=mesh['section'=4,'chip'=16,'core'=2] {'core'}, dimensions={1} | all-to-all | bytes 4718592 | tf_op jit(solution)/shard_map/all_to_all | solution.py:300
  114.2 26.7 %all_to_all.11 = bf16[16,72,512]{2,1,0:T(8,128)(2,1)S(1)} all-to-all(bf16[16,72,512]{2,1,0:T(8,128)(2,1)S(1)} %reduce_sum.21), channel_id=1, replica_groups=mesh['section'=4,'chip'=16,'core'=2] {'chip'}, dimensions={0} | all-to-all | bytes 2359296 | tf_op jit(solution)/shard_map/all_to_all | solution.py:300
  (34 shorter events, 13.1 us)
Async XLA Ops:
  12.9 7.5 %collective-permute-start = (bf16[128,512]{1,0:T(8,128)(2,1)}, bf16[128,512]{1,0:T(8,128)(2,1)S(1)}, u32[]{:S(2)}, u32[]{:S(2)}) collective-permute-start(bf16[128,512]{1,0:T(8,128)(2,1)} %get-tuple-element.42), channel_id=1, source_target_pairs={{32,0},{64,32},{96,64},{33,1},{65,33},{97,65},{34,2},{66,34},{98,6... | collective-permute-start | bytes 393224 | tf_op jit(solution)/shard_map/ppermute | solution.py:18
  20.4 0.7 copy-start
  26.5 7.3 %collective-permute-start.1 = (bf16[128,512]{1,0:T(8,128)(2,1)}, bf16[128,512]{1,0:T(8,128)(2,1)S(1)}, u32[]{:S(2)}, u32[]{:S(2)}) collective-permute-start(bf16[128,512]{1,0:T(8,128)(2,1)} %get-tuple-element.47), channel_id=1, source_target_pairs={{32,0},{64,32},{96,64},{33,1},{65,33},{97,65},{34,2},{66,34},{98,6... | collective-permute-start | bytes 393224 | tf_op jit(solution)/shard_map/ppermute | solution.py:18
  33.8 0.7 copy-start.2
  39.8 7.2 %collective-permute-start.2 = (bf16[128,512]{1,0:T(8,128)(2,1)}, bf16[128,512]{1,0:T(8,128)(2,1)S(1)}, u32[]{:S(2)}, u32[]{:S(2)}) collective-permute-start(bf16[128,512]{1,0:T(8,128)(2,1)} %get-tuple-element.52), channel_id=1, source_target_pairs={{32,0},{64,32},{96,64},{33,1},{65,33},{97,65},{34,2},{66,34},{98,6... | collective-permute-start | bytes 393224 | tf_op jit(solution)/shard_map/ppermute | solution.py:18
  47.0 0.7 copy-start.3
  53.0 7.3 %collective-permute-start.3 = (bf16[128,512]{1,0:T(8,128)(2,1)}, bf16[128,512]{1,0:T(8,128)(2,1)S(1)}, u32[]{:S(2)}, u32[]{:S(2)}) collective-permute-start(bf16[128,512]{1,0:T(8,128)(2,1)} %get-tuple-element.57), channel_id=1, source_target_pairs={{32,0},{64,32},{96,64},{33,1},{65,33},{97,65},{34,2},{66,34},{98,6... | collective-permute-start | bytes 393224 | tf_op jit(solution)/shard_map/ppermute | solution.py:18
  60.3 0.7 copy-start.4
  66.4 7.0 %collective-permute-start.4 = (bf16[128,512]{1,0:T(8,128)(2,1)}, bf16[128,512]{1,0:T(8,128)(2,1)S(1)}, u32[]{:S(2)}, u32[]{:S(2)}) collective-permute-start(bf16[128,512]{1,0:T(8,128)(2,1)} %get-tuple-element.62), channel_id=1, source_target_pairs={{32,0},{64,32},{96,64},{33,1},{65,33},{97,65},{34,2},{66,34},{98,6... | collective-permute-start | bytes 393224 | tf_op jit(solution)/shard_map/ppermute | solution.py:18
  73.4 0.7 copy-start.5
  79.4 7.1 %collective-permute-start.5 = (bf16[128,512]{1,0:T(8,128)(2,1)}, bf16[128,512]{1,0:T(8,128)(2,1)S(1)}, u32[]{:S(2)}, u32[]{:S(2)}) collective-permute-start(bf16[128,512]{1,0:T(8,128)(2,1)} %get-tuple-element.67), channel_id=1, source_target_pairs={{32,0},{64,32},{96,64},{33,1},{65,33},{97,65},{34,2},{66,34},{98,6... | collective-permute-start | bytes 393224 | tf_op jit(solution)/shard_map/ppermute | solution.py:18
  86.5 0.7 copy-start.1

commit v7 on v6

--- a/solution.py
+++ b/solution.py
@@ -137,7 +137,7 @@
         )
         point = point * scale
         for d in range(replicas):
-            send_ref[np.unravel_index(d, lead) + (slice(layer * share, (layer + 1) * share),)] = point[
+            send_ref[(d % lead[0], d // lead[0], slice(layer * share, (layer + 1) * share))] = point[
                 d * share : (d + 1) * share
             ].astype(jnp.bfloat16)
         xf = xs_ref[layer].astype(jnp.float32)
@@ -162,14 +162,14 @@
             moved = extra if amount == 0 else pltpu.roll(extra, amount, 1)
             keep = (row == 0) & (lane >= start) & (lane < start + share)
             slot = jnp.where(keep, moved, slot)
-        send_ref[np.unravel_index(d, lead) + (slice(layers * share, None),)] = slot.astype(
+        send_ref[(d % lead[0], d // lead[0], slice(layers * share, None))] = slot.astype(
             jnp.bfloat16
         )
 
 
 def body(section_inputs, grad_out, point_weights, depth_weights):
     sections = lax.axis_size("section")
-    lead = (lax.axis_size("chip"), lax.axis_size("core"))
+    lead = (lax.axis_size("core"), lax.axis_size("chip"))
     replicas = math.prod(lead)
     my_section = lax.axis_index("section")
     batches = grad_out.shape[0]
@@ -296,10 +296,10 @@
         compiler_params=params,
     )(first, hbuf, acts, xs, zs, weights, kerns)
     part = send
-    for axis, name in reversed(list(enumerate(("chip", "core")))):
-        part = lax.all_to_all(part, name, axis, axis, tiled=True)
-        part = jnp.sum(part.astype(jnp.float32), axis=axis)
-        if axis:
+    for stage, name in enumerate(("core", "chip")):
+        part = lax.all_to_all(part, name, 0, 0, tiled=True)
+        part = jnp.sum(part.astype(jnp.float32), axis=0)
+        if stage == 0:
             part = part.astype(jnp.bfloat16)
     summed = part
     point_red = summed[: layers * share].reshape(layers, share, chans)

time: 143 us -> 143 us (level)
  local copies, waits for them, and re-layouts: 7.85 us -> 6.03 us
    pallas_call x1 -> x0, local copies, waits for them, and re-layouts: 1.82 us -> none  [body(): pl.pallas_call(functools.partial(grad_kernel, height=height, width=width,...]
  transfers between devices with their start and end apart: 6 -> 6, of which waited for: 0 -> 0; matrix products, arithmetic and copies ran while one was open for 3% -> 3% of each run, Pallas kernels for 17% -> 18%
where the time goes in v7:
time: 143 us; the launch traced here: 142 us
  Pallas kernels  79.8 us (56%)
  blocking collectives  33.5 us (23%)
  starting transfers between devices  14.8 us (10%)
  other arithmetic  7.06 us (5%)
  local copies, waits for them, and re-layouts  6.03 us (4%)
    pallas_call x7, Pallas kernels, body(): pl.pallas_call(functools.partial(step_kernel, height=height, width=width)...  37.7 us
    all_to_all x2, blocking collectives, body(): part = lax.all_to_all(part, name, 0, 0, tiled=True)  33.5 us
    pallas_call x6, Pallas kernels, body(): pl.pallas_call(functools.partial(fwd_kernel, height=height, width=width),...  24.9 us
    ppermute x6, starting transfers between devices, from_behind(): return lax.ppermute(shard, axis, pairs)  14.8 us
    pallas_call x1, Pallas kernels, body(): pl.pallas_call(functools.partial(grad_kernel, height=height, width=width,...  13 us
    another operation x7, other arithmetic, body(): scalars = jnp.stack([picked, is_last, valid]).astype(jnp.int32)  4.23 us
    pallas_call x1, Pallas kernels, body(): pl.pallas_call(functools.partial(fwd_first_kernel, height=height, width=w...  4.19 us
    unnamed x12, local copies, waits for them, and re-layouts  3.93 us
  transfers between devices with their start and end apart: 6, of which 0 were waited for; matrix products, arithmetic and copies ran while one was open for 3% of the time, Pallas kernels for 18%

profile of v7, /device:TPU:6, one launch (start us, length us, event | category | flops | bytes accessed | tf_op | source)
XLA Modules:
  0.0 141.9 jit_solution(16801870674469358559)
XLA Ops:
  0.6 1.4 %bitcast_convert_fusion.k_ref = f32[4,9,512]{2,1,0:T(8,128)} fusion(bf16[1,4,9,512]{3,1,2,0:T(4,128)(2,1)} %param.7), kind=kLoop, calls=%fused_computation.1 | loop fusion | flops 18432 | bytes 110592 | tf_op jit(solution)/shard_map/convert_element_type | solution.py:183
  2.7 4.2 %shard_map.67 = (f32[4,4,128,512]{3,2,1,0:T(8,128)}, bf16[4,4,128,512]{3,2,1,0:T(8,128)(2,1)}, bf16[4,4,128,512]{3,2,1,0:T(8,128)(2,1)}, bf16[5,7,128,512]{3,2,1,0:T(8,128)(2,1)}) custom-call(s32[1]{0:T(128)} %bitcast.15.p_ref, bf16[4,128,512]{2,1,0:T(8,128)(2,1)} %bitcast.55, bf16[4,512,512]{2,1,0:T(8,128)(2,1)} %bitcast.31, ...), custom_call_target="tpu_custom_call" | custom-call | flops 282591232 | bytes 4194304 | tf_op jit(solution)/shard_map/pallas_call | solution.py:215
  7.5 5.4 %shard_map.68 = (bf16[128,512]{1,0:T(8,128)(2,1)}, bf16[5,7,128,512]{3,2,1,0:T(8,128)(2,1)}) custom-call(s32[3]{0:T(128)} %pad_add_fusion.6.p_ref, bf16[4,128,512]{2,1,0:T(8,128)(2,1)} %bitcast.48, bf16[128,512]{1,0:T(8,128)(2,1)} %broadcast_in_dim.6.car_ref, f32[4,4,128,512]{3,2,1,0:T(8,128)} %get-tuple-element.40.z_ref.refs_0_, ...), custom_call_target="tpu_custom_call", output_to_operand_aliasing={{1}: (6, {})} | custom-call | flops 282591232 | bytes 4194304 | tf_op jit(solution)/shard_map/pallas_call | solution.py:252
  12.9 2.7 %collective-permute-start = (bf16[128,512]{1,0:T(8,128)(2,1)}, bf16[128,512]{1,0:T(8,128)(2,1)S(1)}, u32[]{:S(2)}, u32[]{:S(2)}) collective-permute-start(bf16[128,512]{1,0:T(8,128)(2,1)} %get-tuple-element.42), channel_id=1, source_target_pairs={{32,0},{64,32},{96,64},{33,1},{65,33},{97,65},{34,2},{66,34},{98,6... | collective-permute-start | bytes 393224 | tf_op jit(solution)/shard_map/ppermute | solution.py:18
  15.7 4.2 %shard_map.69 = (f32[4,4,128,512]{3,2,1,0:T(8,128)}, bf16[4,4,128,512]{3,2,1,0:T(8,128)(2,1)}, bf16[4,4,128,512]{3,2,1,0:T(8,128)(2,1)}) custom-call(s32[1]{0:T(128)} %bitcast.13.p_ref, bf16[4,128,512]{2,1,0:T(8,128)(2,1)} %bitcast.56, bf16[4,512,512]{2,1,0:T(8,128)(2,1)} %bitcast.33, ...), custom_call_target="tpu_custom_call", output_to_operand_aliasing={{0}: (4, {}), {1}: (5, {}), {2}: (6, {})} | custom-call | flops 282591232 | bytes 4194304 | tf_op jit(solution)/shard_map/pallas_call | solution.py:266
  21.1 5.4 %shard_map.70 = (bf16[128,512]{1,0:T(8,128)(2,1)}, bf16[5,7,128,512]{3,2,1,0:T(8,128)(2,1)}) custom-call(s32[3]{0:T(128)} %pad_add_fusion.5.p_ref, bf16[4,128,512]{2,1,0:T(8,128)(2,1)} %bitcast.49, bf16[128,512]{1,0:T(8,128)(2,1)} %copy-done, f32[4,4,128,512]{3,2,1,0:T(8,128)} %get-tuple-element.45.z_ref.refs_0_, ...), custom_call_target="tpu_custom_call", output_to_operand_aliasing={{1}: (6, {})} | custom-call | flops 282591232 | bytes 4194304 | tf_op jit(solution)/shard_map/pallas_call | solution.py:252
  26.5 2.5 %collective-permute-start.1 = (bf16[128,512]{1,0:T(8,128)(2,1)}, bf16[128,512]{1,0:T(8,128)(2,1)S(1)}, u32[]{:S(2)}, u32[]{:S(2)}) collective-permute-start(bf16[128,512]{1,0:T(8,128)(2,1)} %get-tuple-element.47), channel_id=1, source_target_pairs={{32,0},{64,32},{96,64},{33,1},{65,33},{97,65},{34,2},{66,34},{98,6... | collective-permute-start | bytes 393224 | tf_op jit(solution)/shard_map/ppermute | solution.py:18
  29.6 4.2 %shard_map.71 = (f32[4,4,128,512]{3,2,1,0:T(8,128)}, bf16[4,4,128,512]{3,2,1,0:T(8,128)(2,1)}, bf16[4,4,128,512]{3,2,1,0:T(8,128)(2,1)}) custom-call(s32[1]{0:T(128)} %bitcast.11.p_ref, bf16[4,128,512]{2,1,0:T(8,128)(2,1)} %bitcast.57, bf16[4,512,512]{2,1,0:T(8,128)(2,1)} %bitcast.35, ...), custom_call_target="tpu_custom_call", output_to_operand_aliasing={{0}: (4, {}), {1}: (5, {}), {2}: (6, {})} | custom-call | flops 282591232 | bytes 4194304 | tf_op jit(solution)/shard_map/pallas_call | solution.py:266
  34.4 5.4 %shard_map.72 = (bf16[128,512]{1,0:T(8,128)(2,1)}, bf16[5,7,128,512]{3,2,1,0:T(8,128)(2,1)}) custom-call(s32[3]{0:T(128)} %pad_add_fusion.4.p_ref, bf16[4,128,512]{2,1,0:T(8,128)(2,1)} %bitcast.50, bf16[128,512]{1,0:T(8,128)(2,1)} %copy-done.2, f32[4,4,128,512]{3,2,1,0:T(8,128)} %get-tuple-element.50.z_ref.refs_0_, ...), custom_call_target="tpu_custom_call", output_to_operand_aliasing={{1}: (6, {})} | custom-call | flops 282591232 | bytes 4194304 | tf_op jit(solution)/shard_map/pallas_call | solution.py:252
  39.8 2.4 %collective-permute-start.2 = (bf16[128,512]{1,0:T(8,128)(2,1)}, bf16[128,512]{1,0:T(8,128)(2,1)S(1)}, u32[]{:S(2)}, u32[]{:S(2)}) collective-permute-start(bf16[128,512]{1,0:T(8,128)(2,1)} %get-tuple-element.52), channel_id=1, source_target_pairs={{32,0},{64,32},{96,64},{33,1},{65,33},{97,65},{34,2},{66,34},{98,6... | collective-permute-start | bytes 393224 | tf_op jit(solution)/shard_map/ppermute | solution.py:18
  42.9 4.1 %shard_map.73 = (f32[4,4,128,512]{3,2,1,0:T(8,128)}, bf16[4,4,128,512]{3,2,1,0:T(8,128)(2,1)}, bf16[4,4,128,512]{3,2,1,0:T(8,128)(2,1)}) custom-call(s32[1]{0:T(128)} %bitcast.9.p_ref, bf16[4,128,512]{2,1,0:T(8,128)(2,1)} %bitcast.58, bf16[4,512,512]{2,1,0:T(8,128)(2,1)} %bitcast.37, ...), custom_call_target="tpu_custom_call", output_to_operand_aliasing={{0}: (4, {}), {1}: (5, {}), {2}: (6, {})} | custom-call | flops 282591232 | bytes 4194304 | tf_op jit(solution)/shard_map/pallas_call | solution.py:266
  47.7 5.4 %shard_map.74 = (bf16[128,512]{1,0:T(8,128)(2,1)}, bf16[5,7,128,512]{3,2,1,0:T(8,128)(2,1)}) custom-call(s32[3]{0:T(128)} %pad_add_fusion.3.p_ref, bf16[4,128,512]{2,1,0:T(8,128)(2,1)} %bitcast.51, bf16[128,512]{1,0:T(8,128)(2,1)} %copy-done.3, f32[4,4,128,512]{3,2,1,0:T(8,128)} %get-tuple-element.55.z_ref.refs_0_, ...), custom_call_target="tpu_custom_call", output_to_operand_aliasing={{1}: (6, {})} | custom-call | flops 282591232 | bytes 4194304 | tf_op jit(solution)/shard_map/pallas_call | solution.py:252
  53.0 2.5 %collective-permute-start.3 = (bf16[128,512]{1,0:T(8,128)(2,1)}, bf16[128,512]{1,0:T(8,128)(2,1)S(1)}, u32[]{:S(2)}, u32[]{:S(2)}) collective-permute-start(bf16[128,512]{1,0:T(8,128)(2,1)} %get-tuple-element.57), channel_id=1, source_target_pairs={{32,0},{64,32},{96,64},{33,1},{65,33},{97,65},{34,2},{66,34},{98,6... | collective-permute-start | bytes 393224 | tf_op jit(solution)/shard_map/ppermute | solution.py:18
  56.2 4.1 %shard_map.75 = (f32[4,4,128,512]{3,2,1,0:T(8,128)}, bf16[4,4,128,512]{3,2,1,0:T(8,128)(2,1)}, bf16[4,4,128,512]{3,2,1,0:T(8,128)(2,1)}) custom-call(s32[1]{0:T(128)} %bitcast.7.p_ref, bf16[4,128,512]{2,1,0:T(8,128)(2,1)} %bitcast.59, bf16[4,512,512]{2,1,0:T(8,128)(2,1)} %bitcast.39, ...), custom_call_target="tpu_custom_call", output_to_operand_aliasing={{0}: (4, {}), {1}: (5, {}), {2}: (6, {})} | custom-call | flops 282591232 | bytes 4194304 | tf_op jit(solution)/shard_map/pallas_call | solution.py:266
  61.0 5.4 %shard_map.76 = (bf16[128,512]{1,0:T(8,128)(2,1)}, bf16[5,7,128,512]{3,2,1,0:T(8,128)(2,1)}) custom-call(s32[3]{0:T(128)} %pad_add_fusion.2.p_ref, bf16[4,128,512]{2,1,0:T(8,128)(2,1)} %bitcast.52, bf16[128,512]{1,0:T(8,128)(2,1)} %copy-done.4, f32[4,4,128,512]{3,2,1,0:T(8,128)} %get-tuple-element.60.z_ref.refs_0_, ...), custom_call_target="tpu_custom_call", output_to_operand_aliasing={{1}: (6, {})} | custom-call | flops 282591232 | bytes 4194304 | tf_op jit(solution)/shard_map/pallas_call | solution.py:252
  66.4 2.3 %collective-permute-start.4 = (bf16[128,512]{1,0:T(8,128)(2,1)}, bf16[128,512]{1,0:T(8,128)(2,1)S(1)}, u32[]{:S(2)}, u32[]{:S(2)}) collective-permute-start(bf16[128,512]{1,0:T(8,128)(2,1)} %get-tuple-element.62), channel_id=1, source_target_pairs={{32,0},{64,32},{96,64},{33,1},{65,33},{97,65},{34,2},{66,34},{98,6... | collective-permute-start | bytes 393224 | tf_op jit(solution)/shard_map/ppermute | solution.py:18
  69.2 4.1 %shard_map.77 = (f32[4,4,128,512]{3,2,1,0:T(8,128)}, bf16[4,4,128,512]{3,2,1,0:T(8,128)(2,1)}, bf16[4,4,128,512]{3,2,1,0:T(8,128)(2,1)}) custom-call(s32[1]{0:T(128)} %bitcast.5.p_ref, bf16[4,128,512]{2,1,0:T(8,128)(2,1)} %bitcast.60, bf16[4,512,512]{2,1,0:T(8,128)(2,1)} %bitcast.41, ...), custom_call_target="tpu_custom_call", output_to_operand_aliasing={{0}: (4, {}), {1}: (5, {}), {2}: (6, {})} | custom-call | flops 282591232 | bytes 4194304 | tf_op jit(solution)/shard_map/pallas_call | solution.py:266
  74.0 5.4 %shard_map.78 = (bf16[128,512]{1,0:T(8,128)(2,1)}, bf16[5,7,128,512]{3,2,1,0:T(8,128)(2,1)}) custom-call(s32[3]{0:T(128)} %pad_add_fusion.1.p_ref, bf16[4,128,512]{2,1,0:T(8,128)(2,1)} %bitcast.53, bf16[128,512]{1,0:T(8,128)(2,1)} %copy-done.5, f32[4,4,128,512]{3,2,1,0:T(8,128)} %get-tuple-element.65.z_ref.refs_0_, ...), custom_call_target="tpu_custom_call", output_to_operand_aliasing={{1}: (6, {})} | custom-call | flops 282591232 | bytes 4194304 | tf_op jit(solution)/shard_map/pallas_call | solution.py:252
  79.4 2.3 %collective-permute-start.5 = (bf16[128,512]{1,0:T(8,128)(2,1)}, bf16[128,512]{1,0:T(8,128)(2,1)S(1)}, u32[]{:S(2)}, u32[]{:S(2)}) collective-permute-start(bf16[128,512]{1,0:T(8,128)(2,1)} %get-tuple-element.67), channel_id=1, source_target_pairs={{32,0},{64,32},{96,64},{33,1},{65,33},{97,65},{34,2},{66,34},{98,6... | collective-permute-start | bytes 393224 | tf_op jit(solution)/shard_map/ppermute | solution.py:18
  82.4 4.1 %shard_map.79 = (f32[4,4,128,512]{3,2,1,0:T(8,128)}, bf16[4,4,128,512]{3,2,1,0:T(8,128)(2,1)}, bf16[4,4,128,512]{3,2,1,0:T(8,128)(2,1)}) custom-call(s32[1]{0:T(128)} %bitcast.1.p_ref, bf16[4,128,512]{2,1,0:T(8,128)(2,1)} %bitcast.61, bf16[4,512,512]{2,1,0:T(8,128)(2,1)} %bitcast.43, ...), custom_call_target="tpu_custom_call", output_to_operand_aliasing={{0}: (4, {}), {1}: (5, {}), {2}: (6, {})} | custom-call | flops 282591232 | bytes 4194304 | tf_op jit(solution)/shard_map/pallas_call | solution.py:266
  87.2 5.4 %shard_map.80 = (bf16[128,512]{1,0:T(8,128)(2,1)}, bf16[5,7,128,512]{3,2,1,0:T(8,128)(2,1)}) custom-call(s32[3]{0:T(128)} %pad_add_fusion.p_ref, bf16[4,128,512]{2,1,0:T(8,128)(2,1)} %bitcast.54, bf16[128,512]{1,0:T(8,128)(2,1)} %copy-done.1, f32[4,4,128,512]{3,2,1,0:T(8,128)} %get-tuple-element.70.z_ref, ...), custom_call_target="tpu_custom_call", output_to_operand_aliasing={{1}: (6, {})} | custom-call | flops 282591232 | bytes 4194304 | tf_op jit(solution)/shard_map/pallas_call | solution.py:252
  92.5 13.0 %shard_map.81 = (bf16[2,16,72,512]{3,2,1,0:T(8,128)(2,1)}, bf16[4,128,512]{2,1,0:T(8,128)(2,1)}) custom-call(s32[1]{0:T(128)} %bitcast.p_ref, bf16[5,7,128,512]{3,2,1,0:T(8,128)(2,1)} %get-tuple-element.72.h_ref, bf16[4,512,512]{2,1,0:T(8,128)(2,1)} %bitcast.46, bf16[4,512,512]{2,1,0:T(8,128)(2,1)} %bitcast.47, f32[4,512,512]{2,1,0:T(8,128)} %bitcast.30, ...), custom_call_target="tpu_custom_call" | custom-call | tf_op jit(solution)/shard_map/pallas_call | solution.py:288
  105.6 6.8 %all_to_all.10 = bf16[2,16,72,512]{3,2,1,0:T(8,128)(2,1)S(1)} all-to-all(bf16[2,16,72,512]{3,2,1,0:T(8,128)(2,1)} %get-tuple-element.76), channel_id=1, replica_groups=mesh['section'=4,'chip'=16,'core'=2] {'core'}, dimensions={0} | all-to-all | bytes 4718592 | tf_op jit(solution)/shard_map/all_to_all | solution.py:300
  113.6 26.7 %all_to_all.11 = bf16[16,72,512]{2,1,0:T(8,128)(2,1)S(1)} all-to-all(bf16[16,72,512]{2,1,0:T(8,128)(2,1)S(1)} %reduce_sum.21), channel_id=1, replica_groups=mesh['section'=4,'chip'=16,'core'=2] {'chip'}, dimensions={0} | all-to-all | bytes 2359296 | tf_op jit(solution)/shard_map/all_to_all | solution.py:300
  (33 shorter events, 11.7 us)
Async XLA Ops:
  12.9 7.5 %collective-permute-start = (bf16[128,512]{1,0:T(8,128)(2,1)}, bf16[128,512]{1,0:T(8,128)(2,1)S(1)}, u32[]{:S(2)}, u32[]{:S(2)}) collective-permute-start(bf16[128,512]{1,0:T(8,128)(2,1)} %get-tuple-element.42), channel_id=1, source_target_pairs={{32,0},{64,32},{96,64},{33,1},{65,33},{97,65},{34,2},{66,34},{98,6... | collective-permute-start | bytes 393224 | tf_op jit(solution)/shard_map/ppermute | solution.py:18
  20.4 0.7 copy-start
  26.5 7.3 %collective-permute-start.1 = (bf16[128,512]{1,0:T(8,128)(2,1)}, bf16[128,512]{1,0:T(8,128)(2,1)S(1)}, u32[]{:S(2)}, u32[]{:S(2)}) collective-permute-start(bf16[128,512]{1,0:T(8,128)(2,1)} %get-tuple-element.47), channel_id=1, source_target_pairs={{32,0},{64,32},{96,64},{33,1},{65,33},{97,65},{34,2},{66,34},{98,6... | collective-permute-start | bytes 393224 | tf_op jit(solution)/shard_map/ppermute | solution.py:18
  33.8 0.7 copy-start.2
  39.8 7.2 %collective-permute-start.2 = (bf16[128,512]{1,0:T(8,128)(2,1)}, bf16[128,512]{1,0:T(8,128)(2,1)S(1)}, u32[]{:S(2)}, u32[]{:S(2)}) collective-permute-start(bf16[128,512]{1,0:T(8,128)(2,1)} %get-tuple-element.52), channel_id=1, source_target_pairs={{32,0},{64,32},{96,64},{33,1},{65,33},{97,65},{34,2},{66,34},{98,6... | collective-permute-start | bytes 393224 | tf_op jit(solution)/shard_map/ppermute | solution.py:18
  47.0 0.7 copy-start.3
  53.0 7.3 %collective-permute-start.3 = (bf16[128,512]{1,0:T(8,128)(2,1)}, bf16[128,512]{1,0:T(8,128)(2,1)S(1)}, u32[]{:S(2)}, u32[]{:S(2)}) collective-permute-start(bf16[128,512]{1,0:T(8,128)(2,1)} %get-tuple-element.57), channel_id=1, source_target_pairs={{32,0},{64,32},{96,64},{33,1},{65,33},{97,65},{34,2},{66,34},{98,6... | collective-permute-start | bytes 393224 | tf_op jit(solution)/shard_map/ppermute | solution.py:18
  60.3 0.7 copy-start.4
  66.4 7.0 %collective-permute-start.4 = (bf16[128,512]{1,0:T(8,128)(2,1)}, bf16[128,512]{1,0:T(8,128)(2,1)S(1)}, u32[]{:S(2)}, u32[]{:S(2)}) collective-permute-start(bf16[128,512]{1,0:T(8,128)(2,1)} %get-tuple-element.62), channel_id=1, source_target_pairs={{32,0},{64,32},{96,64},{33,1},{65,33},{97,65},{34,2},{66,34},{98,6... | collective-permute-start | bytes 393224 | tf_op jit(solution)/shard_map/ppermute | solution.py:18
  73.4 0.7 copy-start.5
  79.4 7.1 %collective-permute-start.5 = (bf16[128,512]{1,0:T(8,128)(2,1)}, bf16[128,512]{1,0:T(8,128)(2,1)S(1)}, u32[]{:S(2)}, u32[]{:S(2)}) collective-permute-start(bf16[128,512]{1,0:T(8,128)(2,1)} %get-tuple-element.67), channel_id=1, source_target_pairs={{32,0},{64,32},{96,64},{33,1},{65,33},{97,65},{34,2},{66,34},{98,6... | collective-permute-start | bytes 393224 | tf_op jit(solution)/shard_map/ppermute | solution.py:18
  86.5 0.7 copy-start.1

commit v8 on v7

--- a/solution.py
+++ b/solution.py
@@ -85,9 +85,9 @@
     fwd_kernel(p_ref, x_ref, w_ref, k_ref, z_ref, a_ref, xs_ref, height=height, width=width)
 
 
-def step_kernel(p_ref, top_ref, car_ref, z_ref, w_ref, k_ref, h_in, g_ref, h_ref, *, height, width):
+def step_kernel(p_ref, top_ref, car_ref, z_ref, wt_ref, k_ref, h_in, g_ref, h_ref, *, height, width):
     del h_in
-    layers = w_ref.shape[0]
+    layers = wt_ref.shape[0]
     top = top_ref[...].astype(jnp.float32)
     car = car_ref[...].astype(jnp.float32)
     g = jnp.where(p_ref[1] == 1, top, car)
@@ -95,9 +95,7 @@
     h_ref[layers] = g
     masks = edge_masks(g.shape, height, width)
     for layer in reversed(range(layers)):
-        back = lax.dot_general(
-            g, w_ref[layer], (((1,), (1,)), ((), ())), preferred_element_type=jnp.float32
-        )
+        back = jnp.dot(g, wt_ref[layer], preferred_element_type=jnp.float32)
         zed = z_ref[layer]
         sig = jax.nn.sigmoid(zed)
         dzed = back * sig * (1.0 + zed * (1.0 - sig))
@@ -109,9 +107,9 @@
 
 
 def grad_kernel(
-    p_ref, h_ref, a_ref, xs_ref, z_ref, w_ref, k_ref, send_ref, res_ref, *, height, width, scale
+    p_ref, h_ref, a_ref, xs_ref, z_ref, wt_ref, k_ref, send_ref, res_ref, *, height, width, scale
 ):
-    layers, chans = w_ref.shape[0], w_ref.shape[2]
+    layers, chans = wt_ref.shape[0], wt_ref.shape[2]
     taps = k_ref.shape[1]
     batches = res_ref.shape[0]
     rows = h_ref.shape[2]
@@ -126,9 +124,7 @@
     masks = edge_masks((batches * rows, chans), height, width)
     for layer in range(layers):
         g = h_ref[layer + 1, pl.ds(first, batches)].reshape(batches * rows, chans)
-        back = lax.dot_general(
-            g, w_ref[layer], (((1,), (1,)), ((), ())), preferred_element_type=jnp.float32
-        )
+        back = jnp.dot(g, wt_ref[layer], preferred_element_type=jnp.float32)
         zed = z_ref[layer]
         sig = jax.nn.sigmoid(zed)
         dzed = back * sig * (1.0 + zed * (1.0 - sig))
@@ -181,6 +177,7 @@
     rows = images * height * width
     weights = point_weights[0]
     kerns = depth_weights[0].astype(jnp.float32)
+    weights_t = jnp.swapaxes(weights, 1, 2)
     vmem = pl.BlockSpec(memory_space=pltpu.VMEM)
     smem = pl.BlockSpec(memory_space=pltpu.SMEM)
     params = pltpu.CompilerParams(vmem_limit_bytes=VMEM_LIMIT)
@@ -259,7 +256,7 @@
             input_output_aliases={6: 1},
             compiler_params=params,
             cost_estimate=fwd_cost,
-        )(scalars, top_all, carried, zbuf, weights, kerns, hbuf)
+        )(scalars, top_all, carried, zbuf, weights_t, kerns, hbuf)
         if step < total_steps - 1:
             carried = from_behind(g, "section", -1)
             nxt, _ = picked_at(step + 1)
@@ -294,7 +291,7 @@
         in_specs=[smem, vmem, vmem, vmem, vmem, vmem, vmem],
         out_specs=(vmem, vmem),
         compiler_params=params,
-    )(first, hbuf, acts, xs, zs, weights, kerns)
+    )(first, hbuf, acts, xs, zs, weights_t, kerns)
     part = send
     for stage, name in enumerate(("core", "chip")):
         part = lax.all_to_all(part, name, 0, 0, tiled=True)

time: 143 us -> 146 us (1.021)
  local copies, waits for them, and re-layouts: 6.03 us -> 10.2 us
    unnamed x12 -> x13, local copies, waits for them, and re-layouts: 3.93 us -> 8.11 us
  transfers between devices with their start and end apart: 6 -> 6, of which waited for: 0 -> 0; matrix products, arithmetic and copies ran while one was open for 3% -> 3% of each run, Pallas kernels for 18% -> 17%
where the time goes in v8:
time: 146 us; the launch traced here: 145 us
  Pallas kernels  79 us (54%)
  blocking collectives  33.5 us (23%)
  starting transfers between devices  14.6 us (10%)
  local copies, waits for them, and re-layouts  10.2 us (7%)
  other arithmetic  7.06 us (5%)
    pallas_call x7, Pallas kernels, body(): pl.pallas_call(functools.partial(step_kernel, height=height, width=width)...  36.7 us
    all_to_all x2, blocking collectives, body(): part = lax.all_to_all(part, name, 0, 0, tiled=True)  33.5 us
    pallas_call x6, Pallas kernels, body(): pl.pallas_call(functools.partial(fwd_kernel, height=height, width=width),...  25.1 us
    ppermute x6, starting transfers between devices, from_behind(): return lax.ppermute(shard, axis, pairs)  14.6 us
    pallas_call x1, Pallas kernels, body(): pl.pallas_call(functools.partial(grad_kernel, height=height, width=width,...  13 us
    unnamed x13, local copies, waits for them, and re-layouts  8.11 us
    another operation x7, other arithmetic, body(): scalars = jnp.stack([picked, is_last, valid]).astype(jnp.int32)  4.23 us
    pallas_call x1, Pallas kernels, body(): pl.pallas_call(functools.partial(fwd_first_kernel, height=height, width=w...  4.16 us
  transfers between devices with their start and end apart: 6, of which 0 were waited for; matrix products, arithmetic and copies ran while one was open for 3% of the time, Pallas kernels for 17%

profile of v8, /device:TPU:6, one launch (start us, length us, event | category | flops | bytes accessed | tf_op | source)
XLA Modules:
  0.0 145.2 jit_solution(13023725796884642716)
XLA Ops:
  2.1 4.2 %copy.41 = bf16[1,4,512,512]{2,3,1,0:T(8,128)(2,1)} copy(bf16[1,4,512,512]{3,2,1,0:T(8,128)(2,1)} %param.6) | data formatting | bytes 4194304 | tf_op args[2]
  6.9 4.2 %shard_map.67 = (f32[4,4,128,512]{3,2,1,0:T(8,128)}, bf16[4,4,128,512]{3,2,1,0:T(8,128)(2,1)}, bf16[4,4,128,512]{3,2,1,0:T(8,128)(2,1)}, bf16[5,7,128,512]{3,2,1,0:T(8,128)(2,1)}) custom-call(s32[1]{0:T(128)} %bitcast.15.p_ref, bf16[4,128,512]{2,1,0:T(8,128)(2,1)} %bitcast.58, bf16[4,512,512]{2,1,0:T(8,128)(2,1)} %bitcast.42, ...), custom_call_target="tpu_custom_call" | custom-call | flops 282591232 | bytes 4194304 | tf_op jit(solution)/shard_map/pallas_call | solution.py:212
  11.7 5.2 %shard_map.68 = (bf16[128,512]{1,0:T(8,128)(2,1)}, bf16[5,7,128,512]{3,2,1,0:T(8,128)(2,1)}) custom-call(s32[3]{0:T(128)} %pad_add_fusion.6.p_ref, bf16[4,128,512]{2,1,0:T(8,128)(2,1)} %bitcast.51, bf16[128,512]{1,0:T(8,128)(2,1)} %broadcast_in_dim.6.car_ref, f32[4,4,128,512]{3,2,1,0:T(8,128)} %get-tuple-element.40.z_ref.refs_0_, ...), custom_call_target="tpu_custom_call", output_to_operand_aliasing={{1}: (6, {})} | custom-call | flops 282591232 | bytes 4194304 | tf_op jit(solution)/shard_map/pallas_call | solution.py:249
  16.9 2.7 %collective-permute-start = (bf16[128,512]{1,0:T(8,128)(2,1)}, bf16[128,512]{1,0:T(8,128)(2,1)S(1)}, u32[]{:S(2)}, u32[]{:S(2)}) collective-permute-start(bf16[128,512]{1,0:T(8,128)(2,1)} %get-tuple-element.42), channel_id=1, source_target_pairs={{32,0},{64,32},{96,64},{33,1},{65,33},{97,65},{34,2},{66,34},{98,6... | collective-permute-start | bytes 393224 | tf_op jit(solution)/shard_map/ppermute | solution.py:18
  19.7 4.1 %shard_map.69 = (f32[4,4,128,512]{3,2,1,0:T(8,128)}, bf16[4,4,128,512]{3,2,1,0:T(8,128)(2,1)}, bf16[4,4,128,512]{3,2,1,0:T(8,128)(2,1)}) custom-call(s32[1]{0:T(128)} %bitcast.13.p_ref, bf16[4,128,512]{2,1,0:T(8,128)(2,1)} %bitcast.59, bf16[4,512,512]{2,1,0:T(8,128)(2,1)} %bitcast.43, ...), custom_call_target="tpu_custom_call", output_to_operand_aliasing={{0}: (4, {}), {1}: (5, {}), {2}: (6, {})} | custom-call | flops 282591232 | bytes 4194304 | tf_op jit(solution)/shard_map/pallas_call | solution.py:263
  25.1 5.2 %shard_map.70 = (bf16[128,512]{1,0:T(8,128)(2,1)}, bf16[5,7,128,512]{3,2,1,0:T(8,128)(2,1)}) custom-call(s32[3]{0:T(128)} %pad_add_fusion.5.p_ref, bf16[4,128,512]{2,1,0:T(8,128)(2,1)} %bitcast.52, bf16[128,512]{1,0:T(8,128)(2,1)} %copy-done, f32[4,4,128,512]{3,2,1,0:T(8,128)} %get-tuple-element.45.z_ref.refs_0_, ...), custom_call_target="tpu_custom_call", output_to_operand_aliasing={{1}: (6, {})} | custom-call | flops 282591232 | bytes 4194304 | tf_op jit(solution)/shard_map/pallas_call | solution.py:249
  30.3 2.6 %collective-permute-start.1 = (bf16[128,512]{1,0:T(8,128)(2,1)}, bf16[128,512]{1,0:T(8,128)(2,1)S(1)}, u32[]{:S(2)}, u32[]{:S(2)}) collective-permute-start(bf16[128,512]{1,0:T(8,128)(2,1)} %get-tuple-element.47), channel_id=1, source_target_pairs={{32,0},{64,32},{96,64},{33,1},{65,33},{97,65},{34,2},{66,34},{98,6... | collective-permute-start | bytes 393224 | tf_op jit(solution)/shard_map/ppermute | solution.py:18
  33.5 4.2 %shard_map.71 = (f32[4,4,128,512]{3,2,1,0:T(8,128)}, bf16[4,4,128,512]{3,2,1,0:T(8,128)(2,1)}, bf16[4,4,128,512]{3,2,1,0:T(8,128)(2,1)}) custom-call(s32[1]{0:T(128)} %bitcast.11.p_ref, bf16[4,128,512]{2,1,0:T(8,128)(2,1)} %bitcast.60, bf16[4,512,512]{2,1,0:T(8,128)(2,1)} %bitcast.44, ...), custom_call_target="tpu_custom_call", output_to_operand_aliasing={{0}: (4, {}), {1}: (5, {}), {2}: (6, {})} | custom-call | flops 282591232 | bytes 4194304 | tf_op jit(solution)/shard_map/pallas_call | solution.py:263
  38.3 5.2 %shard_map.72 = (bf16[128,512]{1,0:T(8,128)(2,1)}, bf16[5,7,128,512]{3,2,1,0:T(8,128)(2,1)}) custom-call(s32[3]{0:T(128)} %pad_add_fusion.4.p_ref, bf16[4,128,512]{2,1,0:T(8,128)(2,1)} %bitcast.53, bf16[128,512]{1,0:T(8,128)(2,1)} %copy-done.2, f32[4,4,128,512]{3,2,1,0:T(8,128)} %get-tuple-element.50.z_ref.refs_0_, ...), custom_call_target="tpu_custom_call", output_to_operand_aliasing={{1}: (6, {})} | custom-call | flops 282591232 | bytes 4194304 | tf_op jit(solution)/shard_map/pallas_call | solution.py:249
  43.6 2.4 %collective-permute-start.2 = (bf16[128,512]{1,0:T(8,128)(2,1)}, bf16[128,512]{1,0:T(8,128)(2,1)S(1)}, u32[]{:S(2)}, u32[]{:S(2)}) collective-permute-start(bf16[128,512]{1,0:T(8,128)(2,1)} %get-tuple-element.52), channel_id=1, source_target_pairs={{32,0},{64,32},{96,64},{33,1},{65,33},{97,65},{34,2},{66,34},{98,6... | collective-permute-start | bytes 393224 | tf_op jit(solution)/shard_map/ppermute | solution.py:18
  46.6 4.2 %shard_map.73 = (f32[4,4,128,512]{3,2,1,0:T(8,128)}, bf16[4,4,128,512]{3,2,1,0:T(8,128)(2,1)}, bf16[4,4,128,512]{3,2,1,0:T(8,128)(2,1)}) custom-call(s32[1]{0:T(128)} %bitcast.9.p_ref, bf16[4,128,512]{2,1,0:T(8,128)(2,1)} %bitcast.61, bf16[4,512,512]{2,1,0:T(8,128)(2,1)} %bitcast.45, ...), custom_call_target="tpu_custom_call", output_to_operand_aliasing={{0}: (4, {}), {1}: (5, {}), {2}: (6, {})} | custom-call | flops 282591232 | bytes 4194304 | tf_op jit(solution)/shard_map/pallas_call | solution.py:263
  51.5 5.2 %shard_map.74 = (bf16[128,512]{1,0:T(8,128)(2,1)}, bf16[5,7,128,512]{3,2,1,0:T(8,128)(2,1)}) custom-call(s32[3]{0:T(128)} %pad_add_fusion.3.p_ref, bf16[4,128,512]{2,1,0:T(8,128)(2,1)} %bitcast.54, bf16[128,512]{1,0:T(8,128)(2,1)} %copy-done.3, f32[4,4,128,512]{3,2,1,0:T(8,128)} %get-tuple-element.55.z_ref.refs_0_, ...), custom_call_target="tpu_custom_call", output_to_operand_aliasing={{1}: (6, {})} | custom-call | flops 282591232 | bytes 4194304 | tf_op jit(solution)/shard_map/pallas_call | solution.py:249
  56.7 2.5 %collective-permute-start.3 = (bf16[128,512]{1,0:T(8,128)(2,1)}, bf16[128,512]{1,0:T(8,128)(2,1)S(1)}, u32[]{:S(2)}, u32[]{:S(2)}) collective-permute-start(bf16[128,512]{1,0:T(8,128)(2,1)} %get-tuple-element.57), channel_id=1, source_target_pairs={{32,0},{64,32},{96,64},{33,1},{65,33},{97,65},{34,2},{66,34},{98,6... | collective-permute-start | bytes 393224 | tf_op jit(solution)/shard_map/ppermute | solution.py:18
  59.7 4.2 %shard_map.75 = (f32[4,4,128,512]{3,2,1,0:T(8,128)}, bf16[4,4,128,512]{3,2,1,0:T(8,128)(2,1)}, bf16[4,4,128,512]{3,2,1,0:T(8,128)(2,1)}) custom-call(s32[1]{0:T(128)} %bitcast.7.p_ref, bf16[4,128,512]{2,1,0:T(8,128)(2,1)} %bitcast.62, bf16[4,512,512]{2,1,0:T(8,128)(2,1)} %bitcast.46, ...), custom_call_target="tpu_custom_call", output_to_operand_aliasing={{0}: (4, {}), {1}: (5, {}), {2}: (6, {})} | custom-call | flops 282591232 | bytes 4194304 | tf_op jit(solution)/shard_map/pallas_call | solution.py:263
  64.6 5.3 %shard_map.76 = (bf16[128,512]{1,0:T(8,128)(2,1)}, bf16[5,7,128,512]{3,2,1,0:T(8,128)(2,1)}) custom-call(s32[3]{0:T(128)} %pad_add_fusion.2.p_ref, bf16[4,128,512]{2,1,0:T(8,128)(2,1)} %bitcast.55, bf16[128,512]{1,0:T(8,128)(2,1)} %copy-done.4, f32[4,4,128,512]{3,2,1,0:T(8,128)} %get-tuple-element.60.z_ref.refs_0_, ...), custom_call_target="tpu_custom_call", output_to_operand_aliasing={{1}: (6, {})} | custom-call | flops 282591232 | bytes 4194304 | tf_op jit(solution)/shard_map/pallas_call | solution.py:249
  69.9 2.3 %collective-permute-start.4 = (bf16[128,512]{1,0:T(8,128)(2,1)}, bf16[128,512]{1,0:T(8,128)(2,1)S(1)}, u32[]{:S(2)}, u32[]{:S(2)}) collective-permute-start(bf16[128,512]{1,0:T(8,128)(2,1)} %get-tuple-element.62), channel_id=1, source_target_pairs={{32,0},{64,32},{96,64},{33,1},{65,33},{97,65},{34,2},{66,34},{98,6... | collective-permute-start | bytes 393224 | tf_op jit(solution)/shard_map/ppermute | solution.py:18
  72.7 4.2 %shard_map.77 = (f32[4,4,128,512]{3,2,1,0:T(8,128)}, bf16[4,4,128,512]{3,2,1,0:T(8,128)(2,1)}, bf16[4,4,128,512]{3,2,1,0:T(8,128)(2,1)}) custom-call(s32[1]{0:T(128)} %bitcast.5.p_ref, bf16[4,128,512]{2,1,0:T(8,128)(2,1)} %bitcast.63, bf16[4,512,512]{2,1,0:T(8,128)(2,1)} %bitcast.47, ...), custom_call_target="tpu_custom_call", output_to_operand_aliasing={{0}: (4, {}), {1}: (5, {}), {2}: (6, {})} | custom-call | flops 282591232 | bytes 4194304 | tf_op jit(solution)/shard_map/pallas_call | solution.py:263
  77.6 5.3 %shard_map.78 = (bf16[128,512]{1,0:T(8,128)(2,1)}, bf16[5,7,128,512]{3,2,1,0:T(8,128)(2,1)}) custom-call(s32[3]{0:T(128)} %pad_add_fusion.1.p_ref, bf16[4,128,512]{2,1,0:T(8,128)(2,1)} %bitcast.56, bf16[128,512]{1,0:T(8,128)(2,1)} %copy-done.5, f32[4,4,128,512]{3,2,1,0:T(8,128)} %get-tuple-element.65.z_ref.refs_0_, ...), custom_call_target="tpu_custom_call", output_to_operand_aliasing={{1}: (6, {})} | custom-call | flops 282591232 | bytes 4194304 | tf_op jit(solution)/shard_map/pallas_call | solution.py:249
  82.9 2.3 %collective-permute-start.5 = (bf16[128,512]{1,0:T(8,128)(2,1)}, bf16[128,512]{1,0:T(8,128)(2,1)S(1)}, u32[]{:S(2)}, u32[]{:S(2)}) collective-permute-start(bf16[128,512]{1,0:T(8,128)(2,1)} %get-tuple-element.67), channel_id=1, source_target_pairs={{32,0},{64,32},{96,64},{33,1},{65,33},{97,65},{34,2},{66,34},{98,6... | collective-permute-start | bytes 393224 | tf_op jit(solution)/shard_map/ppermute | solution.py:18
  85.7 4.2 %shard_map.79 = (f32[4,4,128,512]{3,2,1,0:T(8,128)}, bf16[4,4,128,512]{3,2,1,0:T(8,128)(2,1)}, bf16[4,4,128,512]{3,2,1,0:T(8,128)(2,1)}) custom-call(s32[1]{0:T(128)} %bitcast.1.p_ref, bf16[4,128,512]{2,1,0:T(8,128)(2,1)} %bitcast.64, bf16[4,512,512]{2,1,0:T(8,128)(2,1)} %bitcast.48, ...), custom_call_target="tpu_custom_call", output_to_operand_aliasing={{0}: (4, {}), {1}: (5, {}), {2}: (6, {})} | custom-call | flops 282591232 | bytes 4194304 | tf_op jit(solution)/shard_map/pallas_call | solution.py:263
  90.6 5.2 %shard_map.80 = (bf16[128,512]{1,0:T(8,128)(2,1)}, bf16[5,7,128,512]{3,2,1,0:T(8,128)(2,1)}) custom-call(s32[3]{0:T(128)} %pad_add_fusion.p_ref, bf16[4,128,512]{2,1,0:T(8,128)(2,1)} %bitcast.57, bf16[128,512]{1,0:T(8,128)(2,1)} %copy-done.1, f32[4,4,128,512]{3,2,1,0:T(8,128)} %get-tuple-element.70.z_ref, ...), custom_call_target="tpu_custom_call", output_to_operand_aliasing={{1}: (6, {})} | custom-call | flops 282591232 | bytes 4194304 | tf_op jit(solution)/shard_map/pallas_call | solution.py:249
  95.8 13.0 %shard_map.81 = (bf16[2,16,72,512]{3,2,1,0:T(8,128)(2,1)}, bf16[4,128,512]{2,1,0:T(8,128)(2,1)}) custom-call(s32[1]{0:T(128)} %bitcast.p_ref, bf16[5,7,128,512]{3,2,1,0:T(8,128)(2,1)} %get-tuple-element.72.h_ref, bf16[4,512,512]{2,1,0:T(8,128)(2,1)} %bitcast.49, bf16[4,512,512]{2,1,0:T(8,128)(2,1)} %bitcast.50, f32[4,512,512]{2,1,0:T(8,128)} %bitcast.33, ...), custom_call_target="tpu_custom_call" | custom-call | tf_op jit(solution)/shard_map/pallas_call | solution.py:285
  108.8 6.8 %all_to_all.10 = bf16[2,16,72,512]{3,2,1,0:T(8,128)(2,1)S(1)} all-to-all(bf16[2,16,72,512]{3,2,1,0:T(8,128)(2,1)} %get-tuple-element.76), channel_id=1, replica_groups=mesh['section'=4,'chip'=16,'core'=2] {'core'}, dimensions={0} | all-to-all | bytes 4718592 | tf_op jit(solution)/shard_map/all_to_all | solution.py:297
  116.9 26.7 %all_to_all.11 = bf16[16,72,512]{2,1,0:T(8,128)(2,1)S(1)} all-to-all(bf16[16,72,512]{2,1,0:T(8,128)(2,1)S(1)} %reduce_sum.21), channel_id=1, replica_groups=mesh['section'=4,'chip'=16,'core'=2] {'chip'}, dimensions={0} | all-to-all | bytes 2359296 | tf_op jit(solution)/shard_map/all_to_all | solution.py:297
  (34 shorter events, 13.1 us)
Async XLA Ops:
  16.9 7.5 %collective-permute-start = (bf16[128,512]{1,0:T(8,128)(2,1)}, bf16[128,512]{1,0:T(8,128)(2,1)S(1)}, u32[]{:S(2)}, u32[]{:S(2)}) collective-permute-start(bf16[128,512]{1,0:T(8,128)(2,1)} %get-tuple-element.42), channel_id=1, source_target_pairs={{32,0},{64,32},{96,64},{33,1},{65,33},{97,65},{34,2},{66,34},{98,6... | collective-permute-start | bytes 393224 | tf_op jit(solution)/shard_map/ppermute | solution.py:18
  24.4 0.7 copy-start
  30.3 7.3 %collective-permute-start.1 = (bf16[128,512]{1,0:T(8,128)(2,1)}, bf16[128,512]{1,0:T(8,128)(2,1)S(1)}, u32[]{:S(2)}, u32[]{:S(2)}) collective-permute-start(bf16[128,512]{1,0:T(8,128)(2,1)} %get-tuple-element.47), channel_id=1, source_target_pairs={{32,0},{64,32},{96,64},{33,1},{65,33},{97,65},{34,2},{66,34},{98,6... | collective-permute-start | bytes 393224 | tf_op jit(solution)/shard_map/ppermute | solution.py:18
  37.7 0.7 copy-start.2
  43.6 7.2 %collective-permute-start.2 = (bf16[128,512]{1,0:T(8,128)(2,1)}, bf16[128,512]{1,0:T(8,128)(2,1)S(1)}, u32[]{:S(2)}, u32[]{:S(2)}) collective-permute-start(bf16[128,512]{1,0:T(8,128)(2,1)} %get-tuple-element.52), channel_id=1, source_target_pairs={{32,0},{64,32},{96,64},{33,1},{65,33},{97,65},{34,2},{66,34},{98,6... | collective-permute-start | bytes 393224 | tf_op jit(solution)/shard_map/ppermute | solution.py:18
  50.8 0.7 copy-start.3
  56.7 7.3 %collective-permute-start.3 = (bf16[128,512]{1,0:T(8,128)(2,1)}, bf16[128,512]{1,0:T(8,128)(2,1)S(1)}, u32[]{:S(2)}, u32[]{:S(2)}) collective-permute-start(bf16[128,512]{1,0:T(8,128)(2,1)} %get-tuple-element.57), channel_id=1, source_target_pairs={{32,0},{64,32},{96,64},{33,1},{65,33},{97,65},{34,2},{66,34},{98,6... | collective-permute-start | bytes 393224 | tf_op jit(solution)/shard_map/ppermute | solution.py:18
  64.0 0.7 copy-start.4
  69.9 7.1 %collective-permute-start.4 = (bf16[128,512]{1,0:T(8,128)(2,1)}, bf16[128,512]{1,0:T(8,128)(2,1)S(1)}, u32[]{:S(2)}, u32[]{:S(2)}) collective-permute-start(bf16[128,512]{1,0:T(8,128)(2,1)} %get-tuple-element.62), channel_id=1, source_target_pairs={{32,0},{64,32},{96,64},{33,1},{65,33},{97,65},{34,2},{66,34},{98,6... | collective-permute-start | bytes 393224 | tf_op jit(solution)/shard_map/ppermute | solution.py:18
  76.9 0.7 copy-start.5
  82.9 7.1 %collective-permute-start.5 = (bf16[128,512]{1,0:T(8,128)(2,1)}, bf16[128,512]{1,0:T(8,128)(2,1)S(1)}, u32[]{:S(2)}, u32[]{:S(2)}) collective-permute-start(bf16[128,512]{1,0:T(8,128)(2,1)} %get-tuple-element.67), channel_id=1, source_target_pairs={{32,0},{64,32},{96,64},{33,1},{65,33},{97,65},{34,2},{66,34},{98,6... | collective-permute-start | bytes 393224 | tf_op jit(solution)/shard_map/ppermute | solution.py:18
  90.0 0.7 copy-start.1

commit v9 on v7

--- a/solution.py
+++ b/solution.py
@@ -60,7 +60,7 @@
 def stencil(x, k_ref, layer, masks, width, sign):
     total = jnp.zeros(x.shape, jnp.float32)
     for tap, moved in shifted_taps(x, masks, width, sign):
-        total = total + k_ref[layer, tap : tap + 1, :] * moved
+        total = total + k_ref[layer, tap : tap + 1, :].astype(jnp.float32) * moved
     return total
 
 
@@ -180,7 +180,7 @@
     images, height, width = inputs.shape[1], inputs.shape[2], inputs.shape[3]
     rows = images * height * width
     weights = point_weights[0]
-    kerns = depth_weights[0].astype(jnp.float32)
+    kerns = depth_weights[0]
     vmem = pl.BlockSpec(memory_space=pltpu.VMEM)
     smem = pl.BlockSpec(memory_space=pltpu.SMEM)
     params = pltpu.CompilerParams(vmem_limit_bytes=VMEM_LIMIT)
@@ -226,7 +226,7 @@
         cost_estimate=fwd_cost,
     )(jnp.reshape(picked, (1,)).astype(jnp.int32), x_all, weights, kerns)
 
-    carried = jnp.zeros((rows, chans), jnp.bfloat16)
+    carried = top_all
     is_last = (my_section == sections - 1).astype(jnp.int32)
     for step in range(total_steps):
         picked, valid = picked_at(step)
@@ -236,7 +236,9 @@
             grid=(1,),
             in_specs=[
                 pl.BlockSpec((None, rows, chans), lambda i, p: (p[0], 0, 0)),
-                pl.BlockSpec((rows, chans), lambda i, p: (0, 0)),
+                pl.BlockSpec((rows, chans), lambda i, p: (0, 0))
+                if step
+                else pl.BlockSpec((None, rows, chans), lambda i, p: (p[0], 0, 0)),
                 pl.BlockSpec((layers, None, rows, chans), lambda i, p: (0, p[0], 0, 0)),
                 pl.BlockSpec((layers, chans, chans), lambda i, p: (0, 0, 0)),
                 pl.BlockSpec((layers, taps, chans), lambda i, p: (0, 0, 0)),

time: 143 us -> 142 us (level)
  other arithmetic: 7.06 us -> 5.61 us
    convert_element_type x1 -> x0, other arithmetic: 1.44 us -> none  [body(): kerns = depth_weights[0].astype(jnp.float32)]
    unnamed x12 -> x13, local copies, waits for them, and re-layouts: 3.93 us -> 5.34 us
where the time goes in v9:
time: 142 us; the launch traced here: 141 us
  Pallas kernels  80 us (56%)
  blocking collectives  33.6 us (24%)
  starting transfers between devices  14.7 us (10%)
  local copies, waits for them, and re-layouts  6.77 us (5%)
  other arithmetic  5.61 us (4%)
    pallas_call x7, Pallas kernels, body(): pl.pallas_call(functools.partial(step_kernel, height=height, width=width)...  37.8 us
    all_to_all x2, blocking collectives, body(): part = lax.all_to_all(part, name, 0, 0, tiled=True)  33.6 us
    pallas_call x6, Pallas kernels, body(): pl.pallas_call(functools.partial(fwd_kernel, height=height, width=width),...  24.9 us
    ppermute x6, starting transfers between devices, from_behind(): return lax.ppermute(shard, axis, pairs)  14.7 us
    pallas_call x1, Pallas kernels, body(): pl.pallas_call(functools.partial(grad_kernel, height=height, width=width,...  13 us
    unnamed x13, local copies, waits for them, and re-layouts  5.34 us
    another operation x7, other arithmetic, body(): scalars = jnp.stack([picked, is_last, valid]).astype(jnp.int32)  4.22 us
    pallas_call x1, Pallas kernels, body(): pl.pallas_call(functools.partial(fwd_first_kernel, height=height, width=w...  4.2 us
  transfers between devices with their start and end apart: 6, of which 0 were waited for; matrix products, arithmetic and copies ran while one was open for 3% of the time, Pallas kernels for 18%

profile of v9, /device:TPU:6, one launch (start us, length us, event | category | flops | bytes accessed | tf_op | source)
XLA Modules:
  0.0 141.4 jit_solution(4863004813275616733)
XLA Ops:
  0.6 1.4 copy.35
  2.6 4.2 %shard_map.67 = (f32[4,4,128,512]{3,2,1,0:T(8,128)}, bf16[4,4,128,512]{3,2,1,0:T(8,128)(2,1)}, bf16[4,4,128,512]{3,2,1,0:T(8,128)(2,1)}, bf16[5,7,128,512]{3,2,1,0:T(8,128)(2,1)}) custom-call(s32[1]{0:T(128)} %bitcast.15.p_ref, bf16[4,128,512]{2,1,0:T(8,128)(2,1)} %bitcast.56, bf16[4,512,512]{2,1,0:T(8,128)(2,1)} %bitcast.31, bf16[4,9,512]{2,1,0:T(8,128)(2,1)} %bitcast.63), custom_call_target="tpu_custom_call" | custom-call | flops 282591232 | bytes 4194304 | tf_op jit(solution)/shard_map/pallas_call | solution.py:215
  6.8 5.4 %shard_map.68 = (bf16[128,512]{1,0:T(8,128)(2,1)}, bf16[5,7,128,512]{3,2,1,0:T(8,128)(2,1)}) custom-call(s32[3]{0:T(128)} %pad_add_fusion.6.p_ref, bf16[4,128,512]{2,1,0:T(8,128)(2,1)} %bitcast.48, bf16[4,128,512]{2,1,0:T(8,128)(2,1)} %bitcast.49, f32[4,4,128,512]{3,2,1,0:T(8,128)} %get-tuple-element.40.z_ref.refs_0_, ...), custom_call_target="tpu_custom_call", output_to_operand_aliasing={{1}: (6, {})} | custom-call | flops 282591232 | bytes 4194304 | tf_op jit(solution)/shard_map/pallas_call | solution.py:254
  12.2 2.7 %collective-permute-start = (bf16[128,512]{1,0:T(8,128)(2,1)}, bf16[128,512]{1,0:T(8,128)(2,1)S(1)}, u32[]{:S(2)}, u32[]{:S(2)}) collective-permute-start(bf16[128,512]{1,0:T(8,128)(2,1)} %get-tuple-element.42), channel_id=1, source_target_pairs={{32,0},{64,32},{96,64},{33,1},{65,33},{97,65},{34,2},{66,34},{98,6... | collective-permute-start | bytes 393224 | tf_op jit(solution)/shard_map/ppermute | solution.py:18
  15.0 4.2 %shard_map.69 = (f32[4,4,128,512]{3,2,1,0:T(8,128)}, bf16[4,4,128,512]{3,2,1,0:T(8,128)(2,1)}, bf16[4,4,128,512]{3,2,1,0:T(8,128)(2,1)}) custom-call(s32[1]{0:T(128)} %bitcast.13.p_ref, bf16[4,128,512]{2,1,0:T(8,128)(2,1)} %bitcast.57, bf16[4,512,512]{2,1,0:T(8,128)(2,1)} %bitcast.33, ...), custom_call_target="tpu_custom_call", output_to_operand_aliasing={{0}: (4, {}), {1}: (5, {}), {2}: (6, {})} | custom-call | flops 282591232 | bytes 4194304 | tf_op jit(solution)/shard_map/pallas_call | solution.py:268
  20.4 5.4 %shard_map.70 = (bf16[128,512]{1,0:T(8,128)(2,1)}, bf16[5,7,128,512]{3,2,1,0:T(8,128)(2,1)}) custom-call(s32[3]{0:T(128)} %pad_add_fusion.5.p_ref, bf16[4,128,512]{2,1,0:T(8,128)(2,1)} %bitcast.50, bf16[128,512]{1,0:T(8,128)(2,1)} %copy-done, f32[4,4,128,512]{3,2,1,0:T(8,128)} %get-tuple-element.45.z_ref.refs_0_, ...), custom_call_target="tpu_custom_call", output_to_operand_aliasing={{1}: (6, {})} | custom-call | flops 282591232 | bytes 4194304 | tf_op jit(solution)/shard_map/pallas_call | solution.py:254
  25.8 2.5 %collective-permute-start.1 = (bf16[128,512]{1,0:T(8,128)(2,1)}, bf16[128,512]{1,0:T(8,128)(2,1)S(1)}, u32[]{:S(2)}, u32[]{:S(2)}) collective-permute-start(bf16[128,512]{1,0:T(8,128)(2,1)} %get-tuple-element.47), channel_id=1, source_target_pairs={{32,0},{64,32},{96,64},{33,1},{65,33},{97,65},{34,2},{66,34},{98,6... | collective-permute-start | bytes 393224 | tf_op jit(solution)/shard_map/ppermute | solution.py:18
  29.0 4.2 %shard_map.71 = (f32[4,4,128,512]{3,2,1,0:T(8,128)}, bf16[4,4,128,512]{3,2,1,0:T(8,128)(2,1)}, bf16[4,4,128,512]{3,2,1,0:T(8,128)(2,1)}) custom-call(s32[1]{0:T(128)} %bitcast.11.p_ref, bf16[4,128,512]{2,1,0:T(8,128)(2,1)} %bitcast.58, bf16[4,512,512]{2,1,0:T(8,128)(2,1)} %bitcast.35, ...), custom_call_target="tpu_custom_call", output_to_operand_aliasing={{0}: (4, {}), {1}: (5, {}), {2}: (6, {})} | custom-call | flops 282591232 | bytes 4194304 | tf_op jit(solution)/shard_map/pallas_call | solution.py:268
  33.8 5.4 %shard_map.72 = (bf16[128,512]{1,0:T(8,128)(2,1)}, bf16[5,7,128,512]{3,2,1,0:T(8,128)(2,1)}) custom-call(s32[3]{0:T(128)} %pad_add_fusion.4.p_ref, bf16[4,128,512]{2,1,0:T(8,128)(2,1)} %bitcast.51, bf16[128,512]{1,0:T(8,128)(2,1)} %copy-done.2, f32[4,4,128,512]{3,2,1,0:T(8,128)} %get-tuple-element.50.z_ref.refs_0_, ...), custom_call_target="tpu_custom_call", output_to_operand_aliasing={{1}: (6, {})} | custom-call | flops 282591232 | bytes 4194304 | tf_op jit(solution)/shard_map/pallas_call | solution.py:254
  39.2 2.4 %collective-permute-start.2 = (bf16[128,512]{1,0:T(8,128)(2,1)}, bf16[128,512]{1,0:T(8,128)(2,1)S(1)}, u32[]{:S(2)}, u32[]{:S(2)}) collective-permute-start(bf16[128,512]{1,0:T(8,128)(2,1)} %get-tuple-element.52), channel_id=1, source_target_pairs={{32,0},{64,32},{96,64},{33,1},{65,33},{97,65},{34,2},{66,34},{98,6... | collective-permute-start | bytes 393224 | tf_op jit(solution)/shard_map/ppermute | solution.py:18
  42.3 4.2 %shard_map.73 = (f32[4,4,128,512]{3,2,1,0:T(8,128)}, bf16[4,4,128,512]{3,2,1,0:T(8,128)(2,1)}, bf16[4,4,128,512]{3,2,1,0:T(8,128)(2,1)}) custom-call(s32[1]{0:T(128)} %bitcast.9.p_ref, bf16[4,128,512]{2,1,0:T(8,128)(2,1)} %bitcast.59, bf16[4,512,512]{2,1,0:T(8,128)(2,1)} %bitcast.37, ...), custom_call_target="tpu_custom_call", output_to_operand_aliasing={{0}: (4, {}), {1}: (5, {}), {2}: (6, {})} | custom-call | flops 282591232 | bytes 4194304 | tf_op jit(solution)/shard_map/pallas_call | solution.py:268
  47.1 5.4 %shard_map.74 = (bf16[128,512]{1,0:T(8,128)(2,1)}, bf16[5,7,128,512]{3,2,1,0:T(8,128)(2,1)}) custom-call(s32[3]{0:T(128)} %pad_add_fusion.3.p_ref, bf16[4,128,512]{2,1,0:T(8,128)(2,1)} %bitcast.52, bf16[128,512]{1,0:T(8,128)(2,1)} %copy-done.3, f32[4,4,128,512]{3,2,1,0:T(8,128)} %get-tuple-element.55.z_ref.refs_0_, ...), custom_call_target="tpu_custom_call", output_to_operand_aliasing={{1}: (6, {})} | custom-call | flops 282591232 | bytes 4194304 | tf_op jit(solution)/shard_map/pallas_call | solution.py:254
  52.5 2.5 %collective-permute-start.3 = (bf16[128,512]{1,0:T(8,128)(2,1)}, bf16[128,512]{1,0:T(8,128)(2,1)S(1)}, u32[]{:S(2)}, u32[]{:S(2)}) collective-permute-start(bf16[128,512]{1,0:T(8,128)(2,1)} %get-tuple-element.57), channel_id=1, source_target_pairs={{32,0},{64,32},{96,64},{33,1},{65,33},{97,65},{34,2},{66,34},{98,6... | collective-permute-start | bytes 393224 | tf_op jit(solution)/shard_map/ppermute | solution.py:18
  55.5 4.2 %shard_map.75 = (f32[4,4,128,512]{3,2,1,0:T(8,128)}, bf16[4,4,128,512]{3,2,1,0:T(8,128)(2,1)}, bf16[4,4,128,512]{3,2,1,0:T(8,128)(2,1)}) custom-call(s32[1]{0:T(128)} %bitcast.7.p_ref, bf16[4,128,512]{2,1,0:T(8,128)(2,1)} %bitcast.60, bf16[4,512,512]{2,1,0:T(8,128)(2,1)} %bitcast.39, ...), custom_call_target="tpu_custom_call", output_to_operand_aliasing={{0}: (4, {}), {1}: (5, {}), {2}: (6, {})} | custom-call | flops 282591232 | bytes 4194304 | tf_op jit(solution)/shard_map/pallas_call | solution.py:268
  60.4 5.4 %shard_map.76 = (bf16[128,512]{1,0:T(8,128)(2,1)}, bf16[5,7,128,512]{3,2,1,0:T(8,128)(2,1)}) custom-call(s32[3]{0:T(128)} %pad_add_fusion.2.p_ref, bf16[4,128,512]{2,1,0:T(8,128)(2,1)} %bitcast.53, bf16[128,512]{1,0:T(8,128)(2,1)} %copy-done.4, f32[4,4,128,512]{3,2,1,0:T(8,128)} %get-tuple-element.60.z_ref.refs_0_, ...), custom_call_target="tpu_custom_call", output_to_operand_aliasing={{1}: (6, {})} | custom-call | flops 282591232 | bytes 4194304 | tf_op jit(solution)/shard_map/pallas_call | solution.py:254
  65.8 2.3 %collective-permute-start.4 = (bf16[128,512]{1,0:T(8,128)(2,1)}, bf16[128,512]{1,0:T(8,128)(2,1)S(1)}, u32[]{:S(2)}, u32[]{:S(2)}) collective-permute-start(bf16[128,512]{1,0:T(8,128)(2,1)} %get-tuple-element.62), channel_id=1, source_target_pairs={{32,0},{64,32},{96,64},{33,1},{65,33},{97,65},{34,2},{66,34},{98,6... | collective-permute-start | bytes 393224 | tf_op jit(solution)/shard_map/ppermute | solution.py:18
  68.6 4.2 %shard_map.77 = (f32[4,4,128,512]{3,2,1,0:T(8,128)}, bf16[4,4,128,512]{3,2,1,0:T(8,128)(2,1)}, bf16[4,4,128,512]{3,2,1,0:T(8,128)(2,1)}) custom-call(s32[1]{0:T(128)} %bitcast.5.p_ref, bf16[4,128,512]{2,1,0:T(8,128)(2,1)} %bitcast.61, bf16[4,512,512]{2,1,0:T(8,128)(2,1)} %bitcast.41, ...), custom_call_target="tpu_custom_call", output_to_operand_aliasing={{0}: (4, {}), {1}: (5, {}), {2}: (6, {})} | custom-call | flops 282591232 | bytes 4194304 | tf_op jit(solution)/shard_map/pallas_call | solution.py:268
  73.5 5.4 %shard_map.78 = (bf16[128,512]{1,0:T(8,128)(2,1)}, bf16[5,7,128,512]{3,2,1,0:T(8,128)(2,1)}) custom-call(s32[3]{0:T(128)} %pad_add_fusion.1.p_ref, bf16[4,128,512]{2,1,0:T(8,128)(2,1)} %bitcast.54, bf16[128,512]{1,0:T(8,128)(2,1)} %copy-done.5, f32[4,4,128,512]{3,2,1,0:T(8,128)} %get-tuple-element.65.z_ref.refs_0_, ...), custom_call_target="tpu_custom_call", output_to_operand_aliasing={{1}: (6, {})} | custom-call | flops 282591232 | bytes 4194304 | tf_op jit(solution)/shard_map/pallas_call | solution.py:254
  78.9 2.3 %collective-permute-start.5 = (bf16[128,512]{1,0:T(8,128)(2,1)}, bf16[128,512]{1,0:T(8,128)(2,1)S(1)}, u32[]{:S(2)}, u32[]{:S(2)}) collective-permute-start(bf16[128,512]{1,0:T(8,128)(2,1)} %get-tuple-element.67), channel_id=1, source_target_pairs={{32,0},{64,32},{96,64},{33,1},{65,33},{97,65},{34,2},{66,34},{98,6... | collective-permute-start | bytes 393224 | tf_op jit(solution)/shard_map/ppermute | solution.py:18
  81.8 4.2 %shard_map.79 = (f32[4,4,128,512]{3,2,1,0:T(8,128)}, bf16[4,4,128,512]{3,2,1,0:T(8,128)(2,1)}, bf16[4,4,128,512]{3,2,1,0:T(8,128)(2,1)}) custom-call(s32[1]{0:T(128)} %bitcast.1.p_ref, bf16[4,128,512]{2,1,0:T(8,128)(2,1)} %bitcast.62, bf16[4,512,512]{2,1,0:T(8,128)(2,1)} %bitcast.43, ...), custom_call_target="tpu_custom_call", output_to_operand_aliasing={{0}: (4, {}), {1}: (5, {}), {2}: (6, {})} | custom-call | flops 282591232 | bytes 4194304 | tf_op jit(solution)/shard_map/pallas_call | solution.py:268
  86.6 5.4 %shard_map.80 = (bf16[128,512]{1,0:T(8,128)(2,1)}, bf16[5,7,128,512]{3,2,1,0:T(8,128)(2,1)}) custom-call(s32[3]{0:T(128)} %pad_add_fusion.p_ref, bf16[4,128,512]{2,1,0:T(8,128)(2,1)} %bitcast.55, bf16[128,512]{1,0:T(8,128)(2,1)} %copy-done.1, f32[4,4,128,512]{3,2,1,0:T(8,128)} %get-tuple-element.70.z_ref, ...), custom_call_target="tpu_custom_call", output_to_operand_aliasing={{1}: (6, {})} | custom-call | flops 282591232 | bytes 4194304 | tf_op jit(solution)/shard_map/pallas_call | solution.py:254
  92.0 13.0 %shard_map.81 = (bf16[2,16,72,512]{3,2,1,0:T(8,128)(2,1)}, bf16[4,128,512]{2,1,0:T(8,128)(2,1)}) custom-call(s32[1]{0:T(128)} %bitcast.p_ref, bf16[5,7,128,512]{3,2,1,0:T(8,128)(2,1)} %get-tuple-element.72.h_ref, bf16[4,512,512]{2,1,0:T(8,128)(2,1)} %bitcast.46, bf16[4,512,512]{2,1,0:T(8,128)(2,1)} %bitcast.47, f32[4,512,512]{2,1,0:T(8,128)} %bitcast.30, ...), custom_call_target="tpu_custom_call" | custom-call | tf_op jit(solution)/shard_map/pallas_call | solution.py:290
  105.0 6.8 %all_to_all.10 = bf16[2,16,72,512]{3,2,1,0:T(8,128)(2,1)S(1)} all-to-all(bf16[2,16,72,512]{3,2,1,0:T(8,128)(2,1)} %get-tuple-element.76), channel_id=1, replica_groups=mesh['section'=4,'chip'=16,'core'=2] {'core'}, dimensions={0} | all-to-all | bytes 4718592 | tf_op jit(solution)/shard_map/all_to_all | solution.py:302
  113.1 26.7 %all_to_all.11 = bf16[16,72,512]{2,1,0:T(8,128)(2,1)S(1)} all-to-all(bf16[16,72,512]{2,1,0:T(8,128)(2,1)S(1)} %reduce_sum.21), channel_id=1, replica_groups=mesh['section'=4,'chip'=16,'core'=2] {'chip'}, dimensions={0} | all-to-all | bytes 2359296 | tf_op jit(solution)/shard_map/all_to_all | solution.py:302
  (32 shorter events, 11.0 us)
Async XLA Ops:
  12.2 7.5 %collective-permute-start = (bf16[128,512]{1,0:T(8,128)(2,1)}, bf16[128,512]{1,0:T(8,128)(2,1)S(1)}, u32[]{:S(2)}, u32[]{:S(2)}) collective-permute-start(bf16[128,512]{1,0:T(8,128)(2,1)} %get-tuple-element.42), channel_id=1, source_target_pairs={{32,0},{64,32},{96,64},{33,1},{65,33},{97,65},{34,2},{66,34},{98,6... | collective-permute-start | bytes 393224 | tf_op jit(solution)/shard_map/ppermute | solution.py:18
  19.8 0.7 copy-start
  25.8 7.3 %collective-permute-start.1 = (bf16[128,512]{1,0:T(8,128)(2,1)}, bf16[128,512]{1,0:T(8,128)(2,1)S(1)}, u32[]{:S(2)}, u32[]{:S(2)}) collective-permute-start(bf16[128,512]{1,0:T(8,128)(2,1)} %get-tuple-element.47), channel_id=1, source_target_pairs={{32,0},{64,32},{96,64},{33,1},{65,33},{97,65},{34,2},{66,34},{98,6... | collective-permute-start | bytes 393224 | tf_op jit(solution)/shard_map/ppermute | solution.py:18
  33.1 0.7 copy-start.2
  39.2 7.2 %collective-permute-start.2 = (bf16[128,512]{1,0:T(8,128)(2,1)}, bf16[128,512]{1,0:T(8,128)(2,1)S(1)}, u32[]{:S(2)}, u32[]{:S(2)}) collective-permute-start(bf16[128,512]{1,0:T(8,128)(2,1)} %get-tuple-element.52), channel_id=1, source_target_pairs={{32,0},{64,32},{96,64},{33,1},{65,33},{97,65},{34,2},{66,34},{98,6... | collective-permute-start | bytes 393224 | tf_op jit(solution)/shard_map/ppermute | solution.py:18
  46.4 0.7 copy-start.3
  52.5 7.2 %collective-permute-start.3 = (bf16[128,512]{1,0:T(8,128)(2,1)}, bf16[128,512]{1,0:T(8,128)(2,1)S(1)}, u32[]{:S(2)}, u32[]{:S(2)}) collective-permute-start(bf16[128,512]{1,0:T(8,128)(2,1)} %get-tuple-element.57), channel_id=1, source_target_pairs={{32,0},{64,32},{96,64},{33,1},{65,33},{97,65},{34,2},{66,34},{98,6... | collective-permute-start | bytes 393224 | tf_op jit(solution)/shard_map/ppermute | solution.py:18
  59.7 0.7 copy-start.4
  65.8 7.0 %collective-permute-start.4 = (bf16[128,512]{1,0:T(8,128)(2,1)}, bf16[128,512]{1,0:T(8,128)(2,1)S(1)}, u32[]{:S(2)}, u32[]{:S(2)}) collective-permute-start(bf16[128,512]{1,0:T(8,128)(2,1)} %get-tuple-element.62), channel_id=1, source_target_pairs={{32,0},{64,32},{96,64},{33,1},{65,33},{97,65},{34,2},{66,34},{98,6... | collective-permute-start | bytes 393224 | tf_op jit(solution)/shard_map/ppermute | solution.py:18
  72.8 0.7 copy-start.5
  78.9 7.1 %collective-permute-start.5 = (bf16[128,512]{1,0:T(8,128)(2,1)}, bf16[128,512]{1,0:T(8,128)(2,1)S(1)}, u32[]{:S(2)}, u32[]{:S(2)}) collective-permute-start(bf16[128,512]{1,0:T(8,128)(2,1)} %get-tuple-element.67), channel_id=1, source_target_pairs={{32,0},{64,32},{96,64},{33,1},{65,33},{97,65},{34,2},{66,34},{98,6... | collective-permute-start | bytes 393224 | tf_op jit(solution)/shard_map/ppermute | solution.py:18
  86.0 0.7 copy-start.1

commit v10 on v7

--- a/solution.py
+++ b/solution.py
@@ -295,15 +295,11 @@
         out_specs=(vmem, vmem),
         compiler_params=params,
     )(first, hbuf, acts, xs, zs, weights, kerns)
-    part = send
-    for stage, name in enumerate(("core", "chip")):
-        part = lax.all_to_all(part, name, 0, 0, tiled=True)
-        part = jnp.sum(part.astype(jnp.float32), axis=0)
-        if stage == 0:
-            part = part.astype(jnp.bfloat16)
-    summed = part
-    point_red = summed[: layers * share].reshape(layers, share, chans)
-    dk_rows = summed[layers * share : layers * share + pad_taps]
+    part = lax.all_to_all(send, "core", 0, 0, tiled=True)
+    part = jnp.sum(part.astype(jnp.float32), axis=0).astype(jnp.bfloat16)
+    recv = lax.all_to_all(part, "chip", 0, 0, tiled=True).astype(jnp.float32)
+    point_red = jnp.sum(recv[:, : layers * share], axis=0).reshape(layers, share, chans)
+    dk_rows = jnp.sum(recv[:, layers * share : layers * share + pad_taps], axis=0)
     depth_red = jnp.concatenate(
         [dk_rows[:, : layers * share], dk_rows[:1, layers * share : 2 * layers * share]], axis=0
     )

time: 143 us -> 143 us (level)
  no operation moved by 1% of the time
where the time goes in v10:
time: 143 us
  Pallas kernels  80 us (56%)
  blocking collectives  33.6 us (23%)
  starting transfers between devices  14.6 us (10%)
  other arithmetic  8.19 us (6%)
  local copies, waits for them, and re-layouts  5.36 us (4%)
    pallas_call x7, Pallas kernels, body(): pl.pallas_call(functools.partial(step_kernel, height=height, width=width)...  37.7 us
    all_to_all x1, blocking collectives, body(): recv = lax.all_to_all(part, 'chip', 0, 0, tiled=True).astype(jnp.float32)  26.7 us
    pallas_call x6, Pallas kernels, body(): pl.pallas_call(functools.partial(fwd_kernel, height=height, width=width),...  25.1 us
    ppermute x6, starting transfers between devices, from_behind(): return lax.ppermute(shard, axis, pairs)  14.6 us
    pallas_call x1, Pallas kernels, body(): pl.pallas_call(functools.partial(grad_kernel, height=height, width=width,...  13 us
    all_to_all x1, blocking collectives, body(): part = lax.all_to_all(send, 'core', 0, 0, tiled=True)  6.85 us
    another operation x7, other arithmetic, body(): scalars = jnp.stack([picked, is_last, valid]).astype(jnp.int32)  4.34 us
    pallas_call x1, Pallas kernels, body(): pl.pallas_call(functools.partial(fwd_first_kernel, height=height, width=w...  4.16 us
  transfers between devices with their start and end apart: 6, of which 0 were waited for; matrix products, arithmetic and copies ran while one was open for 3% of the time, Pallas kernels for 18%

profile of v10, /device:TPU:6, one launch (start us, length us, event | category | flops | bytes accessed | tf_op | source)
XLA Modules:
  0.0 142.5 jit_solution(8669308912292144379)
XLA Ops:
  0.6 1.4 %bitcast_convert_fusion.k_ref = f32[4,9,512]{2,1,0:T(8,128)} fusion(bf16[1,4,9,512]{3,1,2,0:T(4,128)(2,1)} %param.7), kind=kLoop, calls=%fused_computation.2 | loop fusion | flops 18432 | bytes 110592 | tf_op jit(solution)/shard_map/convert_element_type | solution.py:183
  2.7 4.2 %shard_map.67 = (f32[4,4,128,512]{3,2,1,0:T(8,128)}, bf16[4,4,128,512]{3,2,1,0:T(8,128)(2,1)}, bf16[4,4,128,512]{3,2,1,0:T(8,128)(2,1)}, bf16[5,7,128,512]{3,2,1,0:T(8,128)(2,1)}) custom-call(s32[1]{0:T(128)} %bitcast.15.p_ref, bf16[4,128,512]{2,1,0:T(8,128)(2,1)} %bitcast.55, bf16[4,512,512]{2,1,0:T(8,128)(2,1)} %bitcast.31, ...), custom_call_target="tpu_custom_call" | custom-call | flops 282591232 | bytes 4194304 | tf_op jit(solution)/shard_map/pallas_call | solution.py:215
  7.6 5.4 %shard_map.68 = (bf16[128,512]{1,0:T(8,128)(2,1)}, bf16[5,7,128,512]{3,2,1,0:T(8,128)(2,1)}) custom-call(s32[3]{0:T(128)} %pad_add_fusion.6.p_ref, bf16[4,128,512]{2,1,0:T(8,128)(2,1)} %bitcast.48, bf16[128,512]{1,0:T(8,128)(2,1)} %broadcast_in_dim.6.car_ref, f32[4,4,128,512]{3,2,1,0:T(8,128)} %get-tuple-element.40.z_ref.refs_0_, ...), custom_call_target="tpu_custom_call", output_to_operand_aliasing={{1}: (6, {})} | custom-call | flops 282591232 | bytes 4194304 | tf_op jit(solution)/shard_map/pallas_call | solution.py:252
  13.0 2.7 %collective-permute-start = (bf16[128,512]{1,0:T(8,128)(2,1)}, bf16[128,512]{1,0:T(8,128)(2,1)S(1)}, u32[]{:S(2)}, u32[]{:S(2)}) collective-permute-start(bf16[128,512]{1,0:T(8,128)(2,1)} %get-tuple-element.42), channel_id=1, source_target_pairs={{32,0},{64,32},{96,64},{33,1},{65,33},{97,65},{34,2},{66,34},{98,6... | collective-permute-start | bytes 393224 | tf_op jit(solution)/shard_map/ppermute | solution.py:18
  15.7 4.2 %shard_map.69 = (f32[4,4,128,512]{3,2,1,0:T(8,128)}, bf16[4,4,128,512]{3,2,1,0:T(8,128)(2,1)}, bf16[4,4,128,512]{3,2,1,0:T(8,128)(2,1)}) custom-call(s32[1]{0:T(128)} %bitcast.13.p_ref, bf16[4,128,512]{2,1,0:T(8,128)(2,1)} %bitcast.56, bf16[4,512,512]{2,1,0:T(8,128)(2,1)} %bitcast.33, ...), custom_call_target="tpu_custom_call", output_to_operand_aliasing={{0}: (4, {}), {1}: (5, {}), {2}: (6, {})} | custom-call | flops 282591232 | bytes 4194304 | tf_op jit(solution)/shard_map/pallas_call | solution.py:266
  21.2 5.4 %shard_map.70 = (bf16[128,512]{1,0:T(8,128)(2,1)}, bf16[5,7,128,512]{3,2,1,0:T(8,128)(2,1)}) custom-call(s32[3]{0:T(128)} %pad_add_fusion.5.p_ref, bf16[4,128,512]{2,1,0:T(8,128)(2,1)} %bitcast.49, bf16[128,512]{1,0:T(8,128)(2,1)} %copy-done, f32[4,4,128,512]{3,2,1,0:T(8,128)} %get-tuple-element.45.z_ref.refs_0_, ...), custom_call_target="tpu_custom_call", output_to_operand_aliasing={{1}: (6, {})} | custom-call | flops 282591232 | bytes 4194304 | tf_op jit(solution)/shard_map/pallas_call | solution.py:252
  26.6 2.5 %collective-permute-start.1 = (bf16[128,512]{1,0:T(8,128)(2,1)}, bf16[128,512]{1,0:T(8,128)(2,1)S(1)}, u32[]{:S(2)}, u32[]{:S(2)}) collective-permute-start(bf16[128,512]{1,0:T(8,128)(2,1)} %get-tuple-element.47), channel_id=1, source_target_pairs={{32,0},{64,32},{96,64},{33,1},{65,33},{97,65},{34,2},{66,34},{98,6... | collective-permute-start | bytes 393224 | tf_op jit(solution)/shard_map/ppermute | solution.py:18
  29.8 4.2 %shard_map.71 = (f32[4,4,128,512]{3,2,1,0:T(8,128)}, bf16[4,4,128,512]{3,2,1,0:T(8,128)(2,1)}, bf16[4,4,128,512]{3,2,1,0:T(8,128)(2,1)}) custom-call(s32[1]{0:T(128)} %bitcast.11.p_ref, bf16[4,128,512]{2,1,0:T(8,128)(2,1)} %bitcast.57, bf16[4,512,512]{2,1,0:T(8,128)(2,1)} %bitcast.35, ...), custom_call_target="tpu_custom_call", output_to_operand_aliasing={{0}: (4, {}), {1}: (5, {}), {2}: (6, {})} | custom-call | flops 282591232 | bytes 4194304 | tf_op jit(solution)/shard_map/pallas_call | solution.py:266
  34.6 5.4 %shard_map.72 = (bf16[128,512]{1,0:T(8,128)(2,1)}, bf16[5,7,128,512]{3,2,1,0:T(8,128)(2,1)}) custom-call(s32[3]{0:T(128)} %pad_add_fusion.4.p_ref, bf16[4,128,512]{2,1,0:T(8,128)(2,1)} %bitcast.50, bf16[128,512]{1,0:T(8,128)(2,1)} %copy-done.2, f32[4,4,128,512]{3,2,1,0:T(8,128)} %get-tuple-element.50.z_ref.refs_0_, ...), custom_call_target="tpu_custom_call", output_to_operand_aliasing={{1}: (6, {})} | custom-call | flops 282591232 | bytes 4194304 | tf_op jit(solution)/shard_map/pallas_call | solution.py:252
  40.0 2.4 %collective-permute-start.2 = (bf16[128,512]{1,0:T(8,128)(2,1)}, bf16[128,512]{1,0:T(8,128)(2,1)S(1)}, u32[]{:S(2)}, u32[]{:S(2)}) collective-permute-start(bf16[128,512]{1,0:T(8,128)(2,1)} %get-tuple-element.52), channel_id=1, source_target_pairs={{32,0},{64,32},{96,64},{33,1},{65,33},{97,65},{34,2},{66,34},{98,6... | collective-permute-start | bytes 393224 | tf_op jit(solution)/shard_map/ppermute | solution.py:18
  43.0 4.2 %shard_map.73 = (f32[4,4,128,512]{3,2,1,0:T(8,128)}, bf16[4,4,128,512]{3,2,1,0:T(8,128)(2,1)}, bf16[4,4,128,512]{3,2,1,0:T(8,128)(2,1)}) custom-call(s32[1]{0:T(128)} %bitcast.9.p_ref, bf16[4,128,512]{2,1,0:T(8,128)(2,1)} %bitcast.58, bf16[4,512,512]{2,1,0:T(8,128)(2,1)} %bitcast.37, ...), custom_call_target="tpu_custom_call", output_to_operand_aliasing={{0}: (4, {}), {1}: (5, {}), {2}: (6, {})} | custom-call | flops 282591232 | bytes 4194304 | tf_op jit(solution)/shard_map/pallas_call | solution.py:266
  47.8 5.4 %shard_map.74 = (bf16[128,512]{1,0:T(8,128)(2,1)}, bf16[5,7,128,512]{3,2,1,0:T(8,128)(2,1)}) custom-call(s32[3]{0:T(128)} %pad_add_fusion.3.p_ref, bf16[4,128,512]{2,1,0:T(8,128)(2,1)} %bitcast.51, bf16[128,512]{1,0:T(8,128)(2,1)} %copy-done.3, f32[4,4,128,512]{3,2,1,0:T(8,128)} %get-tuple-element.55.z_ref.refs_0_, ...), custom_call_target="tpu_custom_call", output_to_operand_aliasing={{1}: (6, {})} | custom-call | flops 282591232 | bytes 4194304 | tf_op jit(solution)/shard_map/pallas_call | solution.py:252
  53.2 2.5 %collective-permute-start.3 = (bf16[128,512]{1,0:T(8,128)(2,1)}, bf16[128,512]{1,0:T(8,128)(2,1)S(1)}, u32[]{:S(2)}, u32[]{:S(2)}) collective-permute-start(bf16[128,512]{1,0:T(8,128)(2,1)} %get-tuple-element.57), channel_id=1, source_target_pairs={{32,0},{64,32},{96,64},{33,1},{65,33},{97,65},{34,2},{66,34},{98,6... | collective-permute-start | bytes 393224 | tf_op jit(solution)/shard_map/ppermute | solution.py:18
  56.4 4.2 %shard_map.75 = (f32[4,4,128,512]{3,2,1,0:T(8,128)}, bf16[4,4,128,512]{3,2,1,0:T(8,128)(2,1)}, bf16[4,4,128,512]{3,2,1,0:T(8,128)(2,1)}) custom-call(s32[1]{0:T(128)} %bitcast.7.p_ref, bf16[4,128,512]{2,1,0:T(8,128)(2,1)} %bitcast.59, bf16[4,512,512]{2,1,0:T(8,128)(2,1)} %bitcast.39, ...), custom_call_target="tpu_custom_call", output_to_operand_aliasing={{0}: (4, {}), {1}: (5, {}), {2}: (6, {})} | custom-call | flops 282591232 | bytes 4194304 | tf_op jit(solution)/shard_map/pallas_call | solution.py:266
  61.2 5.4 %shard_map.76 = (bf16[128,512]{1,0:T(8,128)(2,1)}, bf16[5,7,128,512]{3,2,1,0:T(8,128)(2,1)}) custom-call(s32[3]{0:T(128)} %pad_add_fusion.2.p_ref, bf16[4,128,512]{2,1,0:T(8,128)(2,1)} %bitcast.52, bf16[128,512]{1,0:T(8,128)(2,1)} %copy-done.4, f32[4,4,128,512]{3,2,1,0:T(8,128)} %get-tuple-element.60.z_ref.refs_0_, ...), custom_call_target="tpu_custom_call", output_to_operand_aliasing={{1}: (6, {})} | custom-call | flops 282591232 | bytes 4194304 | tf_op jit(solution)/shard_map/pallas_call | solution.py:252
  66.6 2.2 %collective-permute-start.4 = (bf16[128,512]{1,0:T(8,128)(2,1)}, bf16[128,512]{1,0:T(8,128)(2,1)S(1)}, u32[]{:S(2)}, u32[]{:S(2)}) collective-permute-start(bf16[128,512]{1,0:T(8,128)(2,1)} %get-tuple-element.62), channel_id=1, source_target_pairs={{32,0},{64,32},{96,64},{33,1},{65,33},{97,65},{34,2},{66,34},{98,6... | collective-permute-start | bytes 393224 | tf_op jit(solution)/shard_map/ppermute | solution.py:18
  69.4 4.2 %shard_map.77 = (f32[4,4,128,512]{3,2,1,0:T(8,128)}, bf16[4,4,128,512]{3,2,1,0:T(8,128)(2,1)}, bf16[4,4,128,512]{3,2,1,0:T(8,128)(2,1)}) custom-call(s32[1]{0:T(128)} %bitcast.5.p_ref, bf16[4,128,512]{2,1,0:T(8,128)(2,1)} %bitcast.60, bf16[4,512,512]{2,1,0:T(8,128)(2,1)} %bitcast.41, ...), custom_call_target="tpu_custom_call", output_to_operand_aliasing={{0}: (4, {}), {1}: (5, {}), {2}: (6, {})} | custom-call | flops 282591232 | bytes 4194304 | tf_op jit(solution)/shard_map/pallas_call | solution.py:266
  74.3 5.4 %shard_map.78 = (bf16[128,512]{1,0:T(8,128)(2,1)}, bf16[5,7,128,512]{3,2,1,0:T(8,128)(2,1)}) custom-call(s32[3]{0:T(128)} %pad_add_fusion.1.p_ref, bf16[4,128,512]{2,1,0:T(8,128)(2,1)} %bitcast.53, bf16[128,512]{1,0:T(8,128)(2,1)} %copy-done.5, f32[4,4,128,512]{3,2,1,0:T(8,128)} %get-tuple-element.65.z_ref.refs_0_, ...), custom_call_target="tpu_custom_call", output_to_operand_aliasing={{1}: (6, {})} | custom-call | flops 282591232 | bytes 4194304 | tf_op jit(solution)/shard_map/pallas_call | solution.py:252
  79.7 2.3 %collective-permute-start.5 = (bf16[128,512]{1,0:T(8,128)(2,1)}, bf16[128,512]{1,0:T(8,128)(2,1)S(1)}, u32[]{:S(2)}, u32[]{:S(2)}) collective-permute-start(bf16[128,512]{1,0:T(8,128)(2,1)} %get-tuple-element.67), channel_id=1, source_target_pairs={{32,0},{64,32},{96,64},{33,1},{65,33},{97,65},{34,2},{66,34},{98,6... | collective-permute-start | bytes 393224 | tf_op jit(solution)/shard_map/ppermute | solution.py:18
  82.5 4.2 %shard_map.79 = (f32[4,4,128,512]{3,2,1,0:T(8,128)}, bf16[4,4,128,512]{3,2,1,0:T(8,128)(2,1)}, bf16[4,4,128,512]{3,2,1,0:T(8,128)(2,1)}) custom-call(s32[1]{0:T(128)} %bitcast.1.p_ref, bf16[4,128,512]{2,1,0:T(8,128)(2,1)} %bitcast.61, bf16[4,512,512]{2,1,0:T(8,128)(2,1)} %bitcast.43, ...), custom_call_target="tpu_custom_call", output_to_operand_aliasing={{0}: (4, {}), {1}: (5, {}), {2}: (6, {})} | custom-call | flops 282591232 | bytes 4194304 | tf_op jit(solution)/shard_map/pallas_call | solution.py:266
  87.3 5.4 %shard_map.80 = (bf16[128,512]{1,0:T(8,128)(2,1)}, bf16[5,7,128,512]{3,2,1,0:T(8,128)(2,1)}) custom-call(s32[3]{0:T(128)} %pad_add_fusion.p_ref, bf16[4,128,512]{2,1,0:T(8,128)(2,1)} %bitcast.54, bf16[128,512]{1,0:T(8,128)(2,1)} %copy-done.1, f32[4,4,128,512]{3,2,1,0:T(8,128)} %get-tuple-element.70.z_ref, ...), custom_call_target="tpu_custom_call", output_to_operand_aliasing={{1}: (6, {})} | custom-call | flops 282591232 | bytes 4194304 | tf_op jit(solution)/shard_map/pallas_call | solution.py:252
  92.7 13.0 %shard_map.81 = (bf16[2,16,72,512]{3,2,1,0:T(8,128)(2,1)}, bf16[4,128,512]{2,1,0:T(8,128)(2,1)}) custom-call(s32[1]{0:T(128)} %bitcast.p_ref, bf16[5,7,128,512]{3,2,1,0:T(8,128)(2,1)} %get-tuple-element.72.h_ref, bf16[4,512,512]{2,1,0:T(8,128)(2,1)} %bitcast.46, bf16[4,512,512]{2,1,0:T(8,128)(2,1)} %bitcast.47, f32[4,512,512]{2,1,0:T(8,128)} %bitcast.30, ...), custom_call_target="tpu_custom_call" | custom-call | tf_op jit(solution)/shard_map/pallas_call | solution.py:288
  105.8 6.8 %all_to_all.10 = bf16[2,16,72,512]{3,2,1,0:T(8,128)(2,1)S(1)} all-to-all(bf16[2,16,72,512]{3,2,1,0:T(8,128)(2,1)} %get-tuple-element.76), channel_id=1, replica_groups=mesh['section'=4,'chip'=16,'core'=2] {'core'}, dimensions={0} | all-to-all | bytes 4718592 | tf_op jit(solution)/shard_map/all_to_all | solution.py:298
  113.8 26.7 %all_to_all.11 = bf16[16,72,512]{2,1,0:T(8,128)(2,1)S(1)} all-to-all(bf16[16,72,512]{2,1,0:T(8,128)(2,1)S(1)} %reduce_sum.30), channel_id=1, replica_groups=mesh['section'=4,'chip'=16,'core'=2] {'chip'}, dimensions={0} | all-to-all | bytes 2359296 | tf_op jit(solution)/shard_map/all_to_all | solution.py:300
  (34 shorter events, 12.1 us)
Async XLA Ops:
  13.0 7.5 %collective-permute-start = (bf16[128,512]{1,0:T(8,128)(2,1)}, bf16[128,512]{1,0:T(8,128)(2,1)S(1)}, u32[]{:S(2)}, u32[]{:S(2)}) collective-permute-start(bf16[128,512]{1,0:T(8,128)(2,1)} %get-tuple-element.42), channel_id=1, source_target_pairs={{32,0},{64,32},{96,64},{33,1},{65,33},{97,65},{34,2},{66,34},{98,6... | collective-permute-start | bytes 393224 | tf_op jit(solution)/shard_map/ppermute | solution.py:18
  20.5 0.7 copy-start
  26.6 7.4 %collective-permute-start.1 = (bf16[128,512]{1,0:T(8,128)(2,1)}, bf16[128,512]{1,0:T(8,128)(2,1)S(1)}, u32[]{:S(2)}, u32[]{:S(2)}) collective-permute-start(bf16[128,512]{1,0:T(8,128)(2,1)} %get-tuple-element.47), channel_id=1, source_target_pairs={{32,0},{64,32},{96,64},{33,1},{65,33},{97,65},{34,2},{66,34},{98,6... | collective-permute-start | bytes 393224 | tf_op jit(solution)/shard_map/ppermute | solution.py:18
  33.9 0.7 copy-start.2
  40.0 7.2 %collective-permute-start.2 = (bf16[128,512]{1,0:T(8,128)(2,1)}, bf16[128,512]{1,0:T(8,128)(2,1)S(1)}, u32[]{:S(2)}, u32[]{:S(2)}) collective-permute-start(bf16[128,512]{1,0:T(8,128)(2,1)} %get-tuple-element.52), channel_id=1, source_target_pairs={{32,0},{64,32},{96,64},{33,1},{65,33},{97,65},{34,2},{66,34},{98,6... | collective-permute-start | bytes 393224 | tf_op jit(solution)/shard_map/ppermute | solution.py:18
  47.2 0.7 copy-start.3
  53.2 7.3 %collective-permute-start.3 = (bf16[128,512]{1,0:T(8,128)(2,1)}, bf16[128,512]{1,0:T(8,128)(2,1)S(1)}, u32[]{:S(2)}, u32[]{:S(2)}) collective-permute-start(bf16[128,512]{1,0:T(8,128)(2,1)} %get-tuple-element.57), channel_id=1, source_target_pairs={{32,0},{64,32},{96,64},{33,1},{65,33},{97,65},{34,2},{66,34},{98,6... | collective-permute-start | bytes 393224 | tf_op jit(solution)/shard_map/ppermute | solution.py:18
  60.6 0.7 copy-start.4
  66.6 7.0 %collective-permute-start.4 = (bf16[128,512]{1,0:T(8,128)(2,1)}, bf16[128,512]{1,0:T(8,128)(2,1)S(1)}, u32[]{:S(2)}, u32[]{:S(2)}) collective-permute-start(bf16[128,512]{1,0:T(8,128)(2,1)} %get-tuple-element.62), channel_id=1, source_target_pairs={{32,0},{64,32},{96,64},{33,1},{65,33},{97,65},{34,2},{66,34},{98,6... | collective-permute-start | bytes 393224 | tf_op jit(solution)/shard_map/ppermute | solution.py:18
  73.6 0.7 copy-start.5
  79.7 7.0 %collective-permute-start.5 = (bf16[128,512]{1,0:T(8,128)(2,1)}, bf16[128,512]{1,0:T(8,128)(2,1)S(1)}, u32[]{:S(2)}, u32[]{:S(2)}) collective-permute-start(bf16[128,512]{1,0:T(8,128)(2,1)} %get-tuple-element.67), channel_id=1, source_target_pairs={{32,0},{64,32},{96,64},{33,1},{65,33},{97,65},{34,2},{66,34},{98,6... | collective-permute-start | bytes 393224 | tf_op jit(solution)/shard_map/ppermute | solution.py:18
  86.7 0.7 copy-start.1
